TPU v7x, 512 devices: a whole 4x4x16 slice. The times are simulated.
512 devices in a mesh: rot: 16 (over x, y), slab: 32 (over z, core).
Axes of the slice: x: 4, y: 4, z: 16, core: 2. Of those that a mesh axis runs over, the one named last changes fastest.
Arguments:
- point_feats: bfloat16 [65536, 96], P('slab'), may hold values from -6 to 6
- owners: int32 [16, 65536], P('rot', 'slab'), may hold values from 0 to 31, as said below
- voxel_ids: int32 [16, 65536], P('rot', 'slab'), may hold values from 0 to 2047, as said below
- active_count: int32 [16, 32], P('rot', 'slab'), may hold values from 4 to 16, as said below
- halo_blocks: int32 [16, 32, 2, 2], P('rot', 'slab'), may hold values from 0 to 15, as said below
- neighbors: int32 [16, 27, 65536], P('rot', None, 'slab'), may hold values from 0 to 2560, as said below
- conv1_weight: bfloat16 [27, 96, 128], replicated, may hold values from -0.125 to 0.125
- conv1_scale: float32 [128], replicated, may hold values from 0.1 to 1.9
- conv1_shift: float32 [128], replicated, may hold values from -3 to 3
- conv2_weight: bfloat16 [27, 128, 128], replicated, may hold values from -0.109375 to 0.109375
- conv2_scale: float32 [128], replicated, may hold values from 0.1 to 1.9
- conv2_shift: float32 [128], replicated, may hold values from -3 to 3
- head_weight: bfloat16 [128, 8], replicated, may hold values from -0.5 to 0.5
- head_bias: float32 [8], replicated, may hold values from -4 to 4
Outputs:
- logits: float32 [8, 65536], P(None, 'slab')
Inputs may be any that keep to these rules, and one draw needn't show every extreme that they name: `owners`: in each copy, of the points of one slab at most 192 lie in voxels of any one slab, and one slab receives exactly 192 points from every slab. `voxel_ids`: A point's voxel slot is active in its owner slab: below active_count of that slab times 128. `active_count`: the active blocks of a slab are its first ones; in every copy some slab has all 16 active. `halo_blocks`: every listed block is active in the slab that sends it. `neighbors`: entries index the slab's extended voxel array; row 2560 is the zero row, which all entries of inactive voxels name; offset 13 of an active voxel names itself; rows of own voxels that are named are active.
All inputs are finite; a program needn't handle non-finite values.
Results may differ from a plain program's by a relative error of at most 0.0006.
Values may be sent and summed in bfloat16 or wider, within the bound.
No kernel may reach another device: no remote copies, remote signals or barrier semaphores. Data moves between devices by JAX's collectives and lax.ppermute only.
A program may use at most 64 MiB of HBM per device.

v0:
```python
import functools

import jax
import jax.numpy as jnp
from jax import lax
from jax.experimental import pallas as pl
from jax.experimental.pallas import tpu as pltpu
from jax.sharding import PartitionSpec as P

BLOCK = 128
OFFSETS = 27
CONV_ROWS = 256
POOL_ROWS = 256
POOL_COLS = 512


def passed_along(shard, axis, by):
    devices = lax.axis_size(axis)
    pairs = [(i, i + by) for i in range(devices) if 0 <= i + by < devices]
    return lax.ppermute(shard, axis, pairs)


def extend_rows(features, halo_list):
    channels = features.shape[1]
    block_tiles = features.reshape(-1, BLOCK, channels)
    upward = block_tiles[halo_list[1]].reshape(-1, channels)
    downward = block_tiles[halo_list[0]].reshape(-1, channels)
    from_below = passed_along(upward, "slab", 1)
    from_above = passed_along(downward, "slab", -1)
    rows = features.shape[0] + from_below.shape[0] + from_above.shape[0] + 1
    padding = -rows % 8 + 1
    blank_rows = jnp.zeros((padding, channels), features.dtype)
    extended = jnp.concatenate([features, from_below, from_above, blank_rows], axis=0)
    return extended.astype(jnp.float32)


def conv_kernel(active_ref, nbr_ref, ext_ref, w_ref, scale_ref, shift_ref, *rest, has_residual):
    if has_residual:
        res_ref, out_ref, gathered_ref, acc_ref = rest
    else:
        out_ref, gathered_ref, acc_ref = rest
    rows = out_ref.shape[0]
    total = nbr_ref.shape[0] // OFFSETS
    first = pl.program_id(0) * rows
    active = active_ref[0]

    @pl.when(first < active)
    def _():
        for offset in range(OFFSETS):
            slot = offset % 2
            base = offset * total + first

            def pick(i, carry):
                row = nbr_ref[base + i]
                gathered_ref[slot, pl.ds(i, 1), :] = ext_ref[pl.ds(row, 1), :]
                return carry

            lax.fori_loop(0, rows, pick, 0, unroll=8)
            part = jnp.dot(
                gathered_ref[slot].astype(jnp.bfloat16),
                w_ref[offset],
                preferred_element_type=jnp.float32,
            )
            if offset == 0:
                acc_ref[...] = part
            else:
                acc_ref[...] += part
        values = acc_ref[...] * scale_ref[...] + shift_ref[...]
        if has_residual:
            values = values + res_ref[...].astype(jnp.float32)
        living = first + lax.broadcasted_iota(jnp.int32, values.shape, 0) < active
        out_ref[...] = jnp.where(living, jnp.maximum(values, 0.0), 0.0).astype(out_ref.dtype)

    @pl.when(first >= active)
    def _():
        out_ref[...] = jnp.zeros(out_ref.shape, out_ref.dtype)


def convolve(extended, neighbor_flat, weight, scale_vec, shift_vec, residual, active_rows):
    total = neighbor_flat.shape[0] // OFFSETS
    ext_rows, channels = extended.shape
    width = weight.shape[2]
    in_specs = [
        pl.BlockSpec((ext_rows, channels), lambda s, a, n: (0, 0)),
        pl.BlockSpec(weight.shape, lambda s, a, n: (0, 0, 0)),
        pl.BlockSpec((1, width), lambda s, a, n: (0, 0)),
        pl.BlockSpec((1, width), lambda s, a, n: (0, 0)),
    ]
    operands = [extended, weight, scale_vec.reshape(1, width), shift_vec.reshape(1, width)]
    if residual is not None:
        in_specs.append(pl.BlockSpec((CONV_ROWS, width), lambda s, a, n: (s, 0)))
        operands.append(residual)
    grid_spec = pltpu.PrefetchScalarGridSpec(
        num_scalar_prefetch=2,
        grid=(total // CONV_ROWS,),
        in_specs=in_specs,
        out_specs=pl.BlockSpec((CONV_ROWS, width), lambda s, a, n: (s, 0)),
        scratch_shapes=[
            pltpu.VMEM((2, CONV_ROWS, channels), jnp.float32),
            pltpu.VMEM((CONV_ROWS, width), jnp.float32),
        ],
    )
    return pl.pallas_call(
        functools.partial(conv_kernel, has_residual=residual is not None),
        grid_spec=grid_spec,
        out_shape=jax.ShapeDtypeStruct((total, width), jnp.bfloat16),
    )(active_rows.reshape(1), neighbor_flat, *operands)


def pool_kernel(vox_ref, feats_ref, out_ref):
    rows = out_ref.shape[0]
    first = pl.program_id(0) * rows

    @pl.when(pl.program_id(1) == 0)
    def _():
        out_ref[...] = jnp.zeros(out_ref.shape, out_ref.dtype)

    ids = first + lax.broadcasted_iota(jnp.int32, (rows, vox_ref.shape[1]), 0)
    onehot = (ids == vox_ref[...]).astype(jnp.bfloat16)
    out_ref[...] += jnp.dot(onehot, feats_ref[...], preferred_element_type=jnp.float32)


def pool(voxel_of_slot, slot_feats, voxel_total):
    slots, width = slot_feats.shape
    return pl.pallas_call(
        pool_kernel,
        grid=(voxel_total // POOL_ROWS, slots // POOL_COLS),
        in_specs=[
            pl.BlockSpec((1, POOL_COLS), lambda v, s: (0, s)),
            pl.BlockSpec((POOL_COLS, width), lambda v, s: (s, 0)),
        ],
        out_specs=pl.BlockSpec((POOL_ROWS, width), lambda v, s: (v, 0)),
        out_shape=jax.ShapeDtypeStruct((voxel_total, width), jnp.float32),
    )(voxel_of_slot.reshape(1, slots), slot_feats)


def per_device(
    point_feats,
    owners,
    voxel_ids,
    active_count,
    halo_blocks,
    neighbors,
    conv1_weight,
    conv1_scale,
    conv1_shift,
    conv2_weight,
    conv2_scale,
    conv2_shift,
    head_weight,
    head_bias,
):
    slab_count = lax.axis_size("slab")
    point_count, in_width = point_feats.shape
    capacity = 3 * point_count // slab_count
    voxel_total = neighbors.shape[2]
    owner_row = owners[0]
    voxel_row = voxel_ids[0]
    owner_hot = (owner_row[:, None] == jnp.arange(slab_count)[None, :]).astype(jnp.int32)
    earlier = jnp.cumsum(owner_hot, axis=0) - owner_hot
    ranking = jnp.sum(earlier * owner_hot, axis=1)
    slot_number = owner_row * capacity + ranking
    send_feats = (
        jnp.zeros((slab_count * capacity, in_width), jnp.bfloat16)
        .at[slot_number]
        .set(point_feats)
    )
    send_voxels = (
        jnp.full((slab_count * capacity,), voxel_total, jnp.int32).at[slot_number].set(voxel_row)
    )
    got_feats = lax.all_to_all(
        send_feats.reshape(slab_count, capacity, -1), "slab", 0, 0, tiled=True
    )
    got_voxels = lax.all_to_all(
        send_voxels.reshape(slab_count, capacity), "slab", 0, 0, tiled=True
    )
    flat_voxels = got_voxels.reshape(-1)
    slot_total = flat_voxels.shape[0]
    pool_width = -(in_width + 1) // 128 * -128
    slot_rows = jnp.concatenate(
        [
            got_feats.reshape(slot_total, in_width),
            jnp.ones((slot_total, 1), jnp.bfloat16),
            jnp.zeros((slot_total, pool_width - in_width - 1), jnp.bfloat16),
        ],
        axis=1,
    )
    pooled = pool(flat_voxels, slot_rows, voxel_total)
    totals = pooled[:, :in_width]
    counts = pooled[:, in_width]
    voxel_in = (totals / jnp.maximum(counts, 1.0)[:, None]).astype(jnp.bfloat16)
    active_rows = active_count[0, 0] * BLOCK
    halo_list = halo_blocks[0, 0]
    neighbor_flat = neighbors[0].reshape(-1)
    hidden = convolve(
        extend_rows(voxel_in, halo_list),
        neighbor_flat,
        conv1_weight,
        conv1_scale,
        conv1_shift,
        None,
        active_rows,
    )
    refined = convolve(
        extend_rows(hidden, halo_list),
        neighbor_flat,
        conv2_weight,
        conv2_scale,
        conv2_shift,
        hidden,
        active_rows,
    )
    voxel_logits = jnp.dot(refined, head_weight, preferred_element_type=jnp.float32) + head_bias
    voxel_logits = jnp.concatenate(
        [voxel_logits, jnp.zeros((1, voxel_logits.shape[1]), jnp.float32)], axis=0
    )
    slot_logits = voxel_logits[flat_voxels].reshape(slab_count, capacity, -1)
    returned = lax.all_to_all(slot_logits, "slab", 0, 0, tiled=True)
    point_logits = returned.reshape(slab_count * capacity, -1)[slot_number].T
    summed = lax.psum(point_logits, "rot")
    return summed / lax.axis_size("rot")


def solution(mesh):
    return jax.shard_map(
        per_device,
        mesh=mesh,
        in_specs=(
            P("slab", None),
            P("rot", "slab"),
            P("rot", "slab"),
            P("rot", "slab"),
            P("rot", "slab", None, None),
            P("rot", None, "slab"),
            P(),
            P(),
            P(),
            P(),
            P(),
            P(),
            P(),
            P(),
        ),
        out_specs=P(None, "slab"),
        check_vma=False,
    )
```

profile of v0, /device:TPU:24, one launch (start us, length us, event | category | flops | bytes accessed | tf_op | source)
XLA Modules:
  0.0 614.4 jit_solution(8299626256933406299)
XLA Ops:
  6.5 0.0 copy-start
  6.5 0.0 copy-start.3
  6.5 0.0 copy-start.2
  6.5 0.8 fusion.7
  7.3 9.1 %reduce-window.6 = s32[32,16,128]{2,1,0:T(8,128)S(1)} reduce-window(s32[32,16,128]{2,1,0:T(8,128)S(1)} %fusion.7, s32[]{:T(128)} %constant.15.clone.1), window={size=1x1x128 pad=0_0x0_0x127_0}, to_apply=%region_0.0 | reduce-window | flops 8323072 | bytes 524292 | tf_op jit(solution)/shard_map/reduce-window
  16.4 0.1 slice.40
  16.5 0.2 copy.36
  16.8 0.2 reduce-window.9
  17.0 0.1 broadcast_add_fusion
  17.1 0.0 copy-done.3
  17.1 0.1 fusion.6
  17.3 8.2 %scatter_custom_fusion = s32[6144]{0:T(1024)S(1)} fusion(s32[2048]{0:T(1024)S(1)} %bitcast.81, s32[2048]{0:T(1024)} %bitcast.88, s32[]{:T(128)} %constant.13.clone.1), kind=kCustom, calls=%fused_computation.30 | custom fusion | bytes 25088 | tf_op jit(solution)/shard_map/scatter | solution.py:169
  25.5 0.7 all_to_all.12
  26.2 15.5 %all-to-all-start = ((s32[32,1,192]{2,1,0:T(1,128)}), s32[32,1,192]{2,1,0:T(1,128)S(1)}, u32[]{:S(2)}, u32[]{:S(2)}) async-start(s32[32,1,192]{2,1,0:T(1,128)} %all_to_all.12), calls=%async_computation | async-start | bytes 65536 | tf_op jit(solution)/shard_map/all_to_all | solution.py:174
  41.7 0.0 copy-done.2
  41.7 0.3 copy.31
  42.0 7.1 %scatter_custom_fusion.1 = bf16[6144,96]{1,0:T(8,128)(2,1)} fusion(s32[2048]{0:T(1024)S(1)} %bitcast.82, bf16[2048,96]{1,0:T(8,128)(2,1)S(1)} %copy.31, bf16[]{:T(256)} %constant.17.clone.1), kind=kCustom, calls=%fused_computation.14 | custom fusion | bytes 1179650 | tf_op jit(solution)/shard_map/scatter | solution.py:166
  49.1 5.6 all-to-all-done
  54.7 0.0 copy-start.4
  54.7 6.7 %all-to-all-start.1 = ((bf16[32,192,96]{2,1,0:T(8,128)(2,1)}), bf16[32,192,96]{2,1,0:T(8,128)(2,1)S(1)}, u32[]{:S(2)}, u32[]{:S(2)}) async-start(bf16[32,192,96]{2,1,0:T(8,128)(2,1)} %bitcast.11), calls=%async_computation.1 | async-start | bytes 3145728 | tf_op jit(solution)/shard_map/all_to_all | solution.py:171
  62.1 0.1 pad.11.clone
  62.2 0.1 pad.10.clone
  62.3 0.0 copy-done.4
  62.3 0.1 reduce
  62.4 0.1 reshape.206
  62.5 0.7 reshape_reshape.3.vox_ref
  63.2 76.5 %all-to-all-done.1 = bf16[32,192,96]{2,1,0:T(8,128)(2,1)S(1)} async-done(((bf16[32,192,96]{2,1,0:T(8,128)(2,1)}), bf16[32,192,96]{2,1,0:T(8,128)(2,1)S(1)}, u32[]{:S(2)}, u32[]{:S(2)}) %all-to-all-start.1) | async-done | bytes 1179680 | tf_op jit(solution)/shard_map/all_to_all | solution.py:171
  139.6 1.7 maximum_maximum_fusion.feats_ref
  141.3 57.3 %shard_map.136 = f32[2048,128]{1,0:T(8,128)} custom-call(s32[1,6144]{1,0:T(1,128)} %reshape_reshape.3.vox_ref, bf16[6144,128]{1,0:T(8,128)(2,1)} %maximum_maximum_fusion.feats_ref), custom_call_target="tpu_custom_call" | custom-call | tf_op jit(solution)/shard_map/pallas_call | solution.py:125
  198.6 1.9 fusion
  200.5 0.0 copy-done.1
  200.6 0.3 fusion.1
  200.9 0.6 gather_fusion.1
  201.5 0.6 gather_fusion
  202.0 1.8 collective-permute-start
  203.9 1.3 collective-permute-start.1
  205.2 0.0 collective-permute-done
  205.2 1.8 collective-permute-done.1
  207.0 1.5 maximum_convert_fusion.ext_ref
  208.5 45.1 %shard_map.137.rest_0_ = bf16[2048,128]{1,0:T(8,128)(2,1)} custom-call(s32[1]{0:T(128)} %bitcast.active_ref, s32[55296]{0:T(1024)} %bitcast.68, f32[2568,96]{1,0:T(8,128)} %maximum_convert_fusion.ext_ref, bf16[27,96,128]{2,1,0:T(8,128)(2,1)} %w_ref.2, f32[1,128]{1,0:T(1,128)} %bitcast.84, f32[1,128]{1,0:T(1,128)} %bitcast.85), custom_call_target="tpu_custom_call" | custom-call | tf_op jit(solution)/shard_map/pallas_call | solution.py:103
  253.5 1.6 gather_fusion.3
  255.2 1.6 gather_fusion.2
  256.8 41.0 %collective-permute-start.2 = (bf16[256,128]{1,0:T(8,128)(2,1)S(1)}, bf16[256,128]{1,0:T(8,128)(2,1)S(1)}, u32[]{:S(2)}, u32[]{:S(2)}) collective-permute-start(bf16[256,128]{1,0:T(8,128)(2,1)S(1)} %bitcast.78), channel_id=1, source_target_pairs={{0,1},{1,2},{2,3},{3,4},{4,5},{5,6},{6,7},{7,8},{8,9},{9,10},{10,1... | collective-permute-start | bytes 196616 | tf_op jit(solution)/shard_map/ppermute | solution.py:20
  297.8 1.3 collective-permute-start.3
  299.1 0.0 collective-permute-done.2
  299.1 13.1 %collective-permute-done.3 = bf16[256,128]{1,0:T(8,128)(2,1)S(1)} collective-permute-done((bf16[256,128]{1,0:T(8,128)(2,1)S(1)}, bf16[256,128]{1,0:T(8,128)(2,1)S(1)}, u32[]{:S(2)}, u32[]{:S(2)}) %collective-permute-start.3) | collective-permute-done | bytes 65568 | tf_op jit(solution)/shard_map/ppermute | solution.py:20
  312.2 2.5 maximum_convert_fusion.1.ext_ref
  314.7 46.8 %shard_map.138 = bf16[2048,128]{1,0:T(8,128)(2,1)} custom-call(s32[1]{0:T(128)} %bitcast.active_ref, s32[55296]{0:T(1024)} %bitcast.69, f32[2568,128]{1,0:T(8,128)} %maximum_convert_fusion.1.ext_ref, bf16[27,128,128]{2,1,0:T(8,128)(2,1)} %w_ref.3, f32[1,128]{1,0:T(1,128)} %bitcast.86, f32[1,128]{1,0:T(1,128)} %bitcast.87, bf16[2048,128]{1,0:T(8,128)(2,1)} %shard_map.137.rest_0_), custom_call_target="tpu_custom_call" | custom-call | tf_op jit(solution)/shard_map/pallas_call | solution.py:103
  361.6 0.0 copy-done
  361.6 0.0 copy-done.5
  361.6 1.3 convolution_add_fusion
  362.9 0.3 copy.37
  363.2 0.1 concatenate.15.clone
  363.3 20.9 %gather_fusion.4 = f32[6144,8]{1,0:T(8,128)} fusion(f32[2049,8]{1,0:T(8,128)S(1)} %concatenate.15.clone, s32[6144]{0:T(1024)S(1)} %broadcast_clamp_fusion), kind=kCustom, calls=%fused_computation.4 | custom fusion | bytes 417792 | tf_op jit(solution)/shard_map/gather | solution.py:217
  384.2 3.2 copy.33
  387.4 83.1 %all-to-all-start.2 = ((f32[32,192,8]{1,2,0:T(8,128)}), f32[32,192,8]{1,2,0:T(8,128)S(1)}, u32[]{:S(2)}, u32[]{:S(2)}) async-start(f32[32,192,8]{1,2,0:T(8,128)} %copy.33), calls=%async_computation.2 | async-start | bytes 524288 | tf_op jit(solution)/shard_map/all_to_all | solution.py:218
  470.5 0.0 all-reduce.3.cloned.1.call-start
  470.5 22.7 %all-to-all-done.2 = f32[32,192,8]{1,2,0:T(8,128)S(1)} async-done(((f32[32,192,8]{1,2,0:T(8,128)}), f32[32,192,8]{1,2,0:T(8,128)S(1)}, u32[]{:S(2)}, u32[]{:S(2)}) %all-to-all-start.2) | async-done | bytes 196640 | tf_op jit(solution)/shard_map/all_to_all | solution.py:218
  493.2 1.0 copy.34
  494.3 7.6 %gather_fusion.5 = f32[2048,8]{1,0:T(8,128)} fusion(f32[6144,8]{1,0:T(8,128)S(1)} %bitcast.60, s32[2048]{0:T(1024)S(1)} %broadcast_clamp_fusion.1), kind=kCustom, calls=%fused_computation.5 | custom fusion | bytes 139264 | tf_op jit(solution)/shard_map/gather | solution.py:219
  501.8 2.2 copy.35
  504.0 0.0 all-reduce.3.cloned.1.call-update
  504.0 102.1 %all-reduce.3.cloned.1.call-done = f32[8,2048]{1,0:T(8,128)} async-done(((f32[8,2048]{1,0:T(8,128)}), f32[8,2048]{1,0:T(8,128)}) %all-reduce.3.cloned.1.call-update) | async-done | bytes 65552 | tf_op jit(solution)/shard_map/psum | solution.py:220
  606.1 1.5 broadcast_multiply_fusion
  (11 shorter events, 0.1 us)
Async XLA Ops:
  6.5 355.1 %copy-start = (bf16[128,8]{0,1:T(8,128)(2,1)S(1)}, bf16[128,8]{0,1:T(8,128)(2,1)}, u32[]{:S(2)}) copy-start(bf16[128,8]{0,1:T(8,128)(2,1)} %param.26) | copy-start | bytes 6148
  6.5 10.6 %copy-start.3 = (s32[1,2048]{1,0:T(1,128)S(1)}, s32[1,2048]{1,0:T(1,128)}, u32[]{:S(2)}) copy-start(s32[1,2048]{1,0:T(1,128)} %param.15) | copy-start | bytes 24580
  6.5 35.2 %copy-start.2 = (bf16[2048,96]{0,1:T(8,128)(2,1)S(1)}, bf16[2048,96]{0,1:T(8,128)(2,1)}, u32[]{:S(2)}) copy-start(bf16[2048,96]{0,1:T(8,128)(2,1)} %param.14) | copy-start | bytes 1179652
  26.2 28.5 %all-to-all-start = ((s32[32,1,192]{2,1,0:T(1,128)}), s32[32,1,192]{2,1,0:T(1,128)S(1)}, u32[]{:S(2)}, u32[]{:S(2)}) async-start(s32[32,1,192]{2,1,0:T(1,128)} %all_to_all.12), calls=%async_computation | async-start | bytes 65536 | tf_op jit(solution)/shard_map/all_to_all | solution.py:174
  54.7 7.6 %copy-start.4 = (s32[1,1,2,2]{3,2,1,0:T(2,128)S(1)}, s32[1,1,2,2]{3,2,1,0:T(2,128)}, u32[]{:S(2)}) copy-start(s32[1,1,2,2]{3,2,1,0:T(2,128)} %param.18) | copy-start | bytes 52
  54.7 84.9 %all-to-all-start.1 = ((bf16[32,192,96]{2,1,0:T(8,128)(2,1)}), bf16[32,192,96]{2,1,0:T(8,128)(2,1)S(1)}, u32[]{:S(2)}, u32[]{:S(2)}) async-start(bf16[32,192,96]{2,1,0:T(8,128)(2,1)} %bitcast.11), calls=%async_computation.1 | async-start | bytes 3145728 | tf_op jit(solution)/shard_map/all_to_all | solution.py:171
  198.6 2.0 copy-start.1
  202.0 3.2 collective-permute-start
  203.9 3.1 collective-permute-start.1
  256.8 42.3 %collective-permute-start.2 = (bf16[256,128]{1,0:T(8,128)(2,1)S(1)}, bf16[256,128]{1,0:T(8,128)(2,1)S(1)}, u32[]{:S(2)}, u32[]{:S(2)}) collective-permute-start(bf16[256,128]{1,0:T(8,128)(2,1)S(1)} %bitcast.78), channel_id=1, source_target_pairs={{0,1},{1,2},{2,3},{3,4},{4,5},{5,6},{6,7},{7,8},{8,9},{9,10},{10,1... | collective-permute-start | bytes 196616 | tf_op jit(solution)/shard_map/ppermute | solution.py:20
  297.8 14.5 %collective-permute-start.3 = (bf16[256,128]{1,0:T(8,128)(2,1)S(1)}, bf16[256,128]{1,0:T(8,128)(2,1)S(1)}, u32[]{:S(2)}, u32[]{:S(2)}) collective-permute-start(bf16[256,128]{1,0:T(8,128)(2,1)S(1)} %bitcast.76), channel_id=1, source_target_pairs={{1,0},{2,1},{3,2},{4,3},{5,4},{6,5},{7,6},{8,7},{9,8},{10,9},{11,1... | collective-permute-start | bytes 196616 | tf_op jit(solution)/shard_map/ppermute | solution.py:20
  314.7 46.8 %copy-start.5 = (f32[8]{0:T(128)S(1)}, f32[8]{0:T(128)}, u32[]{:S(2)}) copy-start(f32[8]{0:T(128)} %param.27) | copy-start | bytes 100
  387.4 105.8 %all-to-all-start.2 = ((f32[32,192,8]{1,2,0:T(8,128)}), f32[32,192,8]{1,2,0:T(8,128)S(1)}, u32[]{:S(2)}, u32[]{:S(2)}) async-start(f32[32,192,8]{1,2,0:T(8,128)} %copy.33), calls=%async_computation.2 | async-start | bytes 524288 | tf_op jit(solution)/shard_map/all_to_all | solution.py:218
  470.5 135.6 %all-reduce.3.cloned.1.call-start = ((), (), s32[]{:S(2)}) async-start(), calls=%async_computation.3 | async-start | bytes 131072 | tf_op jit(solution)/shard_map/psum | solution.py:220
Sparse Core Ops, SparseCore 0:
  504.2 101.8 all-reduce.2
where the time goes:
time: 617 us; the launch traced here: 614 us
  waiting for transfers between devices  222 us (36%)
  starting transfers between devices  151 us (24%)
  Pallas kernels  149 us (24%)
  local copies, waits for them, and re-layouts  57.3 us (9%)
  other arithmetic  19.9 us (3%)
  between operations  14.3 us (2%)
    psum x1, waiting for transfers between devices, per_device(): summed = lax.psum(point_logits, 'rot')  102 us
    pallas_call x2, Pallas kernels, convolve(): pl.pallas_call(functools.partial(conv_kernel, has_residual=residual is no...  91.9 us
    all_to_all x1, starting transfers between devices, per_device(): returned = lax.all_to_all(slot_logits, 'slab', 0, 0, tiled=True)  83.1 us
    all_to_all x1, waiting for transfers between devices, per_device(): lax.all_to_all(send_feats.reshape(slab_count, capacity, -1), 'slab', 0, 0...  76.5 us
    pallas_call x1, Pallas kernels, pool(): pl.pallas_call(pool_kernel, grid=(voxel_total // POOL_ROWS, slots // POOL...  57.3 us
    ppermute x4, starting transfers between devices, passed_along(): return lax.ppermute(shard, axis, pairs)  45.4 us
    all_to_all x1, waiting for transfers between devices, per_device(): returned = lax.all_to_all(slot_logits, 'slab', 0, 0, tiled=True)  22.7 us
    gather x1, local copies, waits for them, and re-layouts, per_device(): slot_logits = voxel_logits[flat_voxels].reshape(slab_count, capacity, -1)  20.9 us
  transfers between devices with their start and end apart: 8, of which 6 were waited for; matrix products, arithmetic and copies ran while one was open for 1% of the time, Pallas kernels for 0%

commit v1 on v0

v1 whole, which is shorter than its diff:
```python
import functools

import jax
import jax.numpy as jnp
from jax import lax
from jax.experimental import pallas as pl
from jax.experimental.pallas import tpu as pltpu
from jax.sharding import PartitionSpec as P

BLOCK = 128
OFFSETS = 27
CENTRE = 13
UNROLL = 32
CONV_ROWS = 256
POOL_ROWS = 256
POOL_COLS = 512
SLOT_WIDTH = 128
DIGIT = 64


def passed_along(shard, axis, by):
    devices = lax.axis_size(axis)
    pairs = [(i, i + by) for i in range(devices) if 0 <= i + by < devices]
    return lax.ppermute(shard, axis, pairs)


def all_summed(values, axis):
    devices = lax.axis_size(axis)
    if devices & (devices - 1):
        return lax.psum(values, axis)
    step = 1
    while step < devices:
        pairs = [(i, i ^ step) for i in range(devices)]
        values = values + lax.ppermute(values, axis, pairs)
        step *= 2
    return values


def extend_rows(features, halo_list):
    channels = features.shape[1]
    block_tiles = features.reshape(-1, BLOCK, channels)
    upward = block_tiles[halo_list[1]].reshape(-1, channels)
    downward = block_tiles[halo_list[0]].reshape(-1, channels)
    from_below = passed_along(upward, "slab", 1)
    from_above = passed_along(downward, "slab", -1)
    rows = features.shape[0] + from_below.shape[0] + from_above.shape[0] + 1
    padding = -rows % 8 + 1
    blank_rows = jnp.zeros((padding, channels), features.dtype)
    extended = jnp.concatenate([features, from_below, from_above, blank_rows], axis=0)
    return extended.astype(jnp.float32)


def conv_kernel(active_ref, nbr_ref, ext_ref, w_ref, scale_ref, shift_ref, *rest, has_residual):
    if has_residual:
        res_ref, out_ref, gathered_ref, acc_ref = rest
    else:
        out_ref, gathered_ref, acc_ref = rest
    rows = out_ref.shape[0]
    first = pl.multiple_of(pl.program_id(0) * rows, rows)
    active = active_ref[0]

    @pl.when(first < active)
    def _():
        for offset in range(OFFSETS):
            slot = offset % 2
            if offset == CENTRE:
                picked = ext_ref[pl.ds(first, rows), :]
            else:
                base = offset * rows

                def pick(i, carry):
                    row = nbr_ref[base + i]
                    gathered_ref[slot, pl.ds(i, 1), :] = ext_ref[pl.ds(row, 1), :]
                    return carry

                lax.fori_loop(0, rows, pick, 0, unroll=UNROLL)
                picked = gathered_ref[slot]
            part = jnp.dot(
                picked.astype(jnp.bfloat16),
                w_ref[offset],
                preferred_element_type=jnp.float32,
            )
            if offset == 0:
                acc_ref[...] = part
            else:
                acc_ref[...] += part
        values = acc_ref[...] * scale_ref[...] + shift_ref[...]
        if has_residual:
            values = values + res_ref[...].astype(jnp.float32)
        living = first + lax.broadcasted_iota(jnp.int32, values.shape, 0) < active
        out_ref[...] = jnp.where(living, jnp.maximum(values, 0.0), 0.0).astype(out_ref.dtype)

    @pl.when(first >= active)
    def _():
        out_ref[...] = jnp.zeros(out_ref.shape, out_ref.dtype)


def convolve(extended, neighbor_table, weight, scale_vec, shift_vec, residual, active_rows):
    total = neighbor_table.shape[1]
    steps = total // CONV_ROWS
    per_step = OFFSETS * CONV_ROWS
    step_block = -per_step // 1024 * -1024
    neighbor_steps = jnp.pad(
        neighbor_table.reshape(OFFSETS, steps, CONV_ROWS).transpose(1, 0, 2).reshape(steps, -1),
        ((0, 0), (0, step_block - per_step)),
    ).reshape(-1)
    ext_rows, channels = extended.shape
    width = weight.shape[2]
    in_specs = [
        pl.BlockSpec((step_block,), lambda s, a: (s,), memory_space=pltpu.SMEM),
        pl.BlockSpec((ext_rows, channels), lambda s, a: (0, 0)),
        pl.BlockSpec(weight.shape, lambda s, a: (0, 0, 0)),
        pl.BlockSpec((1, width), lambda s, a: (0, 0)),
        pl.BlockSpec((1, width), lambda s, a: (0, 0)),
    ]
    operands = [
        neighbor_steps,
        extended,
        weight,
        scale_vec.reshape(1, width),
        shift_vec.reshape(1, width),
    ]
    if residual is not None:
        in_specs.append(pl.BlockSpec((CONV_ROWS, width), lambda s, a: (s, 0)))
        operands.append(residual)
    grid_spec = pltpu.PrefetchScalarGridSpec(
        num_scalar_prefetch=1,
        grid=(steps,),
        in_specs=in_specs,
        out_specs=pl.BlockSpec((CONV_ROWS, width), lambda s, a: (s, 0)),
        scratch_shapes=[
            pltpu.VMEM((2, CONV_ROWS, channels), jnp.float32),
            pltpu.VMEM((CONV_ROWS, width), jnp.float32),
        ],
    )
    return pl.pallas_call(
        functools.partial(conv_kernel, has_residual=residual is not None),
        grid_spec=grid_spec,
        out_shape=jax.ShapeDtypeStruct((total, width), jnp.bfloat16),
    )(active_rows.reshape(1), *operands)


def pool_kernel(vox_ref, feats_ref, out_ref):
    rows = out_ref.shape[0]
    first = pl.program_id(0) * rows
    summed = None
    for chunk in range(vox_ref.shape[1] // POOL_COLS):
        cols = slice(chunk * POOL_COLS, (chunk + 1) * POOL_COLS)
        ids = first + lax.broadcasted_iota(jnp.int32, (rows, POOL_COLS), 0)
        onehot = (ids == vox_ref[:, cols]).astype(jnp.bfloat16)
        part = jnp.dot(onehot, feats_ref[cols, :], preferred_element_type=jnp.float32)
        summed = part if summed is None else summed + part
    out_ref[...] = summed


def pool(voxel_of_slot, slot_feats, voxel_total):
    slots, width = slot_feats.shape
    return pl.pallas_call(
        pool_kernel,
        grid=(voxel_total // POOL_ROWS,),
        in_specs=[
            pl.BlockSpec((1, slots), lambda v: (0, 0)),
            pl.BlockSpec((slots, width), lambda v: (0, 0)),
        ],
        out_specs=pl.BlockSpec((POOL_ROWS, width), lambda v: (v, 0)),
        out_shape=jax.ShapeDtypeStruct((voxel_total, width), jnp.float32),
    )(voxel_of_slot.reshape(1, slots), slot_feats)


def per_device(
    point_feats,
    owners,
    voxel_ids,
    active_count,
    halo_blocks,
    neighbors,
    conv1_weight,
    conv1_scale,
    conv1_shift,
    conv2_weight,
    conv2_scale,
    conv2_shift,
    head_weight,
    head_bias,
):
    slab_count = lax.axis_size("slab")
    point_count, in_width = point_feats.shape
    capacity = 3 * point_count // slab_count
    voxel_total = neighbors.shape[2]
    owner_row = owners[0]
    voxel_row = voxel_ids[0]
    owner_hot = (owner_row[:, None] == jnp.arange(slab_count)[None, :]).astype(jnp.int32)
    earlier = jnp.cumsum(owner_hot, axis=0) - owner_hot
    ranking = jnp.sum(earlier * owner_hot, axis=1)
    slot_number = owner_row * capacity + ranking
    digits = (voxel_row // DIGIT, voxel_row % DIGIT)
    carried = jnp.concatenate(
        [
            point_feats,
            digits[0].astype(jnp.bfloat16)[:, None],
            digits[1].astype(jnp.bfloat16)[:, None],
            jnp.ones((point_count, 1), jnp.bfloat16),
            jnp.zeros((point_count, SLOT_WIDTH - in_width - 3), jnp.bfloat16),
        ],
        axis=1,
    )
    send_rows = (
        jnp.zeros((slab_count * capacity, SLOT_WIDTH), jnp.bfloat16).at[slot_number].set(carried)
    )
    got_rows = lax.all_to_all(
        send_rows.reshape(slab_count, capacity, SLOT_WIDTH), "slab", 0, 0, tiled=True
    ).reshape(slab_count * capacity, SLOT_WIDTH)
    flat_voxels = (
        got_rows[:, in_width].astype(jnp.int32) * DIGIT
        + got_rows[:, in_width + 1].astype(jnp.int32)
    )
    pooled = pool(flat_voxels, got_rows, voxel_total)
    totals = pooled[:, :in_width]
    counts = pooled[:, in_width + 2]
    voxel_in = (totals / jnp.maximum(counts, 1.0)[:, None]).astype(jnp.bfloat16)
    active_rows = active_count[0, 0] * BLOCK
    halo_list = halo_blocks[0, 0]
    neighbor_table = neighbors[0]
    hidden = convolve(
        extend_rows(voxel_in, halo_list),
        neighbor_table,
        conv1_weight,
        conv1_scale,
        conv1_shift,
        None,
        active_rows,
    )
    refined = convolve(
        extend_rows(hidden, halo_list),
        neighbor_table,
        conv2_weight,
        conv2_scale,
        conv2_shift,
        hidden,
        active_rows,
    )
    voxel_logits = jnp.dot(refined, head_weight, preferred_element_type=jnp.float32) + head_bias
    slot_logits = voxel_logits[flat_voxels].reshape(slab_count, capacity, -1)
    returned = lax.all_to_all(slot_logits, "slab", 0, 0, tiled=True)
    point_logits = returned.reshape(slab_count * capacity, -1)[slot_number].T
    summed = all_summed(point_logits, "rot")
    return summed / lax.axis_size("rot")


def solution(mesh):
    return jax.shard_map(
        per_device,
        mesh=mesh,
        in_specs=(
            P("slab", None),
            P("rot", "slab"),
            P("rot", "slab"),
            P("rot", "slab"),
            P("rot", "slab", None, None),
            P("rot", None, "slab"),
            P(),
            P(),
            P(),
            P(),
            P(),
            P(),
            P(),
            P(),
        ),
        out_specs=P(None, "slab"),
        check_vma=False,
    )
```

time: 617 us -> 398 us (0.65)
  waiting for transfers between devices: 222 us -> 130 us
  Pallas kernels: 149 us -> 91.3 us
  starting transfers between devices: 151 us -> 102 us
  between operations: 14.3 us -> 0.98 us
  local copies, waits for them, and re-layouts: 57.3 us -> 48 us
    psum x1 -> x0, waiting for transfers between devices: 102 us -> none  [per_device(): summed = lax.psum(point_logits, 'rot')]
    pallas_call x1, Pallas kernels: 57.3 us -> 9.95 us  [pool(): pl.pallas_call(pool_kernel, grid=(voxel_total // POOL_ROWS,), in_specs=[p...]
    ppermute x4, starting transfers between devices: 45.4 us -> 17.3 us  [passed_along(): return lax.ppermute(shard, axis, pairs)]
    all_to_all x1, starting transfers between devices: 83.1 us -> 60.8 us  [per_device(): returned = lax.all_to_all(slot_logits, 'slab', 0, 0, tiled=True)]
    ppermute x0 -> x4, waiting for transfers between devices: none -> 19.7 us  [all_summed(): values = values + lax.ppermute(values, axis, pairs)]
    pallas_call x2, Pallas kernels: 91.9 us -> 81.3 us  [convolve(): pl.pallas_call(functools.partial(conv_kernel, has_residual=residual is no...]
    ppermute x0 -> x4, starting transfers between devices: none -> 8.4 us  [all_summed(): values = values + lax.ppermute(values, axis, pairs)]
    scatter x2 -> x1, local copies, waits for them, and re-layouts: 15.4 us -> 7.12 us  [per_device(): jnp.zeros((slab_count * capacity, SLOT_WIDTH), jnp.bfloat16).at[slot_number]]
  transfers between devices with their start and end apart: 8 -> 10, of which waited for: 6 -> 8; matrix products, arithmetic and copies ran while one was open for 1% -> 0% of each run, Pallas kernels for 0% -> 0%
where the time goes in v1:
time: 398 us; the launch traced here: 396 us
  waiting for transfers between devices  130 us (33%)
  starting transfers between devices  102 us (26%)
  Pallas kernels  91.3 us (23%)
  local copies, waits for them, and re-layouts  48 us (12%)
  other arithmetic  22.8 us (6%)
    pallas_call x2, Pallas kernels, convolve(): pl.pallas_call(functools.partial(conv_kernel, has_residual=residual is no...  81.3 us
    all_to_all x1, waiting for transfers between devices, per_device(): lax.all_to_all(send_rows.reshape(slab_count, capacity, SLOT_WIDTH), 'slab...  77.5 us
    all_to_all x1, starting transfers between devices, per_device(): returned = lax.all_to_all(slot_logits, 'slab', 0, 0, tiled=True)  60.8 us
    all_to_all x1, waiting for transfers between devices, per_device(): returned = lax.all_to_all(slot_logits, 'slab', 0, 0, tiled=True)  22.7 us
    gather x1, local copies, waits for them, and re-layouts, per_device(): slot_logits = voxel_logits[flat_voxels].reshape(slab_count, capacity, -1)  20.9 us
    ppermute x4, waiting for transfers between devices, all_summed(): values = values + lax.ppermute(values, axis, pairs)  19.7 us
    ppermute x4, starting transfers between devices, passed_along(): return lax.ppermute(shard, axis, pairs)  17.3 us
    all_to_all x1, starting transfers between devices, per_device(): lax.all_to_all(send_rows.reshape(slab_count, capacity, SLOT_WIDTH), 'slab...  15.6 us
  transfers between devices with their start and end apart: 10, of which 8 were waited for; matrix products, arithmetic and copies ran while one was open for 0% of the time, Pallas kernels for 0%

profile of v1, /device:TPU:24, one launch (start us, length us, event | category | flops | bytes accessed | tf_op | source)
XLA Modules:
  0.0 396.3 jit_solution(11294040292240325624)
XLA Ops:
  0.0 0.0 copy-start
  0.0 0.8 fusion.10
  0.8 0.7 fusion.11
  1.5 0.7 fusion.9
  2.3 9.1 %reduce-window.6 = s32[32,16,128]{2,1,0:T(8,128)S(1)} reduce-window(s32[32,16,128]{2,1,0:T(8,128)S(1)} %fusion.9, s32[]{:T(128)} %constant.25.clone.1), window={size=1x1x128 pad=0_0x0_0x127_0}, to_apply=%region_0.0 | reduce-window | flops 8323072 | bytes 524292 | tf_op jit(solution)/shard_map/reduce-window
  11.3 0.1 slice.48
  11.5 0.2 copy.44
  11.7 0.2 reduce-window.9
  11.9 0.1 broadcast_add_fusion
  12.1 0.0 copy-done.5
  12.1 0.1 fusion.8
  12.2 0.0 copy-done.3
  12.3 0.4 concatenate.9
  12.7 0.3 copy.39
  13.0 7.1 %scatter_custom_fusion = bf16[6144,128]{1,0:T(8,128)(2,1)} fusion(s32[2048]{0:T(1024)S(1)} %bitcast.105, bf16[2048,128]{1,0:T(8,128)(2,1)S(1)} %copy.39, bf16[]{:T(256)} %constant.26.clone.1), kind=kCustom, calls=%fused_computation.16 | custom fusion | bytes 1572866 | tf_op jit(solution)/shard_map/scatter | solution.py:208
  20.1 15.6 %all-to-all-start = ((bf16[32,192,128]{2,1,0:T(8,128)(2,1)}), bf16[32,192,128]{2,1,0:T(8,128)(2,1)S(1)}, u32[]{:S(2)}, u32[]{:S(2)}) async-start(bf16[32,192,128]{2,1,0:T(8,128)(2,1)} %bitcast.12), calls=%async_computation | async-start | bytes 3145728 | tf_op jit(solution)/shard_map/all_to_all | solution.py:210
  35.7 0.0 copy-done.4
  35.7 0.5 reduce
  36.3 0.1 copy.45
  36.4 0.0 copy-done.6
  36.4 77.5 %all-to-all-done = bf16[32,192,128]{2,1,0:T(8,128)(2,1)S(1)} async-done(((bf16[32,192,128]{2,1,0:T(8,128)(2,1)}), bf16[32,192,128]{2,1,0:T(8,128)(2,1)S(1)}, u32[]{:S(2)}, u32[]{:S(2)}) %all-to-all-start) | async-done | bytes 1572896 | tf_op jit(solution)/shard_map/all_to_all | solution.py:210
  113.9 3.5 fusion
  117.4 0.0 copy-done.1
  117.4 9.9 %shard_map.136 = f32[2048,128]{1,0:T(8,128)} custom-call(s32[1,6144]{1,0:T(1,128)} %bitcast.95, bf16[6144,128]{1,0:T(8,128)(2,1)} %bitcast.82), custom_call_target="tpu_custom_call" | custom-call | tf_op jit(solution)/shard_map/pallas_call | solution.py:158
  127.4 1.9 fusion.2
  129.3 0.0 copy-done.2
  129.3 0.3 fusion.3
  129.7 0.6 gather_fusion.1
  130.2 0.6 gather_fusion
  130.8 1.8 collective-permute-start
  132.6 1.3 collective-permute-start.1
  134.6 0.8 copy.46
  135.4 0.0 collective-permute-done
  135.4 0.4 collective-permute-done.1
  135.8 1.5 maximum_convert_fusion.ext_ref
  137.3 40.4 %shard_map.137.rest_0_ = bf16[2048,128]{1,0:T(8,128)(2,1)} custom-call(s32[1]{0:T(128)} %bitcast.active_ref, s32[57344]{0:T(1024)} %bitcast.88, f32[2568,96]{1,0:T(8,128)} %maximum_convert_fusion.ext_ref, bf16[27,96,128]{2,1,0:T(8,128)(2,1)} %w_ref.2, f32[1,128]{1,0:T(1,128)} %bitcast.107, f32[1,128]{1,0:T(1,128)} %bitcast.108), custom_call_target="tpu_custom_call" | custom-call | tf_op jit(solution)/shard_map/pallas_call | solution.py:136
  177.7 1.6 gather_fusion.3
  179.3 1.6 gather_fusion.2
  180.9 12.8 %collective-permute-start.2 = (bf16[256,128]{1,0:T(8,128)(2,1)S(1)}, bf16[256,128]{1,0:T(8,128)(2,1)S(1)}, u32[]{:S(2)}, u32[]{:S(2)}) collective-permute-start(bf16[256,128]{1,0:T(8,128)(2,1)S(1)} %bitcast.103), channel_id=1, source_target_pairs={{0,1},{1,2},{2,3},{3,4},{4,5},{5,6},{6,7},{7,8},{8,9},{9,10},{10,1... | collective-permute-start | bytes 196616 | tf_op jit(solution)/shard_map/ppermute | solution.py:24
  193.6 1.5 collective-permute-start.3
  195.1 0.0 collective-permute-done.2
  195.1 9.5 %collective-permute-done.3 = bf16[256,128]{1,0:T(8,128)(2,1)S(1)} collective-permute-done((bf16[256,128]{1,0:T(8,128)(2,1)S(1)}, bf16[256,128]{1,0:T(8,128)(2,1)S(1)}, u32[]{:S(2)}, u32[]{:S(2)}) %collective-permute-start.3) | collective-permute-done | bytes 65568 | tf_op jit(solution)/shard_map/ppermute | solution.py:24
  204.6 2.5 maximum_convert_fusion.1.ext_ref
  207.1 40.9 %shard_map.138 = bf16[2048,128]{1,0:T(8,128)(2,1)} custom-call(s32[1]{0:T(128)} %bitcast.active_ref, s32[57344]{0:T(1024)} %bitcast.89, f32[2568,128]{1,0:T(8,128)} %maximum_convert_fusion.1.ext_ref, bf16[27,128,128]{2,1,0:T(8,128)(2,1)} %w_ref.3, f32[1,128]{1,0:T(1,128)} %bitcast.109, f32[1,128]{1,0:T(1,128)} %bitcast.110, bf16[2048,128]{1,0:T(8,128)(2,1)} %shard_map.137.rest_0_), custom_call_target="tpu_custom_call" | custom-call | tf_op jit(solution)/shard_map/pallas_call | solution.py:136
  248.1 0.0 copy-done
  248.1 0.0 copy-done.7
  248.1 1.3 convolution_add_fusion
  249.4 0.3 copy.40
  249.7 20.9 %gather_fusion.4 = f32[6144,8]{1,0:T(8,128)} fusion(f32[2048,8]{1,0:T(8,128)S(1)} %copy.40, s32[6144]{0:T(1024)S(1)} %broadcast_clamp_fusion), kind=kCustom, calls=%fused_computation.4 | custom fusion | bytes 417792 | tf_op jit(solution)/shard_map/gather | solution.py:243
  270.7 3.2 copy.41
  273.9 60.8 %all-to-all-start.1 = ((f32[32,192,8]{1,2,0:T(8,128)}), f32[32,192,8]{1,2,0:T(8,128)S(1)}, u32[]{:S(2)}, u32[]{:S(2)}) async-start(f32[32,192,8]{1,2,0:T(8,128)} %copy.41), calls=%async_computation.1 | async-start | bytes 524288 | tf_op jit(solution)/shard_map/all_to_all | solution.py:244
  334.7 22.7 %all-to-all-done.1 = f32[32,192,8]{1,2,0:T(8,128)S(1)} async-done(((f32[32,192,8]{1,2,0:T(8,128)}), f32[32,192,8]{1,2,0:T(8,128)S(1)}, u32[]{:S(2)}, u32[]{:S(2)}) %all-to-all-start.1) | async-done | bytes 196640 | tf_op jit(solution)/shard_map/all_to_all | solution.py:244
  357.5 1.0 copy.42
  358.5 7.6 %gather_fusion.5 = f32[2048,8]{1,0:T(8,128)} fusion(f32[6144,8]{1,0:T(8,128)S(1)} %bitcast.80, s32[2048]{0:T(1024)S(1)} %broadcast_clamp_fusion.1), kind=kCustom, calls=%fused_computation.5 | custom fusion | bytes 139264 | tf_op jit(solution)/shard_map/gather | solution.py:245
  366.1 1.5 copy.43
  367.6 2.6 collective-permute-start.4
  370.2 3.5 collective-permute-done.4
  373.7 1.9 collective-permute-start.5
  375.7 5.7 %collective-permute-done.5 = f32[8,2048]{1,0:T(8,128)S(1)} collective-permute-done((f32[8,2048]{1,0:T(8,128)S(1)}, f32[8,2048]{1,0:T(8,128)S(1)}, u32[]{:S(2)}, u32[]{:S(2)}) %collective-permute-start.5) | collective-permute-done | bytes 65568 | tf_op jit(solution)/shard_map/ppermute | solution.py:34
  381.4 1.9 collective-permute-start.6
  383.3 4.7 %collective-permute-done.6 = f32[8,2048]{1,0:T(8,128)S(1)} collective-permute-done((f32[8,2048]{1,0:T(8,128)S(1)}, f32[8,2048]{1,0:T(8,128)S(1)}, u32[]{:S(2)}, u32[]{:S(2)}) %collective-permute-start.6) | collective-permute-done | bytes 65568 | tf_op jit(solution)/shard_map/ppermute | solution.py:34
  388.0 1.9 collective-permute-start.7
  390.0 5.7 %collective-permute-done.7 = f32[8,2048]{1,0:T(8,128)S(1)} collective-permute-done((f32[8,2048]{1,0:T(8,128)S(1)}, f32[8,2048]{1,0:T(8,128)S(1)}, u32[]{:S(2)}, u32[]{:S(2)}) %collective-permute-start.7) | collective-permute-done | bytes 65568 | tf_op jit(solution)/shard_map/ppermute | solution.py:34
  395.7 0.6 add_multiply_fusion
  (21 shorter events, 0.1 us)
Async XLA Ops:
  0.0 248.1 %copy-start = (bf16[128,8]{0,1:T(8,128)(2,1)S(1)}, bf16[128,8]{0,1:T(8,128)(2,1)}, u32[]{:S(2)}) copy-start(bf16[128,8]{0,1:T(8,128)(2,1)} %param.26) | copy-start | bytes 6148
  0.0 12.1 %copy-start.5 = (s32[1,2048]{1,0:T(1,128)S(1)}, s32[1,2048]{1,0:T(1,128)}, u32[]{:S(2)}) copy-start(s32[1,2048]{1,0:T(1,128)} %param.15) | copy-start | bytes 24580
  0.0 12.2 %copy-start.3 = (bf16[2048,96]{0,1:T(8,128)(2,1)S(1)}, bf16[2048,96]{0,1:T(8,128)(2,1)}, u32[]{:S(2)}) copy-start(bf16[2048,96]{0,1:T(8,128)(2,1)} %param.14) | copy-start | bytes 1179652
  20.1 15.6 %copy-start.4 = (s32[1,27,2048]{2,0,1:T(1,128)S(1)}, s32[1,27,2048]{2,0,1:T(1,128)}, u32[]{:S(2)}) copy-start(s32[1,27,2048]{2,0,1:T(1,128)} %param.19) | copy-start | bytes 663556
  20.1 16.3 %copy-start.6 = (s32[1,1,2,2]{3,2,1,0:T(2,128)S(1)}, s32[1,1,2,2]{3,2,1,0:T(2,128)}, u32[]{:S(2)}) copy-start(s32[1,1,2,2]{3,2,1,0:T(2,128)} %param.18) | copy-start | bytes 52
  20.1 93.8 %all-to-all-start = ((bf16[32,192,128]{2,1,0:T(8,128)(2,1)}), bf16[32,192,128]{2,1,0:T(8,128)(2,1)S(1)}, u32[]{:S(2)}, u32[]{:S(2)}) async-start(bf16[32,192,128]{2,1,0:T(8,128)(2,1)} %bitcast.12), calls=%async_computation | async-start | bytes 3145728 | tf_op jit(solution)/shard_map/all_to_all | solution.py:210
  113.9 3.5 copy-start.1
  127.4 2.0 copy-start.2
  130.8 4.6 %collective-permute-start = (bf16[256,96]{1,0:T(8,128)(2,1)S(1)}, bf16[256,96]{1,0:T(8,128)(2,1)S(1)}, u32[]{:S(2)}, u32[]{:S(2)}) collective-permute-start(bf16[256,96]{1,0:T(8,128)(2,1)S(1)} %bitcast.101), channel_id=1, source_target_pairs={{0,1},{1,2},{2,3},{3,4},{4,5},{5,6},{6,7},{7,8},{8,9},{9,10},{10,1... | collective-permute-start | bytes 147464 | tf_op jit(solution)/shard_map/ppermute | solution.py:24
  132.6 3.1 collective-permute-start.1
  180.9 14.3 %collective-permute-start.2 = (bf16[256,128]{1,0:T(8,128)(2,1)S(1)}, bf16[256,128]{1,0:T(8,128)(2,1)S(1)}, u32[]{:S(2)}, u32[]{:S(2)}) collective-permute-start(bf16[256,128]{1,0:T(8,128)(2,1)S(1)} %bitcast.103), channel_id=1, source_target_pairs={{0,1},{1,2},{2,3},{3,4},{4,5},{5,6},{6,7},{7,8},{8,9},{9,10},{10,1... | collective-permute-start | bytes 196616 | tf_op jit(solution)/shard_map/ppermute | solution.py:24
  193.6 11.0 %collective-permute-start.3 = (bf16[256,128]{1,0:T(8,128)(2,1)S(1)}, bf16[256,128]{1,0:T(8,128)(2,1)S(1)}, u32[]{:S(2)}, u32[]{:S(2)}) collective-permute-start(bf16[256,128]{1,0:T(8,128)(2,1)S(1)} %bitcast.102), channel_id=1, source_target_pairs={{1,0},{2,1},{3,2},{4,3},{5,4},{6,5},{7,6},{8,7},{9,8},{10,9},{11,1... | collective-permute-start | bytes 196616 | tf_op jit(solution)/shard_map/ppermute | solution.py:24
  207.1 40.9 %copy-start.7 = (f32[8]{0:T(128)S(1)}, f32[8]{0:T(128)}, u32[]{:S(2)}) copy-start(f32[8]{0:T(128)} %param.27) | copy-start | bytes 100
  273.9 83.6 %all-to-all-start.1 = ((f32[32,192,8]{1,2,0:T(8,128)}), f32[32,192,8]{1,2,0:T(8,128)S(1)}, u32[]{:S(2)}, u32[]{:S(2)}) async-start(f32[32,192,8]{1,2,0:T(8,128)} %copy.41), calls=%async_computation.1 | async-start | bytes 524288 | tf_op jit(solution)/shard_map/all_to_all | solution.py:244
  367.6 6.2 %collective-permute-start.4 = (f32[8,2048]{1,0:T(8,128)S(1)}, f32[8,2048]{1,0:T(8,128)S(1)}, u32[]{:S(2)}, u32[]{:S(2)}) collective-permute-start(f32[8,2048]{1,0:T(8,128)S(1)} %bitcast.94), channel_id=1, source_target_pairs={{0,32},{32,0},{64,96},{96,64},{128,160},{160,128},{192,224},{224,1... | collective-permute-start | bytes 196616 | tf_op jit(solution)/shard_map/ppermute | solution.py:34
  373.7 7.7 %collective-permute-start.5 = (f32[8,2048]{1,0:T(8,128)S(1)}, f32[8,2048]{1,0:T(8,128)S(1)}, u32[]{:S(2)}, u32[]{:S(2)}) collective-permute-start(f32[8,2048]{1,0:T(8,128)S(1)} %bitcast_add_fusion.1), channel_id=1, source_target_pairs={{0,64},{32,96},{64,0},{96,32},{128,192},{160,224},{192,128},{224,1... | collective-permute-start | bytes 196616 | tf_op jit(solution)/shard_map/ppermute | solution.py:34
  381.4 6.6 %collective-permute-start.6 = (f32[8,2048]{1,0:T(8,128)S(1)}, f32[8,2048]{1,0:T(8,128)S(1)}, u32[]{:S(2)}, u32[]{:S(2)}) collective-permute-start(f32[8,2048]{1,0:T(8,128)S(1)} %add.119), channel_id=1, source_target_pairs={{0,128},{32,160},{64,192},{96,224},{128,0},{160,32},{192,64},{224,... | collective-permute-start | bytes 196616 | tf_op jit(solution)/shard_map/ppermute | solution.py:34
  388.0 7.7 %collective-permute-start.7 = (f32[8,2048]{1,0:T(8,128)S(1)}, f32[8,2048]{1,0:T(8,128)S(1)}, u32[]{:S(2)}, u32[]{:S(2)}) collective-permute-start(f32[8,2048]{1,0:T(8,128)S(1)} %add.120), channel_id=1, source_target_pairs={{0,256},{32,288},{64,320},{96,352},{128,384},{160,416},{192,448},{... | collective-permute-start | bytes 196616 | tf_op jit(solution)/shard_map/ppermute | solution.py:34

commit v2 on v1

--- a/solution.py
+++ b/solution.py
@@ -14,7 +14,6 @@
 CONV_ROWS = 256
 POOL_ROWS = 256
 POOL_COLS = 512
-SLOT_WIDTH = 128
 DIGIT = 64
 
 
@@ -73,7 +72,7 @@
                     gathered_ref[slot, pl.ds(i, 1), :] = ext_ref[pl.ds(row, 1), :]
                     return carry
 
-                lax.fori_loop(0, rows, pick, 0, unroll=UNROLL)
+                lax.fori_loop(0, rows, pick, 0, unroll=True)
                 picked = gathered_ref[slot]
             part = jnp.dot(
                 picked.astype(jnp.bfloat16),
@@ -200,16 +199,20 @@
             digits[0].astype(jnp.bfloat16)[:, None],
             digits[1].astype(jnp.bfloat16)[:, None],
             jnp.ones((point_count, 1), jnp.bfloat16),
-            jnp.zeros((point_count, SLOT_WIDTH - in_width - 3), jnp.bfloat16),
         ],
         axis=1,
     )
+    row_width = carried.shape[1]
     send_rows = (
-        jnp.zeros((slab_count * capacity, SLOT_WIDTH), jnp.bfloat16).at[slot_number].set(carried)
-    )
-    got_rows = lax.all_to_all(
-        send_rows.reshape(slab_count, capacity, SLOT_WIDTH), "slab", 0, 0, tiled=True
-    ).reshape(slab_count * capacity, SLOT_WIDTH)
+        jnp.zeros((slab_count * capacity, row_width), jnp.bfloat16).at[slot_number].set(carried)
+    )
+    chunk = capacity * row_width
+    dense = -chunk // 128 * -128
+    packed = jnp.pad(send_rows.reshape(slab_count, chunk), ((0, 0), (0, dense - chunk)))
+    got_packed = lax.all_to_all(
+        packed.reshape(slab_count, dense // 128, 128), "slab", 0, 0, tiled=True
+    )
+    got_rows = got_packed.reshape(slab_count, dense)[:, :chunk].reshape(-1, row_width)
     flat_voxels = (
         got_rows[:, in_width].astype(jnp.int32) * DIGIT
         + got_rows[:, in_width + 1].astype(jnp.int32)

time: 398 us -> 354 us (0.89)
  starting transfers between devices: 102 us -> 67.7 us
  waiting for transfers between devices: 130 us -> 107 us
  local copies, waits for them, and re-layouts: 48 us -> 56.3 us
  Pallas kernels: 91.3 us -> 97.3 us
    all_to_all x1, starting transfers between devices: 60.8 us -> 21.4 us  [per_device(): returned = lax.all_to_all(slot_logits, 'slab', 0, 0, tiled=True)]
    all_to_all x1, waiting for transfers between devices: 77.5 us -> 63.5 us  [per_device(): lax.all_to_all(packed.reshape(slab_count, dense // 128, 128), 'slab', 0,...]
    reshape x0 -> x3, local copies, waits for them, and re-layouts: none -> 9.23 us  [the longest x1 5.79 us: per_device(): got_packed.reshape(slab_count, dense)[:, :chunk].reshape(-1, row_width)]
    ppermute x4, waiting for transfers between devices: 9.89 us -> 1.74 us  [passed_along(): return lax.ppermute(shard, axis, pairs)]
    pallas_call x2, Pallas kernels: 81.3 us -> 87.3 us  [convolve(): pl.pallas_call(functools.partial(conv_kernel, has_residual=residual is no...]
    ppermute x4, starting transfers between devices: 17.3 us -> 21.6 us  [passed_along(): return lax.ppermute(shard, axis, pairs)]
where the time goes in v2:
time: 354 us; the launch traced here: 352 us
  waiting for transfers between devices  107 us (30%)
  Pallas kernels  97.3 us (27%)
  starting transfers between devices  67.7 us (19%)
  local copies, waits for them, and re-layouts  56.3 us (16%)
  other arithmetic  22.2 us (6%)
    pallas_call x2, Pallas kernels, convolve(): pl.pallas_call(functools.partial(conv_kernel, has_residual=residual is no...  87.3 us
    all_to_all x1, waiting for transfers between devices, per_device(): lax.all_to_all(packed.reshape(slab_count, dense // 128, 128), 'slab', 0,...  63.5 us
    all_to_all x1, waiting for transfers between devices, per_device(): returned = lax.all_to_all(slot_logits, 'slab', 0, 0, tiled=True)  22.7 us
    ppermute x4, starting transfers between devices, passed_along(): return lax.ppermute(shard, axis, pairs)  21.6 us
    all_to_all x1, starting transfers between devices, per_device(): returned = lax.all_to_all(slot_logits, 'slab', 0, 0, tiled=True)  21.4 us
    gather x1, local copies, waits for them, and re-layouts, per_device(): slot_logits = voxel_logits[flat_voxels].reshape(slab_count, capacity, -1)  20.9 us
    ppermute x4, waiting for transfers between devices, all_summed(): values = values + lax.ppermute(values, axis, pairs)  18.7 us
    all_to_all x1, starting transfers between devices, per_device(): lax.all_to_all(packed.reshape(slab_count, dense // 128, 128), 'slab', 0,...  15.8 us
  transfers between devices with their start and end apart: 10, of which 8 were waited for; matrix products, arithmetic and copies ran while one was open for 0% of the time, Pallas kernels for 0%

profile of v2, /device:TPU:24, one launch (start us, length us, event | category | flops | bytes accessed | tf_op | source)
XLA Modules:
  0.0 352.5 jit_solution(7254592551771342865)
XLA Ops:
  0.0 0.0 copy-start
  0.0 0.8 fusion.11
  0.8 0.7 fusion.9
  1.6 9.1 %reduce-window.6 = s32[32,16,128]{2,1,0:T(8,128)S(1)} reduce-window(s32[32,16,128]{2,1,0:T(8,128)S(1)} %fusion.9, s32[]{:T(128)} %constant.46.clone.1), window={size=1x1x128 pad=0_0x0_0x127_0}, to_apply=%region_0.0 | reduce-window | flops 8323072 | bytes 524292 | tf_op jit(solution)/shard_map/reduce-window
  10.6 0.1 slice.52
  10.8 0.2 copy.44
  11.0 0.2 reduce-window.9
  11.2 0.1 broadcast_add_fusion
  11.4 0.1 fusion.8
  11.5 0.1 pad.22.clone
  11.6 0.0 copy-done.3
  11.6 0.1 maximum_maximum_fusion
  11.7 0.3 copy.39
  12.0 6.3 %scatter_custom_fusion = bf16[6144,99]{1,0:T(8,128)(2,1)S(1)} fusion(s32[2048]{0:T(1024)S(1)} %bitcast.109, bf16[2048,99]{1,0:T(8,128)(2,1)S(1)} %copy.39, bf16[]{:T(256)} %constant.47.clone.1), kind=kCustom, calls=%fused_computation.17 | custom fusion | bytes 1216514 | tf_op jit(solution)/shard_map/scatter | solution.py:207
  18.3 1.9 reshape.313
  20.3 0.1 pad.10
  20.4 1.5 reshape.314
  21.8 15.8 %all-to-all-start = ((bf16[32,149,128]{2,1,0:T(8,128)(2,1)}), bf16[32,149,128]{2,1,0:T(8,128)(2,1)S(1)}, u32[]{:S(2)}, u32[]{:S(2)}) async-start(bf16[32,149,128]{2,1,0:T(8,128)(2,1)} %reshape.314), calls=%async_computation | async-start | bytes 2490368 | tf_op jit(solution)/shard_map/all_to_all | solution.py:212
  37.6 0.0 copy-done.4
  37.7 0.5 reduce
  38.2 0.1 copy.45
  38.4 63.5 %all-to-all-done = bf16[32,149,128]{2,1,0:T(8,128)(2,1)S(1)} async-done(((bf16[32,149,128]{2,1,0:T(8,128)(2,1)}), bf16[32,149,128]{2,1,0:T(8,128)(2,1)S(1)}, u32[]{:S(2)}, u32[]{:S(2)}) %all-to-all-start) | async-done | bytes 1220640 | tf_op jit(solution)/shard_map/all_to_all | solution.py:212
  101.8 0.2 copy.51
  102.0 5.8 %reshape.316.feats_ref = bf16[6144,99]{1,0:T(8,128)(2,1)S(1)} reshape(bf16[32,19008]{1,0:T(8,128)(2,1)S(1)} %bitcast.89) | data formatting | bytes 2433024 | tf_op jit(solution)/shard_map/reshape | solution.py:215
  107.8 3.5 fusion
  111.3 9.9 %shard_map.136 = f32[2048,99]{1,0:T(8,128)} custom-call(s32[1,6144]{1,0:T(1,128)} %bitcast.99, bf16[6144,99]{1,0:T(8,128)(2,1)} %copy-done.1), custom_call_target="tpu_custom_call" | custom-call | tf_op jit(solution)/shard_map/pallas_call | solution.py:157
  121.3 1.9 fusion.2
  123.2 0.3 fusion.3
  123.6 0.6 gather_fusion.1
  124.1 0.6 gather_fusion
  124.7 1.9 collective-permute-start
  126.6 1.5 collective-permute-start.1
  128.8 0.8 copy.46
  129.6 0.0 collective-permute-done
  129.6 0.2 collective-permute-done.1
  129.8 1.5 maximum_convert_fusion.ext_ref
  131.2 43.5 %shard_map.137.rest_0_ = bf16[2048,128]{1,0:T(8,128)(2,1)} custom-call(s32[1]{0:T(128)} %bitcast.active_ref, s32[57344]{0:T(1024)} %bitcast.92, f32[2568,96]{1,0:T(8,128)} %maximum_convert_fusion.ext_ref, bf16[27,96,128]{2,1,0:T(8,128)(2,1)} %w_ref.2, f32[1,128]{1,0:T(1,128)} %bitcast.111, f32[1,128]{1,0:T(1,128)} %bitcast.112), custom_call_target="tpu_custom_call" | custom-call | tf_op jit(solution)/shard_map/pallas_call | solution.py:135
  174.8 1.6 gather_fusion.3
  176.4 1.6 gather_fusion.2
  178.0 16.6 %collective-permute-start.2 = (bf16[256,128]{1,0:T(8,128)(2,1)S(1)}, bf16[256,128]{1,0:T(8,128)(2,1)S(1)}, u32[]{:S(2)}, u32[]{:S(2)}) collective-permute-start(bf16[256,128]{1,0:T(8,128)(2,1)S(1)} %bitcast.107), channel_id=1, source_target_pairs={{0,1},{1,2},{2,3},{3,4},{4,5},{5,6},{6,7},{7,8},{8,9},{9,10},{10,1... | collective-permute-start | bytes 196616 | tf_op jit(solution)/shard_map/ppermute | solution.py:23
  194.6 1.6 collective-permute-start.3
  196.2 0.0 collective-permute-done.2
  196.2 1.6 collective-permute-done.3
  197.7 2.5 maximum_convert_fusion.1.ext_ref
  200.3 43.8 %shard_map.138 = bf16[2048,128]{1,0:T(8,128)(2,1)} custom-call(s32[1]{0:T(128)} %bitcast.active_ref, s32[57344]{0:T(1024)} %bitcast.93, f32[2568,128]{1,0:T(8,128)} %maximum_convert_fusion.1.ext_ref, bf16[27,128,128]{2,1,0:T(8,128)(2,1)} %w_ref.3, f32[1,128]{1,0:T(1,128)} %bitcast.113, f32[1,128]{1,0:T(1,128)} %bitcast.114, bf16[2048,128]{1,0:T(8,128)(2,1)} %shard_map.137.rest_0_), custom_call_target="tpu_custom_call" | custom-call | tf_op jit(solution)/shard_map/pallas_call | solution.py:135
  244.0 0.0 copy-done
  244.0 1.3 convolution_add_fusion
  245.3 0.3 copy.40
  245.7 20.9 %gather_fusion.4 = f32[6144,8]{1,0:T(8,128)} fusion(f32[2048,8]{1,0:T(8,128)S(1)} %copy.40, s32[6144]{0:T(1024)S(1)} %broadcast_clamp_fusion), kind=kCustom, calls=%fused_computation.4 | custom fusion | bytes 417792 | tf_op jit(solution)/shard_map/gather | solution.py:246
  266.6 3.2 copy.41
  269.8 21.4 %all-to-all-start.1 = ((f32[32,192,8]{1,2,0:T(8,128)}), f32[32,192,8]{1,2,0:T(8,128)S(1)}, u32[]{:S(2)}, u32[]{:S(2)}) async-start(f32[32,192,8]{1,2,0:T(8,128)} %copy.41), calls=%async_computation.1 | async-start | bytes 524288 | tf_op jit(solution)/shard_map/all_to_all | solution.py:247
  291.3 22.7 %all-to-all-done.1 = f32[32,192,8]{1,2,0:T(8,128)S(1)} async-done(((f32[32,192,8]{1,2,0:T(8,128)}), f32[32,192,8]{1,2,0:T(8,128)S(1)}, u32[]{:S(2)}, u32[]{:S(2)}) %all-to-all-start.1) | async-done | bytes 196640 | tf_op jit(solution)/shard_map/all_to_all | solution.py:247
  314.0 1.0 copy.42
  315.1 7.6 %gather_fusion.5 = f32[2048,8]{1,0:T(8,128)} fusion(f32[6144,8]{1,0:T(8,128)S(1)} %bitcast.84, s32[2048]{0:T(1024)S(1)} %broadcast_clamp_fusion.1), kind=kCustom, calls=%fused_computation.5 | custom fusion | bytes 139264 | tf_op jit(solution)/shard_map/gather | solution.py:248
  322.6 1.5 copy.43
  324.1 1.9 collective-permute-start.4
  326.1 4.2 %collective-permute-done.4 = f32[8,2048]{1,0:T(8,128)S(1)} collective-permute-done((f32[8,2048]{1,0:T(8,128)S(1)}, f32[8,2048]{1,0:T(8,128)S(1)}, u32[]{:S(2)}, u32[]{:S(2)}) %collective-permute-start.4) | collective-permute-done | bytes 65568 | tf_op jit(solution)/shard_map/ppermute | solution.py:33
  330.3 3.1 collective-permute-start.5
  333.4 4.5 %collective-permute-done.5 = f32[8,2048]{1,0:T(8,128)S(1)} collective-permute-done((f32[8,2048]{1,0:T(8,128)S(1)}, f32[8,2048]{1,0:T(8,128)S(1)}, u32[]{:S(2)}, u32[]{:S(2)}) %collective-permute-start.5) | collective-permute-done | bytes 65568 | tf_op jit(solution)/shard_map/ppermute | solution.py:33
  338.0 1.9 collective-permute-start.6
  339.9 4.2 %collective-permute-done.6 = f32[8,2048]{1,0:T(8,128)S(1)} collective-permute-done((f32[8,2048]{1,0:T(8,128)S(1)}, f32[8,2048]{1,0:T(8,128)S(1)}, u32[]{:S(2)}, u32[]{:S(2)}) %collective-permute-start.6) | collective-permute-done | bytes 65568 | tf_op jit(solution)/shard_map/ppermute | solution.py:33
  344.2 1.9 collective-permute-start.7
  346.1 5.7 %collective-permute-done.7 = f32[8,2048]{1,0:T(8,128)S(1)} collective-permute-done((f32[8,2048]{1,0:T(8,128)S(1)}, f32[8,2048]{1,0:T(8,128)S(1)}, u32[]{:S(2)}, u32[]{:S(2)}) %collective-permute-start.7) | collective-permute-done | bytes 65568 | tf_op jit(solution)/shard_map/ppermute | solution.py:33
  351.8 0.6 add_multiply_fusion
  (25 shorter events, 0.2 us)
Async XLA Ops:
  0.0 244.0 %copy-start = (bf16[128,8]{0,1:T(8,128)(2,1)S(1)}, bf16[128,8]{0,1:T(8,128)(2,1)}, u32[]{:S(2)}) copy-start(bf16[128,8]{0,1:T(8,128)(2,1)} %param.26) | copy-start | bytes 6148
  0.0 11.4 %copy-start.5 = (s32[1,2048]{1,0:T(1,128)S(1)}, s32[1,2048]{1,0:T(1,128)}, u32[]{:S(2)}) copy-start(s32[1,2048]{1,0:T(1,128)} %param.15) | copy-start | bytes 24580
  0.0 11.6 %copy-start.3 = (bf16[2048,96]{0,1:T(8,128)(2,1)S(1)}, bf16[2048,96]{0,1:T(8,128)(2,1)}, u32[]{:S(2)}) copy-start(bf16[2048,96]{0,1:T(8,128)(2,1)} %param.14) | copy-start | bytes 1179652
  21.8 15.8 %copy-start.4 = (s32[1,27,2048]{2,0,1:T(1,128)S(1)}, s32[1,27,2048]{2,0,1:T(1,128)}, u32[]{:S(2)}) copy-start(s32[1,27,2048]{2,0,1:T(1,128)} %param.19) | copy-start | bytes 663556
  21.8 16.5 %copy-start.6 = (s32[1,1,2,2]{3,2,1,0:T(2,128)S(1)}, s32[1,1,2,2]{3,2,1,0:T(2,128)}, u32[]{:S(2)}) copy-start(s32[1,1,2,2]{3,2,1,0:T(2,128)} %param.18) | copy-start | bytes 52
  21.8 80.0 %all-to-all-start = ((bf16[32,149,128]{2,1,0:T(8,128)(2,1)}), bf16[32,149,128]{2,1,0:T(8,128)(2,1)S(1)}, u32[]{:S(2)}, u32[]{:S(2)}) async-start(bf16[32,149,128]{2,1,0:T(8,128)(2,1)} %reshape.314), calls=%async_computation | async-start | bytes 2490368 | tf_op jit(solution)/shard_map/all_to_all | solution.py:212
  107.8 3.5 %copy-start.1 = (bf16[6144,99]{1,0:T(8,128)(2,1)}, bf16[6144,99]{1,0:T(8,128)(2,1)S(1)}, u32[]{:S(2)}) copy-start(bf16[6144,99]{1,0:T(8,128)(2,1)S(1)} %reshape.316.feats_ref) | copy-start | bytes 3649540
  121.3 2.0 copy-start.2
  124.7 4.9 %collective-permute-start = (bf16[256,96]{1,0:T(8,128)(2,1)S(1)}, bf16[256,96]{1,0:T(8,128)(2,1)S(1)}, u32[]{:S(2)}, u32[]{:S(2)}) collective-permute-start(bf16[256,96]{1,0:T(8,128)(2,1)S(1)} %bitcast.105), channel_id=1, source_target_pairs={{0,1},{1,2},{2,3},{3,4},{4,5},{5,6},{6,7},{7,8},{8,9},{9,10},{10,1... | collective-permute-start | bytes 147464 | tf_op jit(solution)/shard_map/ppermute | solution.py:23
  126.6 3.1 collective-permute-start.1
  178.0 18.2 %collective-permute-start.2 = (bf16[256,128]{1,0:T(8,128)(2,1)S(1)}, bf16[256,128]{1,0:T(8,128)(2,1)S(1)}, u32[]{:S(2)}, u32[]{:S(2)}) collective-permute-start(bf16[256,128]{1,0:T(8,128)(2,1)S(1)} %bitcast.107), channel_id=1, source_target_pairs={{0,1},{1,2},{2,3},{3,4},{4,5},{5,6},{6,7},{7,8},{8,9},{9,10},{10,1... | collective-permute-start | bytes 196616 | tf_op jit(solution)/shard_map/ppermute | solution.py:23
  194.6 3.1 collective-permute-start.3
  200.3 43.8 %copy-start.7 = (f32[8]{0:T(128)S(1)}, f32[8]{0:T(128)}, u32[]{:S(2)}) copy-start(f32[8]{0:T(128)} %param.27) | copy-start | bytes 100
  269.8 44.2 %all-to-all-start.1 = ((f32[32,192,8]{1,2,0:T(8,128)}), f32[32,192,8]{1,2,0:T(8,128)S(1)}, u32[]{:S(2)}, u32[]{:S(2)}) async-start(f32[32,192,8]{1,2,0:T(8,128)} %copy.41), calls=%async_computation.1 | async-start | bytes 524288 | tf_op jit(solution)/shard_map/all_to_all | solution.py:247
  324.1 6.2 %collective-permute-start.4 = (f32[8,2048]{1,0:T(8,128)S(1)}, f32[8,2048]{1,0:T(8,128)S(1)}, u32[]{:S(2)}, u32[]{:S(2)}) collective-permute-start(f32[8,2048]{1,0:T(8,128)S(1)} %bitcast.98), channel_id=1, source_target_pairs={{0,32},{32,0},{64,96},{96,64},{128,160},{160,128},{192,224},{224,1... | collective-permute-start | bytes 196616 | tf_op jit(solution)/shard_map/ppermute | solution.py:33
  330.3 7.7 %collective-permute-start.5 = (f32[8,2048]{1,0:T(8,128)S(1)}, f32[8,2048]{1,0:T(8,128)S(1)}, u32[]{:S(2)}, u32[]{:S(2)}) collective-permute-start(f32[8,2048]{1,0:T(8,128)S(1)} %bitcast_add_fusion.1), channel_id=1, source_target_pairs={{0,64},{32,96},{64,0},{96,32},{128,192},{160,224},{192,128},{224,1... | collective-permute-start | bytes 196616 | tf_op jit(solution)/shard_map/ppermute | solution.py:33
  338.0 6.2 %collective-permute-start.6 = (f32[8,2048]{1,0:T(8,128)S(1)}, f32[8,2048]{1,0:T(8,128)S(1)}, u32[]{:S(2)}, u32[]{:S(2)}) collective-permute-start(f32[8,2048]{1,0:T(8,128)S(1)} %add.121), channel_id=1, source_target_pairs={{0,128},{32,160},{64,192},{96,224},{128,0},{160,32},{192,64},{224,... | collective-permute-start | bytes 196616 | tf_op jit(solution)/shard_map/ppermute | solution.py:33
  344.2 7.7 %collective-permute-start.7 = (f32[8,2048]{1,0:T(8,128)S(1)}, f32[8,2048]{1,0:T(8,128)S(1)}, u32[]{:S(2)}, u32[]{:S(2)}) collective-permute-start(f32[8,2048]{1,0:T(8,128)S(1)} %add.122), channel_id=1, source_target_pairs={{0,256},{32,288},{64,320},{96,352},{128,384},{160,416},{192,448},{... | collective-permute-start | bytes 196616 | tf_op jit(solution)/shard_map/ppermute | solution.py:33

commit v3 on v2

--- a/solution.py
+++ b/solution.py
@@ -27,11 +27,18 @@
     devices = lax.axis_size(axis)
     if devices & (devices - 1):
         return lax.psum(values, axis)
+
+    def partner(by):
+        return lax.ppermute(values, axis, [(i, i ^ by) for i in range(devices)])
+
     step = 1
     while step < devices:
-        pairs = [(i, i ^ step) for i in range(devices)]
-        values = values + lax.ppermute(values, axis, pairs)
-        step *= 2
+        if step * 4 <= devices:
+            values = (values + partner(step)) + (partner(2 * step) + partner(3 * step))
+            step *= 4
+        else:
+            values = values + partner(step)
+            step *= 2
     return values
 
 
@@ -166,6 +173,26 @@
     )(voxel_of_slot.reshape(1, slots), slot_feats)
 
 
+def gather_kernel(index_ref, table_ref, out_ref):
+    def pick(i, carry):
+        out_ref[pl.ds(i, 1), :] = table_ref[pl.ds(index_ref[i], 1), :]
+        return carry
+
+    lax.fori_loop(0, out_ref.shape[0], pick, 0, unroll=64)
+
+
+def gather_rows(table, index):
+    return pl.pallas_call(
+        gather_kernel,
+        in_specs=[
+            pl.BlockSpec(memory_space=pltpu.SMEM),
+            pl.BlockSpec(memory_space=pltpu.VMEM),
+        ],
+        out_specs=pl.BlockSpec(memory_space=pltpu.VMEM),
+        out_shape=jax.ShapeDtypeStruct((index.shape[0], table.shape[1]), table.dtype),
+    )(index, table)
+
+
 def per_device(
     point_feats,
     owners,
@@ -243,9 +270,9 @@
         active_rows,
     )
     voxel_logits = jnp.dot(refined, head_weight, preferred_element_type=jnp.float32) + head_bias
-    slot_logits = voxel_logits[flat_voxels].reshape(slab_count, capacity, -1)
+    slot_logits = gather_rows(voxel_logits, flat_voxels).reshape(slab_count, capacity, -1)
     returned = lax.all_to_all(slot_logits, "slab", 0, 0, tiled=True)
-    point_logits = returned.reshape(slab_count * capacity, -1)[slot_number].T
+    point_logits = gather_rows(returned.reshape(slab_count * capacity, -1), slot_number).T
     summed = all_summed(point_logits, "rot")
     return summed / lax.axis_size("rot")
 

time: 354 us -> 347 us (0.980)
  Pallas kernels: 97.3 us -> 121 us
  local copies, waits for them, and re-layouts: 56.3 us -> 36.1 us
  waiting for transfers between devices: 107 us -> 92.5 us
  other arithmetic: 22.2 us -> 25.8 us
    gather x3 -> x0, local copies, waits for them, and re-layouts: 30 us -> none  [the longest x1 20.9 us: per_device(): slot_logits = voxel_logits[flat_voxels].reshape(slab_count, capacity, -1)]
    ppermute x4 -> x6, waiting for transfers between devices: 18.7 us -> 5.07 us  [partner(): return lax.ppermute(values, axis, [(i, i ^ by) for i in range(devices)])]
    pallas_call x0 -> x2, Pallas kernels: none -> 12.8 us  [gather_rows(): pl.pallas_call(gather_kernel, in_specs=[pl.BlockSpec(memory_space=pltpu.S...]
    ppermute x4 -> x6, starting transfers between devices: 8.87 us -> 20.8 us  [partner(): return lax.ppermute(values, axis, [(i, i ^ by) for i in range(devices)])]
    pallas_call x2, Pallas kernels: 87.3 us -> 98.5 us  [convolve(): pl.pallas_call(functools.partial(conv_kernel, has_residual=residual is no...]
    all_to_all x1, starting transfers between devices: 21.4 us -> 13 us  [per_device(): returned = lax.all_to_all(slot_logits, 'slab', 0, 0, tiled=True)]
    ppermute x4, starting transfers between devices: 21.6 us -> 16 us  [passed_along(): return lax.ppermute(shard, axis, pairs)]
    add x3, other arithmetic: 0.03 us -> 5.2 us  [the longest x1 2.69 us: per_device(): got_rows[:, in_width].astype(jnp.int32) * DIGIT]
  transfers between devices with their start and end apart: 10 -> 12, of which waited for: 8 -> 6; matrix products, arithmetic and copies ran while one was open for 0% -> 1% of each run, Pallas kernels for 0% -> 0%
where the time goes in v3:
time: 347 us; the launch traced here: 345 us
  Pallas kernels  121 us (35%)
  waiting for transfers between devices  92.5 us (27%)
  starting transfers between devices  65.6 us (19%)
  local copies, waits for them, and re-layouts  36.1 us (10%)
  other arithmetic  25.8 us (7%)
    pallas_call x2, Pallas kernels, convolve(): pl.pallas_call(functools.partial(conv_kernel, has_residual=residual is no...  98.5 us
    all_to_all x1, waiting for transfers between devices, per_device(): lax.all_to_all(packed.reshape(slab_count, dense // 128, 128), 'slab', 0,...  63.5 us
    all_to_all x1, waiting for transfers between devices, per_device(): returned = lax.all_to_all(slot_logits, 'slab', 0, 0, tiled=True)  22.2 us
    ppermute x6, starting transfers between devices, partner(): return lax.ppermute(values, axis, [(i, i ^ by) for i in range(devices)])  20.8 us
    ppermute x4, starting transfers between devices, passed_along(): return lax.ppermute(shard, axis, pairs)  16 us
    all_to_all x1, starting transfers between devices, per_device(): lax.all_to_all(packed.reshape(slab_count, dense // 128, 128), 'slab', 0,...  15.8 us
    all_to_all x1, starting transfers between devices, per_device(): returned = lax.all_to_all(slot_logits, 'slab', 0, 0, tiled=True)  13 us
    pallas_call x2, Pallas kernels, gather_rows(): pl.pallas_call(gather_kernel, in_specs=[pl.BlockSpec(memory_space=pltpu.S...  12.8 us
  transfers between devices with their start and end apart: 12, of which 6 were waited for; matrix products, arithmetic and copies ran while one was open for 1% of the time, Pallas kernels for 0%

profile of v3, /device:TPU:24, one launch (start us, length us, event | category | flops | bytes accessed | tf_op | source)
XLA Modules:
  0.0 344.6 jit_solution(10055501291676706111)
XLA Ops:
  0.0 0.8 fusion.9
  0.8 0.7 fusion.7
  1.6 9.1 %reduce-window.6 = s32[32,16,128]{2,1,0:T(8,128)S(1)} reduce-window(s32[32,16,128]{2,1,0:T(8,128)S(1)} %fusion.7, s32[]{:T(128)} %constant.44.clone.1), window={size=1x1x128 pad=0_0x0_0x127_0}, to_apply=%region_0.0 | reduce-window | flops 8323072 | bytes 524292 | tf_op jit(solution)/shard_map/reduce-window
  10.6 0.1 slice.48
  10.8 0.2 copy.62
  11.0 0.2 reduce-window.9
  11.2 0.1 broadcast_add_fusion
  11.4 0.1 fusion.6
  11.6 0.1 maximum_maximum_fusion
  11.7 0.3 copy.43
  12.0 6.3 %scatter_custom_fusion = bf16[6144,99]{1,0:T(8,128)(2,1)S(1)} fusion(s32[2048]{0:T(1024)S(1)} %bitcast.110, bf16[2048,99]{1,0:T(8,128)(2,1)S(1)} %copy.43, bf16[]{:T(256)} %constant.45.clone.1), kind=kCustom, calls=%fused_computation.14 | custom fusion | bytes 1216514 | tf_op jit(solution)/shard_map/scatter | solution.py:234
  18.3 1.9 reshape.315
  20.4 1.5 reshape.316
  21.8 15.8 %all-to-all-start = ((bf16[32,149,128]{2,1,0:T(8,128)(2,1)}), bf16[32,149,128]{2,1,0:T(8,128)(2,1)S(1)}, u32[]{:S(2)}, u32[]{:S(2)}) async-start(bf16[32,149,128]{2,1,0:T(8,128)(2,1)} %reshape.316), calls=%async_computation | async-start | bytes 2490368 | tf_op jit(solution)/shard_map/all_to_all | solution.py:239
  37.7 0.5 reduce.1
  38.4 63.5 %all-to-all-done = bf16[32,149,128]{2,1,0:T(8,128)(2,1)S(1)} async-done(((bf16[32,149,128]{2,1,0:T(8,128)(2,1)}), bf16[32,149,128]{2,1,0:T(8,128)(2,1)S(1)}, u32[]{:S(2)}, u32[]{:S(2)}) %all-to-all-start) | async-done | bytes 1220640 | tf_op jit(solution)/shard_map/all_to_all | solution.py:239
  101.8 0.2 copy.69
  102.0 5.8 %reshape.318.feats_ref = bf16[6144,99]{1,0:T(8,128)(2,1)S(1)} reshape(bf16[32,19008]{1,0:T(8,128)(2,1)S(1)} %bitcast.90) | data formatting | bytes 2433024 | tf_op jit(solution)/shard_map/reshape | solution.py:242
  107.8 2.7 add_reduce_fusion.index_ref
  110.5 9.9 %shard_map.136 = f32[2048,99]{1,0:T(8,128)} custom-call(s32[1,6144]{1,0:T(1,128)} %bitcast.99, bf16[6144,99]{1,0:T(8,128)(2,1)} %copy-done.1), custom_call_target="tpu_custom_call" | custom-call | tf_op jit(solution)/shard_map/pallas_call | solution.py:164
  120.4 1.9 fusion
  122.4 0.3 fusion.1
  122.7 0.6 gather_fusion.1
  123.3 0.6 gather_fusion
  123.8 1.9 collective-permute-start
  125.8 1.5 collective-permute-start.1
  128.0 0.7 copy.66
  128.7 0.2 collective-permute-done.1
  128.9 1.5 maximum_convert_fusion.ext_ref
  130.4 49.1 %shard_map.137.rest_0_ = bf16[2048,128]{1,0:T(8,128)(2,1)} custom-call(s32[1]{0:T(128)} %bitcast.9.active_ref, s32[57344]{0:T(1024)} %bitcast.93, f32[2568,96]{1,0:T(8,128)} %maximum_convert_fusion.ext_ref, bf16[27,96,128]{2,1,0:T(8,128)(2,1)} %w_ref.2, f32[1,128]{1,0:T(1,128)} %bitcast.111, f32[1,128]{1,0:T(1,128)} %bitcast.112), custom_call_target="tpu_custom_call" | custom-call | tf_op jit(solution)/shard_map/pallas_call | solution.py:142
  179.5 1.6 gather_fusion.3
  181.1 1.6 gather_fusion.2
  182.7 11.0 %collective-permute-start.2 = (bf16[256,128]{1,0:T(8,128)(2,1)S(1)}, bf16[256,128]{1,0:T(8,128)(2,1)S(1)}, u32[]{:S(2)}, u32[]{:S(2)}) collective-permute-start(bf16[256,128]{1,0:T(8,128)(2,1)S(1)} %bitcast.109), channel_id=1, source_target_pairs={{0,1},{1,2},{2,3},{3,4},{4,5},{5,6},{6,7},{7,8},{8,9},{9,10},{10,1... | collective-permute-start | bytes 196616 | tf_op jit(solution)/shard_map/ppermute | solution.py:23
  193.7 1.6 collective-permute-start.3
  195.3 1.6 collective-permute-done.3
  196.9 2.5 maximum_convert_fusion.1.ext_ref
  199.4 49.4 %shard_map.138 = bf16[2048,128]{1,0:T(8,128)(2,1)} custom-call(s32[1]{0:T(128)} %bitcast.9.active_ref, s32[57344]{0:T(1024)} %bitcast.94, f32[2568,128]{1,0:T(8,128)} %maximum_convert_fusion.1.ext_ref, bf16[27,128,128]{2,1,0:T(8,128)(2,1)} %w_ref.3, f32[1,128]{1,0:T(1,128)} %bitcast.113, f32[1,128]{1,0:T(1,128)} %bitcast.114, ...), custom_call_target="tpu_custom_call" | custom-call | tf_op jit(solution)/shard_map/pallas_call | solution.py:142
  248.8 2.3 convolution_add_fusion.table_ref
  251.1 8.2 %shard_map.139 = f32[6144,8]{1,0:T(8,128)} custom-call(s32[6144]{0:T(1024)} %add_reduce_fusion.index_ref, f32[2048,8]{1,0:T(8,128)} %convolution_add_fusion.table_ref), custom_call_target="tpu_custom_call" | custom-call | tf_op jit(solution)/shard_map/pallas_call | solution.py:185
  259.3 3.2 copy.46
  262.5 13.0 %all-to-all-start.1 = ((f32[32,192,8]{1,2,0:T(8,128)}), f32[32,192,8]{1,2,0:T(8,128)S(1)}, u32[]{:S(2)}, u32[]{:S(2)}) async-start(f32[32,192,8]{1,2,0:T(8,128)} %copy.46), calls=%async_computation.1 | async-start | bytes 524288 | tf_op jit(solution)/shard_map/all_to_all | solution.py:274
  275.5 0.6 multiply_add_fusion.index_ref
  276.1 22.2 %all-to-all-done.1 = f32[32,192,8]{1,2,0:T(8,128)S(1)} async-done(((f32[32,192,8]{1,2,0:T(8,128)}), f32[32,192,8]{1,2,0:T(8,128)S(1)}, u32[]{:S(2)}, u32[]{:S(2)}) %all-to-all-start.1) | async-done | bytes 196640 | tf_op jit(solution)/shard_map/all_to_all | solution.py:274
  298.3 2.2 copy.47
  300.5 4.7 %shard_map.140 = f32[2048,8]{1,0:T(8,128)} custom-call(s32[2048]{0:T(1024)} %multiply_add_fusion.index_ref, f32[6144,8]{1,0:T(8,128)} %bitcast.85), custom_call_target="tpu_custom_call" | custom-call | tf_op jit(solution)/shard_map/pallas_call | solution.py:185
  305.1 1.5 copy.48
  306.7 1.9 collective-permute-start.4
  308.6 5.9 %collective-permute-start.5 = (f32[8,2048]{1,0:T(8,128)S(1)}, f32[8,2048]{1,0:T(8,128)S(1)}, u32[]{:S(2)}, u32[]{:S(2)}) collective-permute-start(f32[8,2048]{1,0:T(8,128)S(1)} %copy.48), channel_id=1, source_target_pairs={{0,64},{32,96},{64,0},{96,32},{128,192},{160,224},{192,128},{224,1... | collective-permute-start | bytes 196616 | tf_op jit(solution)/shard_map/ppermute | solution.py:32
  314.5 2.6 collective-permute-start.6
  317.1 0.3 copy.49
  317.5 1.3 copy.52
  318.8 3.1 collective-permute-done.6
  321.9 1.4 copy.53
  323.3 1.9 add_add_fusion
  325.2 0.3 copy.54
  325.5 1.9 collective-permute-start.7
  327.4 3.8 %collective-permute-start.8 = (f32[8,2048]{1,0:T(8,128)S(1)}, f32[8,2048]{1,0:T(8,128)S(1)}, u32[]{:S(2)}, u32[]{:S(2)}) collective-permute-start(f32[8,2048]{1,0:T(8,128)S(1)} %copy.54), channel_id=1, source_target_pairs={{0,256},{32,288},{64,320},{96,352},{128,384},{160,416},{192,448},{... | collective-permute-start | bytes 196616 | tf_op jit(solution)/shard_map/ppermute | solution.py:32
  331.2 4.7 %collective-permute-start.9 = (f32[8,2048]{1,0:T(8,128)S(1)}, f32[8,2048]{1,0:T(8,128)S(1)}, u32[]{:S(2)}, u32[]{:S(2)}) collective-permute-start(f32[8,2048]{1,0:T(8,128)S(1)} %copy.54), channel_id=1, source_target_pairs={{0,384},{32,416},{64,448},{96,480},{128,256},{160,288},{192,320},{... | collective-permute-start | bytes 196616 | tf_op jit(solution)/shard_map/ppermute | solution.py:32
  335.9 0.3 copy.55
  336.3 0.3 copy.58
  336.6 2.0 collective-permute-done.9
  338.6 1.3 copy.59
  339.9 2.5 add_multiply_fusion
  342.4 2.2 copy.60
  (35 shorter events, 0.4 us)
Async XLA Ops:
  0.0 248.8 %copy-start = (bf16[128,8]{0,1:T(8,128)(2,1)S(1)}, bf16[128,8]{0,1:T(8,128)(2,1)}, u32[]{:S(2)}) copy-start(bf16[128,8]{0,1:T(8,128)(2,1)} %param.26) | copy-start | bytes 6148
  0.0 11.4 %copy-start.6 = (s32[1,2048]{1,0:T(1,128)S(1)}, s32[1,2048]{1,0:T(1,128)}, u32[]{:S(2)}) copy-start(s32[1,2048]{1,0:T(1,128)} %param.15) | copy-start | bytes 24580
  0.0 11.6 %copy-start.4 = (bf16[2048,96]{0,1:T(8,128)(2,1)S(1)}, bf16[2048,96]{0,1:T(8,128)(2,1)}, u32[]{:S(2)}) copy-start(bf16[2048,96]{0,1:T(8,128)(2,1)} %param.14) | copy-start | bytes 1179652
  21.8 15.8 %copy-start.5 = (s32[1,27,2048]{2,0,1:T(1,128)S(1)}, s32[1,27,2048]{2,0,1:T(1,128)}, u32[]{:S(2)}) copy-start(s32[1,27,2048]{2,0,1:T(1,128)} %param.19) | copy-start | bytes 663556
  21.8 80.0 %all-to-all-start = ((bf16[32,149,128]{2,1,0:T(8,128)(2,1)}), bf16[32,149,128]{2,1,0:T(8,128)(2,1)S(1)}, u32[]{:S(2)}, u32[]{:S(2)}) async-start(bf16[32,149,128]{2,1,0:T(8,128)(2,1)} %reshape.316), calls=%async_computation | async-start | bytes 2490368 | tf_op jit(solution)/shard_map/all_to_all | solution.py:239
  37.7 0.7 copy-start.7
  107.8 2.7 copy-start.1
  120.4 2.0 copy-start.3
  123.8 4.9 %collective-permute-start = (bf16[256,96]{1,0:T(8,128)(2,1)S(1)}, bf16[256,96]{1,0:T(8,128)(2,1)S(1)}, u32[]{:S(2)}, u32[]{:S(2)}) collective-permute-start(bf16[256,96]{1,0:T(8,128)(2,1)S(1)} %bitcast.107), channel_id=1, source_target_pairs={{0,1},{1,2},{2,3},{3,4},{4,5},{5,6},{6,7},{7,8},{8,9},{9,10},{10,1... | collective-permute-start | bytes 147464 | tf_op jit(solution)/shard_map/ppermute | solution.py:23
  125.8 3.1 collective-permute-start.1
  182.7 12.6 %collective-permute-start.2 = (bf16[256,128]{1,0:T(8,128)(2,1)S(1)}, bf16[256,128]{1,0:T(8,128)(2,1)S(1)}, u32[]{:S(2)}, u32[]{:S(2)}) collective-permute-start(bf16[256,128]{1,0:T(8,128)(2,1)S(1)} %bitcast.109), channel_id=1, source_target_pairs={{0,1},{1,2},{2,3},{3,4},{4,5},{5,6},{6,7},{7,8},{8,9},{9,10},{10,1... | collective-permute-start | bytes 196616 | tf_op jit(solution)/shard_map/ppermute | solution.py:23
  193.7 3.1 collective-permute-start.3
  199.4 49.4 %copy-start.8 = (f32[8]{0:T(128)S(1)}, f32[8]{0:T(128)}, u32[]{:S(2)}) copy-start(f32[8]{0:T(128)} %param.27) | copy-start | bytes 100
  262.5 35.8 %all-to-all-start.1 = ((f32[32,192,8]{1,2,0:T(8,128)}), f32[32,192,8]{1,2,0:T(8,128)S(1)}, u32[]{:S(2)}, u32[]{:S(2)}) async-start(f32[32,192,8]{1,2,0:T(8,128)} %copy.46), calls=%async_computation.1 | async-start | bytes 524288 | tf_op jit(solution)/shard_map/all_to_all | solution.py:274
  306.7 10.5 %collective-permute-start.4 = (f32[8,2048]{1,0:T(8,128)S(1)}, f32[8,2048]{1,0:T(8,128)S(1)}, u32[]{:S(2)}, u32[]{:S(2)}) collective-permute-start(f32[8,2048]{1,0:T(8,128)S(1)} %copy.48), channel_id=1, source_target_pairs={{0,32},{32,0},{64,96},{96,64},{128,160},{160,128},{192,224},{224,1... | collective-permute-start | bytes 196616 | tf_op jit(solution)/shard_map/ppermute | solution.py:32
  308.6 8.9 %collective-permute-start.5 = (f32[8,2048]{1,0:T(8,128)S(1)}, f32[8,2048]{1,0:T(8,128)S(1)}, u32[]{:S(2)}, u32[]{:S(2)}) collective-permute-start(f32[8,2048]{1,0:T(8,128)S(1)} %copy.48), channel_id=1, source_target_pairs={{0,64},{32,96},{64,0},{96,32},{128,192},{160,224},{192,128},{224,1... | collective-permute-start | bytes 196616 | tf_op jit(solution)/shard_map/ppermute | solution.py:32
  314.5 7.4 %collective-permute-start.6 = (f32[8,2048]{1,0:T(8,128)S(1)}, f32[8,2048]{1,0:T(8,128)S(1)}, u32[]{:S(2)}, u32[]{:S(2)}) collective-permute-start(f32[8,2048]{1,0:T(8,128)S(1)} %copy.48), channel_id=1, source_target_pairs={{0,96},{32,64},{64,32},{96,0},{128,224},{160,192},{192,160},{224,1... | collective-permute-start | bytes 196616 | tf_op jit(solution)/shard_map/ppermute | solution.py:32
  317.4 5.8 %copy-start.2 = (f32[2048,8]{1,0:T(8,128)S(1)}, f32[2048,8]{1,0:T(8,128)}, u32[]{:S(2)}) copy-start(f32[2048,8]{1,0:T(8,128)} %shard_map.140) | copy-start | bytes 196612
  325.5 10.5 %collective-permute-start.7 = (f32[8,2048]{1,0:T(8,128)S(1)}, f32[8,2048]{1,0:T(8,128)S(1)}, u32[]{:S(2)}, u32[]{:S(2)}) collective-permute-start(f32[8,2048]{1,0:T(8,128)S(1)} %copy.54), channel_id=1, source_target_pairs={{0,128},{32,160},{64,192},{96,224},{128,0},{160,32},{192,64},{224,... | collective-permute-start | bytes 196616 | tf_op jit(solution)/shard_map/ppermute | solution.py:32
  327.4 8.9 %collective-permute-start.8 = (f32[8,2048]{1,0:T(8,128)S(1)}, f32[8,2048]{1,0:T(8,128)S(1)}, u32[]{:S(2)}, u32[]{:S(2)}) collective-permute-start(f32[8,2048]{1,0:T(8,128)S(1)} %copy.54), channel_id=1, source_target_pairs={{0,256},{32,288},{64,320},{96,352},{128,384},{160,416},{192,448},{... | collective-permute-start | bytes 196616 | tf_op jit(solution)/shard_map/ppermute | solution.py:32
  331.2 7.4 %collective-permute-start.9 = (f32[8,2048]{1,0:T(8,128)S(1)}, f32[8,2048]{1,0:T(8,128)S(1)}, u32[]{:S(2)}, u32[]{:S(2)}) collective-permute-start(f32[8,2048]{1,0:T(8,128)S(1)} %copy.54), channel_id=1, source_target_pairs={{0,384},{32,416},{64,448},{96,480},{128,256},{160,288},{192,320},{... | collective-permute-start | bytes 196616 | tf_op jit(solution)/shard_map/ppermute | solution.py:32

commit v4 on v3

--- a/solution.py
+++ b/solution.py
@@ -27,18 +27,11 @@
     devices = lax.axis_size(axis)
     if devices & (devices - 1):
         return lax.psum(values, axis)
-
-    def partner(by):
-        return lax.ppermute(values, axis, [(i, i ^ by) for i in range(devices)])
-
     step = 1
     while step < devices:
-        if step * 4 <= devices:
-            values = (values + partner(step)) + (partner(2 * step) + partner(3 * step))
-            step *= 4
-        else:
-            values = values + partner(step)
-            step *= 2
+        pairs = [(i, i ^ step) for i in range(devices)]
+        values = values + lax.ppermute(values, axis, pairs)
+        step *= 2
     return values
 
 
@@ -58,39 +51,33 @@
 
 def conv_kernel(active_ref, nbr_ref, ext_ref, w_ref, scale_ref, shift_ref, *rest, has_residual):
     if has_residual:
-        res_ref, out_ref, gathered_ref, acc_ref = rest
+        res_ref, out_ref, gathered_ref = rest
     else:
-        out_ref, gathered_ref, acc_ref = rest
+        out_ref, gathered_ref = rest
     rows = out_ref.shape[0]
+    channels = ext_ref.shape[1]
     first = pl.multiple_of(pl.program_id(0) * rows, rows)
     active = active_ref[0]
 
     @pl.when(first < active)
     def _():
         for offset in range(OFFSETS):
-            slot = offset % 2
+            lanes = pl.ds(offset * channels, channels)
             if offset == CENTRE:
-                picked = ext_ref[pl.ds(first, rows), :]
-            else:
-                base = offset * rows
-
-                def pick(i, carry):
-                    row = nbr_ref[base + i]
-                    gathered_ref[slot, pl.ds(i, 1), :] = ext_ref[pl.ds(row, 1), :]
-                    return carry
-
-                lax.fori_loop(0, rows, pick, 0, unroll=True)
-                picked = gathered_ref[slot]
-            part = jnp.dot(
-                picked.astype(jnp.bfloat16),
-                w_ref[offset],
-                preferred_element_type=jnp.float32,
-            )
-            if offset == 0:
-                acc_ref[...] = part
-            else:
-                acc_ref[...] += part
-        values = acc_ref[...] * scale_ref[...] + shift_ref[...]
+                gathered_ref[:, lanes] = ext_ref[pl.ds(first, rows), :]
+                continue
+            base = offset * rows
+
+            def pick(i, carry):
+                row = nbr_ref[base + i]
+                gathered_ref[pl.ds(i, 1), lanes] = ext_ref[pl.ds(row, 1), :]
+                return carry
+
+            lax.fori_loop(0, rows, pick, 0, unroll=True)
+        summed = jnp.dot(
+            gathered_ref[...].astype(jnp.bfloat16), w_ref[...], preferred_element_type=jnp.float32
+        )
+        values = summed * scale_ref[...] + shift_ref[...]
         if has_residual:
             values = values + res_ref[...].astype(jnp.float32)
         living = first + lax.broadcasted_iota(jnp.int32, values.shape, 0) < active
@@ -110,19 +97,22 @@
         neighbor_table.reshape(OFFSETS, steps, CONV_ROWS).transpose(1, 0, 2).reshape(steps, -1),
         ((0, 0), (0, step_block - per_step)),
     ).reshape(-1)
-    ext_rows, channels = extended.shape
+    ext_rows, width_in = extended.shape
+    channels = -width_in // 128 * -128
     width = weight.shape[2]
+    extended = jnp.pad(extended, ((0, 0), (0, channels - width_in)))
+    weight_flat = jnp.pad(weight, ((0, 0), (0, channels - width_in), (0, 0))).reshape(-1, width)
     in_specs = [
         pl.BlockSpec((step_block,), lambda s, a: (s,), memory_space=pltpu.SMEM),
         pl.BlockSpec((ext_rows, channels), lambda s, a: (0, 0)),
-        pl.BlockSpec(weight.shape, lambda s, a: (0, 0, 0)),
+        pl.BlockSpec(weight_flat.shape, lambda s, a: (0, 0)),
         pl.BlockSpec((1, width), lambda s, a: (0, 0)),
         pl.BlockSpec((1, width), lambda s, a: (0, 0)),
     ]
     operands = [
         neighbor_steps,
         extended,
-        weight,
+        weight_flat,
         scale_vec.reshape(1, width),
         shift_vec.reshape(1, width),
     ]
@@ -134,10 +124,7 @@
         grid=(steps,),
         in_specs=in_specs,
         out_specs=pl.BlockSpec((CONV_ROWS, width), lambda s, a: (s, 0)),
-        scratch_shapes=[
-            pltpu.VMEM((2, CONV_ROWS, channels), jnp.float32),
-            pltpu.VMEM((CONV_ROWS, width), jnp.float32),
-        ],
+        scratch_shapes=[pltpu.VMEM((CONV_ROWS, OFFSETS * channels), jnp.float32)],
     )
     return pl.pallas_call(
         functools.partial(conv_kernel, has_residual=residual is not None),

time: 347 us -> 342 us (0.986)
  Pallas kernels: 121 us -> 85.4 us
  starting transfers between devices: 65.6 us -> 97.1 us
  waiting for transfers between devices: 92.5 us -> 99.5 us
  other arithmetic: 25.8 us -> 21.9 us
    all_to_all x1, starting transfers between devices: 13 us -> 54.6 us  [per_device(): returned = lax.all_to_all(slot_logits, 'slab', 0, 0, tiled=True)]
    pallas_call x2, Pallas kernels: 98.5 us -> 62.6 us  [convolve(): pl.pallas_call(functools.partial(conv_kernel, has_residual=residual is no...]
    ppermute x4, starting transfers between devices: 16 us -> 8.47 us  [passed_along(): return lax.ppermute(shard, axis, pairs)]
    ppermute x6 -> x4, waiting for transfers between devices: 5.07 us -> 12.3 us  [all_summed(): values = values + lax.ppermute(values, axis, pairs)]
    ppermute x6 -> x4, local copies, waits for them, and re-layouts: 4.99 us -> 1.31 us  [all_summed(): values = values + lax.ppermute(values, axis, pairs)]
    ppermute x6 -> x4, starting transfers between devices: 20.8 us -> 18.3 us  [all_summed(): values = values + lax.ppermute(values, axis, pairs)]
  transfers between devices with their start and end apart: 12 -> 10, of which waited for: 6 -> 7; matrix products, arithmetic and copies ran while one was open for 1% -> 1% of each run, Pallas kernels for 0% -> 0%
where the time goes in v4:
time: 342 us; the launch traced here: 340 us
  waiting for transfers between devices  99.5 us (29%)
  starting transfers between devices  97.1 us (28%)
  Pallas kernels  85.4 us (25%)
  local copies, waits for them, and re-layouts  32.9 us (10%)
  other arithmetic  21.9 us (6%)
    all_to_all x1, waiting for transfers between devices, per_device(): lax.all_to_all(packed.reshape(slab_count, dense // 128, 128), 'slab', 0,...  63.5 us
    pallas_call x2, Pallas kernels, convolve(): pl.pallas_call(functools.partial(conv_kernel, has_residual=residual is no...  62.6 us
    all_to_all x1, starting transfers between devices, per_device(): returned = lax.all_to_all(slot_logits, 'slab', 0, 0, tiled=True)  54.6 us
    all_to_all x1, waiting for transfers between devices, per_device(): returned = lax.all_to_all(slot_logits, 'slab', 0, 0, tiled=True)  22.2 us
    ppermute x4, starting transfers between devices, all_summed(): values = values + lax.ppermute(values, axis, pairs)  18.3 us
    all_to_all x1, starting transfers between devices, per_device(): lax.all_to_all(packed.reshape(slab_count, dense // 128, 128), 'slab', 0,...  15.8 us
    pallas_call x2, Pallas kernels, gather_rows(): pl.pallas_call(gather_kernel, in_specs=[pl.BlockSpec(memory_space=pltpu.S...  12.8 us
    ppermute x4, waiting for transfers between devices, all_summed(): values = values + lax.ppermute(values, axis, pairs)  12.3 us
  transfers between devices with their start and end apart: 10, of which 7 were waited for; matrix products, arithmetic and copies ran while one was open for 1% of the time, Pallas kernels for 0%

profile of v4, /device:TPU:24, one launch (start us, length us, event | category | flops | bytes accessed | tf_op | source)
XLA Modules:
  0.0 340.1 jit_solution(18272802282327561563)
XLA Ops:
  0.0 0.8 fusion.9
  0.8 0.7 fusion.7
  1.6 9.1 %reduce-window.6 = s32[32,16,128]{2,1,0:T(8,128)S(1)} reduce-window(s32[32,16,128]{2,1,0:T(8,128)S(1)} %fusion.7, s32[]{:T(128)} %constant.46.clone.1), window={size=1x1x128 pad=0_0x0_0x127_0}, to_apply=%region_0.0 | reduce-window | flops 8323072 | bytes 524292 | tf_op jit(solution)/shard_map/reduce-window
  10.6 0.1 slice.48
  10.8 0.2 copy.54
  11.0 0.2 reduce-window.9
  11.2 0.1 broadcast_add_fusion
  11.6 0.1 maximum_maximum_fusion.1
  11.7 0.3 copy.39
  12.0 6.3 %scatter_custom_fusion = bf16[6144,99]{1,0:T(8,128)(2,1)S(1)} fusion(s32[2048]{0:T(1024)S(1)} %bitcast.114, bf16[2048,99]{1,0:T(8,128)(2,1)S(1)} %copy.39, bf16[]{:T(256)} %constant.47.clone.1), kind=kCustom, calls=%fused_computation.13 | custom fusion | bytes 1216514 | tf_op jit(solution)/shard_map/scatter | solution.py:221
  18.3 1.9 reshape.321
  20.4 1.5 reshape.322
  21.8 15.8 %all-to-all-start = ((bf16[32,149,128]{2,1,0:T(8,128)(2,1)}), bf16[32,149,128]{2,1,0:T(8,128)(2,1)S(1)}, u32[]{:S(2)}, u32[]{:S(2)}) async-start(bf16[32,149,128]{2,1,0:T(8,128)(2,1)} %reshape.322), calls=%async_computation | async-start | bytes 2490368 | tf_op jit(solution)/shard_map/all_to_all | solution.py:226
  37.7 0.5 reduce.1
  38.4 63.5 %all-to-all-done = bf16[32,149,128]{2,1,0:T(8,128)(2,1)S(1)} async-done(((bf16[32,149,128]{2,1,0:T(8,128)(2,1)}), bf16[32,149,128]{2,1,0:T(8,128)(2,1)S(1)}, u32[]{:S(2)}, u32[]{:S(2)}) %all-to-all-start) | async-done | bytes 1220640 | tf_op jit(solution)/shard_map/all_to_all | solution.py:226
  101.8 0.2 copy.61
  102.0 5.8 %reshape.324.feats_ref = bf16[6144,99]{1,0:T(8,128)(2,1)S(1)} reshape(bf16[32,19008]{1,0:T(8,128)(2,1)S(1)} %bitcast.92) | data formatting | bytes 2433024 | tf_op jit(solution)/shard_map/reshape | solution.py:229
  107.8 2.7 add_reduce_fusion.index_ref
  110.5 9.9 %shard_map.136 = f32[2048,99]{1,0:T(8,128)} custom-call(s32[1,6144]{1,0:T(1,128)} %bitcast.103, bf16[6144,99]{1,0:T(8,128)(2,1)} %copy-done.1), custom_call_target="tpu_custom_call" | custom-call | tf_op jit(solution)/shard_map/pallas_call | solution.py:151
  120.4 1.9 fusion
  122.4 0.3 fusion.1
  122.7 0.6 gather_fusion.1
  123.3 0.6 gather_fusion
  123.9 1.9 collective-permute-start
  125.8 1.5 collective-permute-start.1
  128.0 0.7 copy.58
  128.7 1.0 pad.23
  129.8 0.4 maximum_maximum_fusion
  130.2 1.2 pad_convert_fusion.ext_ref
  131.4 31.3 %shard_map.137.rest_0_ = bf16[2048,128]{1,0:T(8,128)(2,1)} custom-call(s32[1]{0:T(128)} %bitcast.9.active_ref, s32[57344]{0:T(1024)} %bitcast.96, f32[2568,128]{1,0:T(8,128)} %pad_convert_fusion.ext_ref, bf16[3456,128]{1,0:T(8,128)(2,1)} %bitcast.93, f32[1,128]{1,0:T(1,128)} %bitcast.115, f32[1,128]{1,0:T(1,128)} %bitcast.116), custom_call_target="tpu_custom_call" | custom-call | tf_op jit(solution)/shard_map/pallas_call | solution.py:129
  162.7 1.6 gather_fusion.3
  164.3 1.6 gather_fusion.2
  165.9 3.5 %collective-permute-start.2 = (bf16[256,128]{1,0:T(8,128)(2,1)S(1)}, bf16[256,128]{1,0:T(8,128)(2,1)S(1)}, u32[]{:S(2)}, u32[]{:S(2)}) collective-permute-start(bf16[256,128]{1,0:T(8,128)(2,1)S(1)} %bitcast.113), channel_id=1, source_target_pairs={{0,1},{1,2},{2,3},{3,4},{4,5},{5,6},{6,7},{7,8},{8,9},{9,10},{10,1... | collective-permute-start | bytes 196616 | tf_op jit(solution)/shard_map/ppermute | solution.py:23
  169.4 1.6 collective-permute-start.3
  170.9 1.6 collective-permute-done.3
  172.5 2.5 maximum_convert_fusion.ext_ref
  175.1 31.4 %shard_map.138 = bf16[2048,128]{1,0:T(8,128)(2,1)} custom-call(s32[1]{0:T(128)} %bitcast.9.active_ref, s32[57344]{0:T(1024)} %bitcast.97, f32[2568,128]{1,0:T(8,128)} %maximum_convert_fusion.ext_ref, bf16[3456,128]{1,0:T(8,128)(2,1)} %bitcast.101, f32[1,128]{1,0:T(1,128)} %bitcast.117, f32[1,128]{1,0:T(1,128)} %bitcast.118, bf16[2048,128]{1,0:T(8,128)(2,1)} %shard_map.137.rest_0_), custom_call_target="tpu_custom_call" | custom-call | tf_op jit(solution)/shard_map/pallas_call | solution.py:129
  206.4 2.3 convolution_add_fusion.table_ref
  208.7 8.2 %shard_map.139 = f32[6144,8]{1,0:T(8,128)} custom-call(s32[6144]{0:T(1024)} %add_reduce_fusion.index_ref, f32[2048,8]{1,0:T(8,128)} %convolution_add_fusion.table_ref), custom_call_target="tpu_custom_call" | custom-call | tf_op jit(solution)/shard_map/pallas_call | solution.py:172
  216.9 3.2 copy.42
  220.1 54.6 %all-to-all-start.1 = ((f32[32,192,8]{1,2,0:T(8,128)}), f32[32,192,8]{1,2,0:T(8,128)S(1)}, u32[]{:S(2)}, u32[]{:S(2)}) async-start(f32[32,192,8]{1,2,0:T(8,128)} %copy.42), calls=%async_computation.1 | async-start | bytes 524288 | tf_op jit(solution)/shard_map/all_to_all | solution.py:261
  274.7 0.6 multiply_add_fusion.index_ref
  275.3 22.2 %all-to-all-done.1 = f32[32,192,8]{1,2,0:T(8,128)S(1)} async-done(((f32[32,192,8]{1,2,0:T(8,128)}), f32[32,192,8]{1,2,0:T(8,128)S(1)}, u32[]{:S(2)}, u32[]{:S(2)}) %all-to-all-start.1) | async-done | bytes 196640 | tf_op jit(solution)/shard_map/all_to_all | solution.py:261
  297.5 2.2 copy.43
  299.6 4.6 %shard_map.140 = f32[2048,8]{1,0:T(8,128)} custom-call(s32[2048]{0:T(1024)} %multiply_add_fusion.index_ref, f32[6144,8]{1,0:T(8,128)} %bitcast.87), custom_call_target="tpu_custom_call" | custom-call | tf_op jit(solution)/shard_map/pallas_call | solution.py:172
  304.3 1.6 copy.44
  305.9 2.5 collective-permute-start.4
  308.4 3.6 %collective-permute-done.4 = f32[8,2048]{1,0:T(8,128)S(1)} collective-permute-done((f32[8,2048]{1,0:T(8,128)S(1)}, f32[8,2048]{1,0:T(8,128)S(1)}, u32[]{:S(2)}, u32[]{:S(2)}) %collective-permute-start.4) | collective-permute-done | bytes 65568 | tf_op jit(solution)/shard_map/ppermute | solution.py:33
  312.0 0.3 copy.45
  312.5 0.3 copy.46
  312.8 3.4 %collective-permute-start.5 = (f32[8,2048]{1,0:T(8,128)S(1)}, f32[8,2048]{1,0:T(8,128)S(1)}, u32[]{:S(2)}, u32[]{:S(2)}) collective-permute-start(f32[8,2048]{1,0:T(8,128)S(1)} %copy.46), channel_id=1, source_target_pairs={{0,64},{32,96},{64,0},{96,32},{128,192},{160,224},{192,128},{224,1... | collective-permute-start | bytes 196616 | tf_op jit(solution)/shard_map/ppermute | solution.py:33
  316.2 4.2 %collective-permute-done.5 = f32[8,2048]{1,0:T(8,128)S(1)} collective-permute-done((f32[8,2048]{1,0:T(8,128)S(1)}, f32[8,2048]{1,0:T(8,128)S(1)}, u32[]{:S(2)}, u32[]{:S(2)}) %collective-permute-start.5) | collective-permute-done | bytes 65568 | tf_op jit(solution)/shard_map/ppermute | solution.py:33
  320.5 0.3 copy.47
  320.9 0.3 copy.48
  321.2 6.8 %collective-permute-start.6 = (f32[8,2048]{1,0:T(8,128)S(1)}, f32[8,2048]{1,0:T(8,128)S(1)}, u32[]{:S(2)}, u32[]{:S(2)}) collective-permute-start(f32[8,2048]{1,0:T(8,128)S(1)} %copy.48), channel_id=1, source_target_pairs={{0,128},{32,160},{64,192},{96,224},{128,0},{160,32},{192,64},{224,... | collective-permute-start | bytes 196616 | tf_op jit(solution)/shard_map/ppermute | solution.py:33
  328.0 2.2 collective-permute-done.6
  330.3 0.3 copy.49
  330.6 0.1 add.110
  330.7 0.3 copy.50
  331.0 5.5 %collective-permute-start.7 = (f32[8,2048]{1,0:T(8,128)S(1)}, f32[8,2048]{1,0:T(8,128)S(1)}, u32[]{:S(2)}, u32[]{:S(2)}) collective-permute-start(f32[8,2048]{1,0:T(8,128)S(1)} %copy.50), channel_id=1, source_target_pairs={{0,256},{32,288},{64,320},{96,352},{128,384},{160,416},{192,448},{... | collective-permute-start | bytes 196616 | tf_op jit(solution)/shard_map/ppermute | solution.py:33
  336.5 2.2 collective-permute-done.7
  338.8 0.3 copy.51
  339.1 0.1 add_multiply_fusion
  339.2 0.9 copy.52
  (37 shorter events, 0.7 us)
Async XLA Ops:
  0.0 206.4 %copy-start = (bf16[128,8]{0,1:T(8,128)(2,1)S(1)}, bf16[128,8]{0,1:T(8,128)(2,1)}, u32[]{:S(2)}) copy-start(bf16[128,8]{0,1:T(8,128)(2,1)} %param.26) | copy-start | bytes 6148
  0.0 11.4 %copy-start.7 = (s32[1,2048]{1,0:T(1,128)S(1)}, s32[1,2048]{1,0:T(1,128)}, u32[]{:S(2)}) copy-start(s32[1,2048]{1,0:T(1,128)} %param.15) | copy-start | bytes 24580
  0.0 11.6 %copy-start.5 = (bf16[2048,96]{0,1:T(8,128)(2,1)S(1)}, bf16[2048,96]{0,1:T(8,128)(2,1)}, u32[]{:S(2)}) copy-start(bf16[2048,96]{0,1:T(8,128)(2,1)} %param.14) | copy-start | bytes 1179652
  21.8 15.8 %copy-start.6 = (s32[1,27,2048]{2,0,1:T(1,128)S(1)}, s32[1,27,2048]{2,0,1:T(1,128)}, u32[]{:S(2)}) copy-start(s32[1,27,2048]{2,0,1:T(1,128)} %param.19) | copy-start | bytes 663556
  21.8 80.0 %all-to-all-start = ((bf16[32,149,128]{2,1,0:T(8,128)(2,1)}), bf16[32,149,128]{2,1,0:T(8,128)(2,1)S(1)}, u32[]{:S(2)}, u32[]{:S(2)}) async-start(bf16[32,149,128]{2,1,0:T(8,128)(2,1)} %reshape.322), calls=%async_computation | async-start | bytes 2490368 | tf_op jit(solution)/shard_map/all_to_all | solution.py:226
  37.7 0.7 copy-start.8
  107.8 2.7 copy-start.1
  120.4 2.0 copy-start.3
  122.4 6.4 %copy-start.4 = (bf16[27,96,128]{2,1,0:T(8,128)(2,1)S(1)}, bf16[27,96,128]{2,1,0:T(8,128)(2,1)}, u32[]{:S(2)}) copy-start(bf16[27,96,128]{2,1,0:T(8,128)(2,1)} %param.20) | copy-start | bytes 1990660
  123.9 5.9 %collective-permute-start = (bf16[256,96]{1,0:T(8,128)(2,1)S(1)}, bf16[256,96]{1,0:T(8,128)(2,1)S(1)}, u32[]{:S(2)}, u32[]{:S(2)}) collective-permute-start(bf16[256,96]{1,0:T(8,128)(2,1)S(1)} %bitcast.111), channel_id=1, source_target_pairs={{0,1},{1,2},{2,3},{3,4},{4,5},{5,6},{6,7},{7,8},{8,9},{9,10},{10,1... | collective-permute-start | bytes 147464 | tf_op jit(solution)/shard_map/ppermute | solution.py:23
  125.8 4.0 %collective-permute-start.1 = (bf16[256,96]{1,0:T(8,128)(2,1)S(1)}, bf16[256,96]{1,0:T(8,128)(2,1)S(1)}, u32[]{:S(2)}, u32[]{:S(2)}) collective-permute-start(bf16[256,96]{1,0:T(8,128)(2,1)S(1)} %bitcast.110), channel_id=1, source_target_pairs={{1,0},{2,1},{3,2},{4,3},{5,4},{6,5},{7,6},{8,7},{9,8},{10,9},{11,1... | collective-permute-start | bytes 147464 | tf_op jit(solution)/shard_map/ppermute | solution.py:23
  165.9 5.1 %collective-permute-start.2 = (bf16[256,128]{1,0:T(8,128)(2,1)S(1)}, bf16[256,128]{1,0:T(8,128)(2,1)S(1)}, u32[]{:S(2)}, u32[]{:S(2)}) collective-permute-start(bf16[256,128]{1,0:T(8,128)(2,1)S(1)} %bitcast.113), channel_id=1, source_target_pairs={{0,1},{1,2},{2,3},{3,4},{4,5},{5,6},{6,7},{7,8},{8,9},{9,10},{10,1... | collective-permute-start | bytes 196616 | tf_op jit(solution)/shard_map/ppermute | solution.py:23
  169.4 3.1 collective-permute-start.3
  175.0 31.4 %copy-start.9 = (f32[8]{0:T(128)S(1)}, f32[8]{0:T(128)}, u32[]{:S(2)}) copy-start(f32[8]{0:T(128)} %param.27) | copy-start | bytes 100
  220.1 77.3 %all-to-all-start.1 = ((f32[32,192,8]{1,2,0:T(8,128)}), f32[32,192,8]{1,2,0:T(8,128)S(1)}, u32[]{:S(2)}, u32[]{:S(2)}) async-start(f32[32,192,8]{1,2,0:T(8,128)} %copy.42), calls=%async_computation.1 | async-start | bytes 524288 | tf_op jit(solution)/shard_map/all_to_all | solution.py:261
  304.3 8.1 %copy-start.2 = (f32[2048,8]{1,0:T(8,128)S(1)}, f32[2048,8]{1,0:T(8,128)}, u32[]{:S(2)}) copy-start(f32[2048,8]{1,0:T(8,128)} %shard_map.140) | copy-start | bytes 196612
  305.9 6.2 %collective-permute-start.4 = (f32[8,2048]{1,0:T(8,128)S(1)}, f32[8,2048]{1,0:T(8,128)S(1)}, u32[]{:S(2)}, u32[]{:S(2)}) collective-permute-start(f32[8,2048]{1,0:T(8,128)S(1)} %copy.44), channel_id=1, source_target_pairs={{0,32},{32,0},{64,96},{96,64},{128,160},{160,128},{192,224},{224,1... | collective-permute-start | bytes 196616 | tf_op jit(solution)/shard_map/ppermute | solution.py:33
  312.8 7.7 %collective-permute-start.5 = (f32[8,2048]{1,0:T(8,128)S(1)}, f32[8,2048]{1,0:T(8,128)S(1)}, u32[]{:S(2)}, u32[]{:S(2)}) collective-permute-start(f32[8,2048]{1,0:T(8,128)S(1)} %copy.46), channel_id=1, source_target_pairs={{0,64},{32,96},{64,0},{96,32},{128,192},{160,224},{192,128},{224,1... | collective-permute-start | bytes 196616 | tf_op jit(solution)/shard_map/ppermute | solution.py:33
  321.2 9.0 %collective-permute-start.6 = (f32[8,2048]{1,0:T(8,128)S(1)}, f32[8,2048]{1,0:T(8,128)S(1)}, u32[]{:S(2)}, u32[]{:S(2)}) collective-permute-start(f32[8,2048]{1,0:T(8,128)S(1)} %copy.48), channel_id=1, source_target_pairs={{0,128},{32,160},{64,192},{96,224},{128,0},{160,32},{192,64},{224,... | collective-permute-start | bytes 196616 | tf_op jit(solution)/shard_map/ppermute | solution.py:33
  331.0 7.7 %collective-permute-start.7 = (f32[8,2048]{1,0:T(8,128)S(1)}, f32[8,2048]{1,0:T(8,128)S(1)}, u32[]{:S(2)}, u32[]{:S(2)}) collective-permute-start(f32[8,2048]{1,0:T(8,128)S(1)} %copy.50), channel_id=1, source_target_pairs={{0,256},{32,288},{64,320},{96,352},{128,384},{160,416},{192,448},{... | collective-permute-start | bytes 196616 | tf_op jit(solution)/shard_map/ppermute | solution.py:33

commit v5 on v4

--- a/solution.py
+++ b/solution.py
@@ -15,6 +15,7 @@
 POOL_ROWS = 256
 POOL_COLS = 512
 DIGIT = 64
+RANK_BLOCK = 128
 
 
 def passed_along(shard, axis, by):
@@ -202,9 +203,16 @@
     voxel_total = neighbors.shape[2]
     owner_row = owners[0]
     voxel_row = voxel_ids[0]
-    owner_hot = (owner_row[:, None] == jnp.arange(slab_count)[None, :]).astype(jnp.int32)
-    earlier = jnp.cumsum(owner_hot, axis=0) - owner_hot
-    ranking = jnp.sum(earlier * owner_hot, axis=1)
+    owner_hot = (owner_row[:, None] == jnp.arange(slab_count)[None, :]).astype(jnp.bfloat16)
+    blocks = owner_hot.reshape(-1, RANK_BLOCK, slab_count)
+    before = (
+        jnp.arange(RANK_BLOCK)[:, None] > jnp.arange(RANK_BLOCK)[None, :]
+    ).astype(jnp.bfloat16)
+    within = jnp.einsum("ij,bjk->bik", before, blocks, preferred_element_type=jnp.float32)
+    block_totals = jnp.sum(blocks.astype(jnp.float32), axis=1)
+    block_starts = jnp.cumsum(block_totals, axis=0) - block_totals
+    earlier = (within + block_starts[:, None, :]).reshape(point_count, slab_count)
+    ranking = jnp.sum(earlier * owner_hot.astype(jnp.float32), axis=1).astype(jnp.int32)
     slot_number = owner_row * capacity + ranking
     digits = (voxel_row // DIGIT, voxel_row % DIGIT)
     carried = jnp.concatenate(

time: 342 us -> 336 us (0.982)
  starting transfers between devices: 97.1 us -> 110 us
  Pallas kernels: 85.4 us -> 73.2 us
  other arithmetic: 21.9 us -> 14.2 us
    ppermute x4, starting transfers between devices: 8.47 us -> 26.7 us  [passed_along(): return lax.ppermute(shard, axis, pairs)]
    pallas_call x2, Pallas kernels: 62.6 us -> 50.4 us  [convolve(): pl.pallas_call(functools.partial(conv_kernel, has_residual=residual is no...]
    another operation x3 -> x1, other arithmetic: 9.41 us -> 0.03 us  [per_device(): block_starts = jnp.cumsum(block_totals, axis=0) - block_totals]
    all_to_all x1, starting transfers between devices: 54.6 us -> 49.7 us  [per_device(): returned = lax.all_to_all(slot_logits, 'slab', 0, 0, tiled=True)]
where the time goes in v5:
time: 336 us; the launch traced here: 333 us
  starting transfers between devices  110 us (33%)
  waiting for transfers between devices  99.1 us (29%)
  Pallas kernels  73.2 us (22%)
  local copies, waits for them, and re-layouts  32.6 us (10%)
  other arithmetic  14.2 us (4%)
    all_to_all x1, waiting for transfers between devices, per_device(): lax.all_to_all(packed.reshape(slab_count, dense // 128, 128), 'slab', 0,...  63.6 us
    pallas_call x2, Pallas kernels, convolve(): pl.pallas_call(functools.partial(conv_kernel, has_residual=residual is no...  50.4 us
    all_to_all x1, starting transfers between devices, per_device(): returned = lax.all_to_all(slot_logits, 'slab', 0, 0, tiled=True)  49.7 us
    ppermute x4, starting transfers between devices, passed_along(): return lax.ppermute(shard, axis, pairs)  26.7 us
    all_to_all x1, waiting for transfers between devices, per_device(): returned = lax.all_to_all(slot_logits, 'slab', 0, 0, tiled=True)  22.1 us
    ppermute x4, starting transfers between devices, all_summed(): values = values + lax.ppermute(values, axis, pairs)  17.6 us
    all_to_all x1, starting transfers between devices, per_device(): lax.all_to_all(packed.reshape(slab_count, dense // 128, 128), 'slab', 0,...  15.6 us
    pallas_call x2, Pallas kernels, gather_rows(): pl.pallas_call(gather_kernel, in_specs=[pl.BlockSpec(memory_space=pltpu.S...  12.8 us
  transfers between devices with their start and end apart: 10, of which 7 were waited for; matrix products, arithmetic and copies ran while one was open for 1% of the time, Pallas kernels for 0%

profile of v5, /device:TPU:24, one launch (start us, length us, event | category | flops | bytes accessed | tf_op | source)
XLA Modules:
  0.0 332.9 jit_solution(4907054845299792283)
XLA Ops:
  0.0 0.9 convert_reduce_fusion
  0.9 1.0 fusion.2
  1.9 0.7 compare_select_fusion
  2.6 0.7 fusion.12
  3.5 1.1 maximum_maximum_fusion.1
  4.6 0.3 copy.33
  4.9 6.3 %scatter_custom_fusion = bf16[6144,99]{1,0:T(8,128)(2,1)S(1)} fusion(s32[2048]{0:T(1024)S(1)} %bitcast.102, bf16[2048,99]{1,0:T(8,128)(2,1)S(1)} %copy.33, bf16[]{:T(256)} %constant.47.clone.1), kind=kCustom, calls=%fused_computation.17 | custom fusion | bytes 1216514 | tf_op jit(solution)/shard_map/scatter | solution.py:229
  11.2 1.9 reshape.351
  13.2 1.5 reshape.352
  14.7 15.6 %all-to-all-start = ((bf16[32,149,128]{2,1,0:T(8,128)(2,1)}), bf16[32,149,128]{2,1,0:T(8,128)(2,1)S(1)}, u32[]{:S(2)}, u32[]{:S(2)}) async-start(bf16[32,149,128]{2,1,0:T(8,128)(2,1)} %reshape.352), calls=%async_computation | async-start | bytes 2490368 | tf_op jit(solution)/shard_map/all_to_all | solution.py:234
  30.4 0.5 reduce.2
  30.9 0.1 copy.49
  31.1 63.6 %all-to-all-done = bf16[32,149,128]{2,1,0:T(8,128)(2,1)S(1)} async-done(((bf16[32,149,128]{2,1,0:T(8,128)(2,1)}), bf16[32,149,128]{2,1,0:T(8,128)(2,1)S(1)}, u32[]{:S(2)}, u32[]{:S(2)}) %all-to-all-start) | async-done | bytes 1220640 | tf_op jit(solution)/shard_map/all_to_all | solution.py:234
  94.7 0.2 copy.52
  94.9 5.8 %reshape.354.feats_ref = bf16[6144,99]{1,0:T(8,128)(2,1)S(1)} reshape(bf16[32,19008]{1,0:T(8,128)(2,1)S(1)} %bitcast.83) | data formatting | bytes 2433024 | tf_op jit(solution)/shard_map/reshape | solution.py:237
  100.7 2.7 add_reduce_fusion.index_ref
  103.4 9.9 %shard_map.136 = f32[2048,99]{1,0:T(8,128)} custom-call(s32[1,6144]{1,0:T(1,128)} %bitcast.93, bf16[6144,99]{1,0:T(8,128)(2,1)} %copy-done.1), custom_call_target="tpu_custom_call" | custom-call | tf_op jit(solution)/shard_map/pallas_call | solution.py:152
  113.3 1.9 fusion.3
  115.3 0.3 fusion.4
  115.6 0.6 gather_fusion.1
  116.2 0.6 gather_fusion
  116.8 1.9 collective-permute-start
  118.7 1.5 collective-permute-start.1
  120.8 0.7 copy.50
  121.6 1.1 pad.23
  122.6 0.4 maximum_maximum_fusion
  123.1 1.2 pad_convert_fusion.ext_ref
  124.2 25.2 %shard_map.137.rest_0_ = bf16[2048,128]{1,0:T(8,128)(2,1)} custom-call(s32[1]{0:T(128)} %bitcast.9.active_ref, s32[57344]{0:T(1024)} %bitcast.87, f32[2568,128]{1,0:T(8,128)} %pad_convert_fusion.ext_ref, bf16[3456,128]{1,0:T(8,128)(2,1)} %bitcast.84, f32[1,128]{1,0:T(1,128)} %bitcast.103, f32[1,128]{1,0:T(1,128)} %bitcast.104), custom_call_target="tpu_custom_call" | custom-call | tf_op jit(solution)/shard_map/pallas_call | solution.py:130
  149.4 1.6 gather_fusion.3
  151.0 1.6 gather_fusion.2
  152.6 21.8 %collective-permute-start.2 = (bf16[256,128]{1,0:T(8,128)(2,1)S(1)}, bf16[256,128]{1,0:T(8,128)(2,1)S(1)}, u32[]{:S(2)}, u32[]{:S(2)}) collective-permute-start(bf16[256,128]{1,0:T(8,128)(2,1)S(1)} %bitcast.99), channel_id=1, source_target_pairs={{0,1},{1,2},{2,3},{3,4},{4,5},{5,6},{6,7},{7,8},{8,9},{9,10},{10,1... | collective-permute-start | bytes 196616 | tf_op jit(solution)/shard_map/ppermute | solution.py:24
  174.4 1.5 collective-permute-start.3
  176.0 1.9 collective-permute-done.3
  177.8 2.5 maximum_convert_fusion.ext_ref
  180.4 25.3 %shard_map.138 = bf16[2048,128]{1,0:T(8,128)(2,1)} custom-call(s32[1]{0:T(128)} %bitcast.9.active_ref, s32[57344]{0:T(1024)} %bitcast.88, f32[2568,128]{1,0:T(8,128)} %maximum_convert_fusion.ext_ref, bf16[3456,128]{1,0:T(8,128)(2,1)} %bitcast.91, f32[1,128]{1,0:T(1,128)} %bitcast.105, f32[1,128]{1,0:T(1,128)} %bitcast.106, bf16[2048,128]{1,0:T(8,128)(2,1)} %shard_map.137.rest_0_), custom_call_target="tpu_custom_call" | custom-call | tf_op jit(solution)/shard_map/pallas_call | solution.py:130
  205.6 2.3 convolution_add_fusion.table_ref
  207.9 8.2 %shard_map.139 = f32[6144,8]{1,0:T(8,128)} custom-call(s32[6144]{0:T(1024)} %add_reduce_fusion.index_ref, f32[2048,8]{1,0:T(8,128)} %convolution_add_fusion.table_ref), custom_call_target="tpu_custom_call" | custom-call | tf_op jit(solution)/shard_map/pallas_call | solution.py:173
  216.1 3.2 copy.36
  219.3 49.7 %all-to-all-start.1 = ((f32[32,192,8]{1,2,0:T(8,128)}), f32[32,192,8]{1,2,0:T(8,128)S(1)}, u32[]{:S(2)}, u32[]{:S(2)}) async-start(f32[32,192,8]{1,2,0:T(8,128)} %copy.36), calls=%async_computation.1 | async-start | bytes 524288 | tf_op jit(solution)/shard_map/all_to_all | solution.py:269
  269.1 0.6 bitcast_add_fusion.1.index_ref
  269.7 22.1 %all-to-all-done.1 = f32[32,192,8]{1,2,0:T(8,128)S(1)} async-done(((f32[32,192,8]{1,2,0:T(8,128)}), f32[32,192,8]{1,2,0:T(8,128)S(1)}, u32[]{:S(2)}, u32[]{:S(2)}) %all-to-all-start.1) | async-done | bytes 196640 | tf_op jit(solution)/shard_map/all_to_all | solution.py:269
  291.8 2.2 copy.37
  294.0 4.6 %shard_map.140 = f32[2048,8]{1,0:T(8,128)} custom-call(s32[2048]{0:T(1024)} %bitcast_add_fusion.1.index_ref, f32[6144,8]{1,0:T(8,128)} %bitcast.78), custom_call_target="tpu_custom_call" | custom-call | tf_op jit(solution)/shard_map/pallas_call | solution.py:173
  298.6 1.6 copy.38
  300.2 3.0 collective-permute-start.4
  303.2 3.2 collective-permute-done.4
  306.4 0.3 copy.39
  306.7 0.1 bitcast_add_fusion.2
  306.8 0.3 copy.40
  307.1 5.1 %collective-permute-start.5 = (f32[8,2048]{1,0:T(8,128)S(1)}, f32[8,2048]{1,0:T(8,128)S(1)}, u32[]{:S(2)}, u32[]{:S(2)}) collective-permute-start(f32[8,2048]{1,0:T(8,128)S(1)} %copy.40), channel_id=1, source_target_pairs={{0,64},{32,96},{64,0},{96,32},{128,192},{160,224},{192,128},{224,1... | collective-permute-start | bytes 196616 | tf_op jit(solution)/shard_map/ppermute | solution.py:34
  312.2 2.6 collective-permute-done.5
  314.8 0.3 copy.41
  315.1 0.1 add.123
  315.2 0.3 copy.42
  315.5 5.3 %collective-permute-start.6 = (f32[8,2048]{1,0:T(8,128)S(1)}, f32[8,2048]{1,0:T(8,128)S(1)}, u32[]{:S(2)}, u32[]{:S(2)}) collective-permute-start(f32[8,2048]{1,0:T(8,128)S(1)} %copy.42), channel_id=1, source_target_pairs={{0,128},{32,160},{64,192},{96,224},{128,0},{160,32},{192,64},{224,... | collective-permute-start | bytes 196616 | tf_op jit(solution)/shard_map/ppermute | solution.py:34
  320.9 2.2 collective-permute-done.6
  323.1 0.3 copy.43
  323.4 0.1 add.124
  323.6 0.3 copy.44
  323.9 4.2 %collective-permute-start.7 = (f32[8,2048]{1,0:T(8,128)S(1)}, f32[8,2048]{1,0:T(8,128)S(1)}, u32[]{:S(2)}, u32[]{:S(2)}) collective-permute-start(f32[8,2048]{1,0:T(8,128)S(1)} %copy.44), channel_id=1, source_target_pairs={{0,256},{32,288},{64,320},{96,352},{128,384},{160,416},{192,448},{... | collective-permute-start | bytes 196616 | tf_op jit(solution)/shard_map/ppermute | solution.py:34
  328.0 3.5 %collective-permute-done.7 = f32[8,2048]{1,0:T(8,128)S(1)} collective-permute-done((f32[8,2048]{1,0:T(8,128)S(1)}, f32[8,2048]{1,0:T(8,128)S(1)}, u32[]{:S(2)}, u32[]{:S(2)}) %collective-permute-start.7) | collective-permute-done | bytes 65568 | tf_op jit(solution)/shard_map/ppermute | solution.py:34
  331.5 0.3 copy.45
  331.9 0.1 add_multiply_fusion
  332.0 0.9 copy.46
  (34 shorter events, 0.4 us)
Async XLA Ops:
  0.0 205.6 %copy-start = (bf16[128,8]{0,1:T(8,128)(2,1)S(1)}, bf16[128,8]{0,1:T(8,128)(2,1)}, u32[]{:S(2)}) copy-start(bf16[128,8]{0,1:T(8,128)(2,1)} %param.26) | copy-start | bytes 6148
  14.7 15.6 %copy-start.5 = (s32[1,27,2048]{2,0,1:T(1,128)S(1)}, s32[1,27,2048]{2,0,1:T(1,128)}, u32[]{:S(2)}) copy-start(s32[1,27,2048]{2,0,1:T(1,128)} %param.19) | copy-start | bytes 663556
  14.7 80.0 %all-to-all-start = ((bf16[32,149,128]{2,1,0:T(8,128)(2,1)}), bf16[32,149,128]{2,1,0:T(8,128)(2,1)S(1)}, u32[]{:S(2)}, u32[]{:S(2)}) async-start(bf16[32,149,128]{2,1,0:T(8,128)(2,1)} %reshape.352), calls=%async_computation | async-start | bytes 2490368 | tf_op jit(solution)/shard_map/all_to_all | solution.py:234
  30.4 0.7 copy-start.7
  100.7 2.7 copy-start.1
  113.3 2.0 copy-start.3
  115.3 6.3 %copy-start.4 = (bf16[27,96,128]{2,1,0:T(8,128)(2,1)S(1)}, bf16[27,96,128]{2,1,0:T(8,128)(2,1)}, u32[]{:S(2)}) copy-start(bf16[27,96,128]{2,1,0:T(8,128)(2,1)} %param.20) | copy-start | bytes 1990660
  116.8 5.9 %collective-permute-start = (bf16[256,96]{1,0:T(8,128)(2,1)S(1)}, bf16[256,96]{1,0:T(8,128)(2,1)S(1)}, u32[]{:S(2)}, u32[]{:S(2)}) collective-permute-start(bf16[256,96]{1,0:T(8,128)(2,1)S(1)} %bitcast.97), channel_id=1, source_target_pairs={{0,1},{1,2},{2,3},{3,4},{4,5},{5,6},{6,7},{7,8},{8,9},{9,10},{10,1... | collective-permute-start | bytes 147464 | tf_op jit(solution)/shard_map/ppermute | solution.py:24
  118.7 4.0 %collective-permute-start.1 = (bf16[256,96]{1,0:T(8,128)(2,1)S(1)}, bf16[256,96]{1,0:T(8,128)(2,1)S(1)}, u32[]{:S(2)}, u32[]{:S(2)}) collective-permute-start(bf16[256,96]{1,0:T(8,128)(2,1)S(1)} %bitcast.96), channel_id=1, source_target_pairs={{1,0},{2,1},{3,2},{4,3},{5,4},{6,5},{7,6},{8,7},{9,8},{10,9},{11,1... | collective-permute-start | bytes 147464 | tf_op jit(solution)/shard_map/ppermute | solution.py:24
  152.6 23.3 %collective-permute-start.2 = (bf16[256,128]{1,0:T(8,128)(2,1)S(1)}, bf16[256,128]{1,0:T(8,128)(2,1)S(1)}, u32[]{:S(2)}, u32[]{:S(2)}) collective-permute-start(bf16[256,128]{1,0:T(8,128)(2,1)S(1)} %bitcast.99), channel_id=1, source_target_pairs={{0,1},{1,2},{2,3},{3,4},{4,5},{5,6},{6,7},{7,8},{8,9},{9,10},{10,1... | collective-permute-start | bytes 196616 | tf_op jit(solution)/shard_map/ppermute | solution.py:24
  174.4 3.4 %collective-permute-start.3 = (bf16[256,128]{1,0:T(8,128)(2,1)S(1)}, bf16[256,128]{1,0:T(8,128)(2,1)S(1)}, u32[]{:S(2)}, u32[]{:S(2)}) collective-permute-start(bf16[256,128]{1,0:T(8,128)(2,1)S(1)} %bitcast.98), channel_id=1, source_target_pairs={{1,0},{2,1},{3,2},{4,3},{5,4},{6,5},{7,6},{8,7},{9,8},{10,9},{11,1... | collective-permute-start | bytes 196616 | tf_op jit(solution)/shard_map/ppermute | solution.py:24
  180.4 25.3 %copy-start.8 = (f32[8]{0:T(128)S(1)}, f32[8]{0:T(128)}, u32[]{:S(2)}) copy-start(f32[8]{0:T(128)} %param.27) | copy-start | bytes 100
  216.1 52.9 %copy-start.6 = (s32[1,2048]{1,0:T(1,128)S(1)}, s32[1,2048]{1,0:T(1,128)}, u32[]{:S(2)}) copy-start(s32[1,2048]{1,0:T(1,128)} %param.15) | copy-start | bytes 24580
  219.3 72.5 %all-to-all-start.1 = ((f32[32,192,8]{1,2,0:T(8,128)}), f32[32,192,8]{1,2,0:T(8,128)S(1)}, u32[]{:S(2)}, u32[]{:S(2)}) async-start(f32[32,192,8]{1,2,0:T(8,128)} %copy.36), calls=%async_computation.1 | async-start | bytes 524288 | tf_op jit(solution)/shard_map/all_to_all | solution.py:269
  298.6 8.1 %copy-start.2 = (f32[2048,8]{1,0:T(8,128)S(1)}, f32[2048,8]{1,0:T(8,128)}, u32[]{:S(2)}) copy-start(f32[2048,8]{1,0:T(8,128)} %shard_map.140) | copy-start | bytes 196612
  300.2 6.2 %collective-permute-start.4 = (f32[8,2048]{1,0:T(8,128)S(1)}, f32[8,2048]{1,0:T(8,128)S(1)}, u32[]{:S(2)}, u32[]{:S(2)}) collective-permute-start(f32[8,2048]{1,0:T(8,128)S(1)} %copy.38), channel_id=1, source_target_pairs={{0,32},{32,0},{64,96},{96,64},{128,160},{160,128},{192,224},{224,1... | collective-permute-start | bytes 196616 | tf_op jit(solution)/shard_map/ppermute | solution.py:34
  307.1 7.7 %collective-permute-start.5 = (f32[8,2048]{1,0:T(8,128)S(1)}, f32[8,2048]{1,0:T(8,128)S(1)}, u32[]{:S(2)}, u32[]{:S(2)}) collective-permute-start(f32[8,2048]{1,0:T(8,128)S(1)} %copy.40), channel_id=1, source_target_pairs={{0,64},{32,96},{64,0},{96,32},{128,192},{160,224},{192,128},{224,1... | collective-permute-start | bytes 196616 | tf_op jit(solution)/shard_map/ppermute | solution.py:34
  315.5 7.6 %collective-permute-start.6 = (f32[8,2048]{1,0:T(8,128)S(1)}, f32[8,2048]{1,0:T(8,128)S(1)}, u32[]{:S(2)}, u32[]{:S(2)}) collective-permute-start(f32[8,2048]{1,0:T(8,128)S(1)} %copy.42), channel_id=1, source_target_pairs={{0,128},{32,160},{64,192},{96,224},{128,0},{160,32},{192,64},{224,... | collective-permute-start | bytes 196616 | tf_op jit(solution)/shard_map/ppermute | solution.py:34
  323.9 7.7 %collective-permute-start.7 = (f32[8,2048]{1,0:T(8,128)S(1)}, f32[8,2048]{1,0:T(8,128)S(1)}, u32[]{:S(2)}, u32[]{:S(2)}) collective-permute-start(f32[8,2048]{1,0:T(8,128)S(1)} %copy.44), channel_id=1, source_target_pairs={{0,256},{32,288},{64,320},{96,352},{128,384},{160,416},{192,448},{... | collective-permute-start | bytes 196616 | tf_op jit(solution)/shard_map/ppermute | solution.py:34

commit v6 on v5

--- a/solution.py
+++ b/solution.py
@@ -104,7 +104,12 @@
     extended = jnp.pad(extended, ((0, 0), (0, channels - width_in)))
     weight_flat = jnp.pad(weight, ((0, 0), (0, channels - width_in), (0, 0))).reshape(-1, width)
     in_specs = [
-        pl.BlockSpec((step_block,), lambda s, a: (s,), memory_space=pltpu.SMEM),
+        pl.BlockSpec(
+            (step_block,),
+            lambda s, a: (s,),
+            memory_space=pltpu.SMEM,
+            pipeline_mode=pl.Buffered(1),
+        ),
         pl.BlockSpec((ext_rows, channels), lambda s, a: (0, 0)),
         pl.BlockSpec(weight_flat.shape, lambda s, a: (0, 0)),
         pl.BlockSpec((1, width), lambda s, a: (0, 0)),

time: 336 us -> 324 us (0.964)
  starting transfers between devices: 110 us -> 63.6 us
  Pallas kernels: 73.2 us -> 92.2 us
  waiting for transfers between devices: 99.1 us -> 113 us
    all_to_all x1, starting transfers between devices: 49.7 us -> 20.1 us  [per_device(): returned = lax.all_to_all(slot_logits, 'slab', 0, 0, tiled=True)]
    pallas_call x2, Pallas kernels: 50.4 us -> 69.5 us  [convolve(): pl.pallas_call(functools.partial(conv_kernel, has_residual=residual is no...]
    ppermute x4, starting transfers between devices: 26.7 us -> 8.2 us  [passed_along(): return lax.ppermute(shard, axis, pairs)]
    ppermute x4, waiting for transfers between devices: 1.89 us -> 16.7 us  [passed_along(): return lax.ppermute(shard, axis, pairs)]
where the time goes in v6:
time: 324 us; the launch traced here: 320 us
  waiting for transfers between devices  113 us (35%)
  Pallas kernels  92.2 us (28%)
  starting transfers between devices  63.6 us (20%)
  local copies, waits for them, and re-layouts  32.6 us (10%)
  other arithmetic  14.2 us (4%)
  matrix products  3.27 us (1%)
    pallas_call x2, Pallas kernels, convolve(): pl.pallas_call(functools.partial(conv_kernel, has_residual=residual is no...  69.5 us
    all_to_all x1, waiting for transfers between devices, per_device(): lax.all_to_all(packed.reshape(slab_count, dense // 128, 128), 'slab', 0,...  63.6 us
    all_to_all x1, waiting for transfers between devices, per_device(): returned = lax.all_to_all(slot_logits, 'slab', 0, 0, tiled=True)  22.1 us
    all_to_all x1, starting transfers between devices, per_device(): returned = lax.all_to_all(slot_logits, 'slab', 0, 0, tiled=True)  20.1 us
    ppermute x4, starting transfers between devices, all_summed(): values = values + lax.ppermute(values, axis, pairs)  19.7 us
    ppermute x4, waiting for transfers between devices, passed_along(): return lax.ppermute(shard, axis, pairs)  16.7 us
    all_to_all x1, starting transfers between devices, per_device(): lax.all_to_all(packed.reshape(slab_count, dense // 128, 128), 'slab', 0,...  15.6 us
    pallas_call x2, Pallas kernels, gather_rows(): pl.pallas_call(gather_kernel, in_specs=[pl.BlockSpec(memory_space=pltpu.S...  12.8 us
  transfers between devices with their start and end apart: 10, of which 7 were waited for; matrix products, arithmetic and copies ran while one was open for 1% of the time, Pallas kernels for 0%

profile of v6, /device:TPU:24, one launch (start us, length us, event | category | flops | bytes accessed | tf_op | source)
XLA Modules:
  0.0 320.2 jit_solution(9202774502121769617)
XLA Ops:
  0.0 0.9 convert_reduce_fusion
  0.9 1.0 fusion.2
  1.9 0.7 compare_select_fusion
  2.6 0.7 fusion.12
  3.5 1.1 maximum_maximum_fusion.1
  4.6 0.3 copy.33
  4.9 6.3 %scatter_custom_fusion = bf16[6144,99]{1,0:T(8,128)(2,1)S(1)} fusion(s32[2048]{0:T(1024)S(1)} %bitcast.102, bf16[2048,99]{1,0:T(8,128)(2,1)S(1)} %copy.33, bf16[]{:T(256)} %constant.47.clone.1), kind=kCustom, calls=%fused_computation.17 | custom fusion | bytes 1216514 | tf_op jit(solution)/shard_map/scatter | solution.py:234
  11.2 1.9 reshape.351
  13.2 1.5 reshape.352
  14.7 15.6 %all-to-all-start = ((bf16[32,149,128]{2,1,0:T(8,128)(2,1)}), bf16[32,149,128]{2,1,0:T(8,128)(2,1)S(1)}, u32[]{:S(2)}, u32[]{:S(2)}) async-start(bf16[32,149,128]{2,1,0:T(8,128)(2,1)} %reshape.352), calls=%async_computation | async-start | bytes 2490368 | tf_op jit(solution)/shard_map/all_to_all | solution.py:239
  30.4 0.5 reduce.2
  30.9 0.1 copy.49
  31.1 63.6 %all-to-all-done = bf16[32,149,128]{2,1,0:T(8,128)(2,1)S(1)} async-done(((bf16[32,149,128]{2,1,0:T(8,128)(2,1)}), bf16[32,149,128]{2,1,0:T(8,128)(2,1)S(1)}, u32[]{:S(2)}, u32[]{:S(2)}) %all-to-all-start) | async-done | bytes 1220640 | tf_op jit(solution)/shard_map/all_to_all | solution.py:239
  94.7 0.2 copy.52
  94.9 5.8 %reshape.354.feats_ref = bf16[6144,99]{1,0:T(8,128)(2,1)S(1)} reshape(bf16[32,19008]{1,0:T(8,128)(2,1)S(1)} %bitcast.83) | data formatting | bytes 2433024 | tf_op jit(solution)/shard_map/reshape | solution.py:242
  100.7 2.7 add_reduce_fusion.index_ref
  103.4 9.9 %shard_map.136 = f32[2048,99]{1,0:T(8,128)} custom-call(s32[1,6144]{1,0:T(1,128)} %bitcast.93, bf16[6144,99]{1,0:T(8,128)(2,1)} %copy-done.1), custom_call_target="tpu_custom_call" | custom-call | tf_op jit(solution)/shard_map/pallas_call | solution.py:157
  113.3 1.9 fusion.3
  115.3 0.3 fusion.4
  115.6 0.6 gather_fusion.1
  116.2 0.6 gather_fusion
  116.8 1.9 collective-permute-start
  118.7 1.5 collective-permute-start.1
  120.8 0.7 copy.50
  121.6 1.1 pad.23
  122.6 0.4 maximum_maximum_fusion
  123.1 1.2 pad_convert_fusion.ext_ref
  124.2 34.7 %shard_map.137.rest_0_ = bf16[2048,128]{1,0:T(8,128)(2,1)} custom-call(s32[1]{0:T(128)} %bitcast.9.active_ref, s32[57344]{0:T(1024)} %bitcast.87, f32[2568,128]{1,0:T(8,128)} %pad_convert_fusion.ext_ref, bf16[3456,128]{1,0:T(8,128)(2,1)} %bitcast.84, f32[1,128]{1,0:T(1,128)} %bitcast.103, f32[1,128]{1,0:T(1,128)} %bitcast.104), custom_call_target="tpu_custom_call" | custom-call | tf_op jit(solution)/shard_map/pallas_call | solution.py:135
  158.9 1.6 gather_fusion.3
  160.5 1.6 gather_fusion.2
  162.1 3.5 %collective-permute-start.2 = (bf16[256,128]{1,0:T(8,128)(2,1)S(1)}, bf16[256,128]{1,0:T(8,128)(2,1)S(1)}, u32[]{:S(2)}, u32[]{:S(2)}) collective-permute-start(bf16[256,128]{1,0:T(8,128)(2,1)S(1)} %bitcast.99), channel_id=1, source_target_pairs={{0,1},{1,2},{2,3},{3,4},{4,5},{5,6},{6,7},{7,8},{8,9},{9,10},{10,1... | collective-permute-start | bytes 196616 | tf_op jit(solution)/shard_map/ppermute | solution.py:24
  165.7 1.3 collective-permute-start.3
  167.0 16.7 %collective-permute-done.3 = bf16[256,128]{1,0:T(8,128)(2,1)S(1)} collective-permute-done((bf16[256,128]{1,0:T(8,128)(2,1)S(1)}, bf16[256,128]{1,0:T(8,128)(2,1)S(1)}, u32[]{:S(2)}, u32[]{:S(2)}) %collective-permute-start.3) | collective-permute-done | bytes 65568 | tf_op jit(solution)/shard_map/ppermute | solution.py:24
  183.7 2.5 maximum_convert_fusion.ext_ref
  186.2 34.8 %shard_map.138 = bf16[2048,128]{1,0:T(8,128)(2,1)} custom-call(s32[1]{0:T(128)} %bitcast.9.active_ref, s32[57344]{0:T(1024)} %bitcast.88, f32[2568,128]{1,0:T(8,128)} %maximum_convert_fusion.ext_ref, bf16[3456,128]{1,0:T(8,128)(2,1)} %bitcast.91, f32[1,128]{1,0:T(1,128)} %bitcast.105, f32[1,128]{1,0:T(1,128)} %bitcast.106, bf16[2048,128]{1,0:T(8,128)(2,1)} %shard_map.137.rest_0_), custom_call_target="tpu_custom_call" | custom-call | tf_op jit(solution)/shard_map/pallas_call | solution.py:135
  221.0 2.3 convolution_add_fusion.table_ref
  223.3 8.2 %shard_map.139 = f32[6144,8]{1,0:T(8,128)} custom-call(s32[6144]{0:T(1024)} %add_reduce_fusion.index_ref, f32[2048,8]{1,0:T(8,128)} %convolution_add_fusion.table_ref), custom_call_target="tpu_custom_call" | custom-call | tf_op jit(solution)/shard_map/pallas_call | solution.py:178
  231.4 3.2 %copy.36 = f32[32,192,8]{1,2,0:T(8,128)} copy(f32[32,192,8]{2,1,0:T(8,128)} %bitcast.77) | data formatting | bytes 393216 | tf_op jit(solution)/shard_map/reshape | solution.py:273
  234.7 20.1 %all-to-all-start.1 = ((f32[32,192,8]{1,2,0:T(8,128)}), f32[32,192,8]{1,2,0:T(8,128)S(1)}, u32[]{:S(2)}, u32[]{:S(2)}) async-start(f32[32,192,8]{1,2,0:T(8,128)} %copy.36), calls=%async_computation.1 | async-start | bytes 524288 | tf_op jit(solution)/shard_map/all_to_all | solution.py:274
  254.8 0.6 bitcast_add_fusion.1.index_ref
  255.4 22.1 %all-to-all-done.1 = f32[32,192,8]{1,2,0:T(8,128)S(1)} async-done(((f32[32,192,8]{1,2,0:T(8,128)}), f32[32,192,8]{1,2,0:T(8,128)S(1)}, u32[]{:S(2)}, u32[]{:S(2)}) %all-to-all-start.1) | async-done | bytes 196640 | tf_op jit(solution)/shard_map/all_to_all | solution.py:274
  277.5 2.2 copy.37
  279.7 4.6 %shard_map.140 = f32[2048,8]{1,0:T(8,128)} custom-call(s32[2048]{0:T(1024)} %bitcast_add_fusion.1.index_ref, f32[6144,8]{1,0:T(8,128)} %bitcast.78), custom_call_target="tpu_custom_call" | custom-call | tf_op jit(solution)/shard_map/pallas_call | solution.py:178
  284.4 1.6 copy.38
  286.0 2.5 collective-permute-start.4
  288.4 3.7 %collective-permute-done.4 = f32[8,2048]{1,0:T(8,128)S(1)} collective-permute-done((f32[8,2048]{1,0:T(8,128)S(1)}, f32[8,2048]{1,0:T(8,128)S(1)}, u32[]{:S(2)}, u32[]{:S(2)}) %collective-permute-start.4) | collective-permute-done | bytes 65568 | tf_op jit(solution)/shard_map/ppermute | solution.py:34
  292.1 0.3 copy.39
  292.5 0.1 bitcast_add_fusion.2
  292.6 0.3 copy.40
  292.9 5.0 %collective-permute-start.5 = (f32[8,2048]{1,0:T(8,128)S(1)}, f32[8,2048]{1,0:T(8,128)S(1)}, u32[]{:S(2)}, u32[]{:S(2)}) collective-permute-start(f32[8,2048]{1,0:T(8,128)S(1)} %copy.40), channel_id=1, source_target_pairs={{0,64},{32,96},{64,0},{96,32},{128,192},{160,224},{192,128},{224,1... | collective-permute-start | bytes 196616 | tf_op jit(solution)/shard_map/ppermute | solution.py:34
  297.9 2.7 collective-permute-done.5
  300.5 0.3 copy.41
  300.9 0.1 add.123
  301.0 0.3 copy.42
  301.3 5.2 %collective-permute-start.6 = (f32[8,2048]{1,0:T(8,128)S(1)}, f32[8,2048]{1,0:T(8,128)S(1)}, u32[]{:S(2)}, u32[]{:S(2)}) collective-permute-start(f32[8,2048]{1,0:T(8,128)S(1)} %copy.42), channel_id=1, source_target_pairs={{0,128},{32,160},{64,192},{96,224},{128,0},{160,32},{192,64},{224,... | collective-permute-start | bytes 196616 | tf_op jit(solution)/shard_map/ppermute | solution.py:34
  306.5 2.2 collective-permute-done.6
  308.7 0.3 copy.43
  309.1 0.1 add.124
  309.2 0.3 copy.44
  309.5 7.0 %collective-permute-start.7 = (f32[8,2048]{1,0:T(8,128)S(1)}, f32[8,2048]{1,0:T(8,128)S(1)}, u32[]{:S(2)}, u32[]{:S(2)}) collective-permute-start(f32[8,2048]{1,0:T(8,128)S(1)} %copy.44), channel_id=1, source_target_pairs={{0,256},{32,288},{64,320},{96,352},{128,384},{160,416},{192,448},{... | collective-permute-start | bytes 196616 | tf_op jit(solution)/shard_map/ppermute | solution.py:34
  316.5 2.2 collective-permute-done.7
  318.8 0.3 copy.45
  319.1 0.1 add_multiply_fusion
  319.2 0.9 copy.46
  (34 shorter events, 0.4 us)
Async XLA Ops:
  0.0 221.0 %copy-start = (bf16[128,8]{0,1:T(8,128)(2,1)S(1)}, bf16[128,8]{0,1:T(8,128)(2,1)}, u32[]{:S(2)}) copy-start(bf16[128,8]{0,1:T(8,128)(2,1)} %param.26) | copy-start | bytes 6148
  14.7 15.6 %copy-start.5 = (s32[1,27,2048]{2,0,1:T(1,128)S(1)}, s32[1,27,2048]{2,0,1:T(1,128)}, u32[]{:S(2)}) copy-start(s32[1,27,2048]{2,0,1:T(1,128)} %param.19) | copy-start | bytes 663556
  14.7 80.0 %all-to-all-start = ((bf16[32,149,128]{2,1,0:T(8,128)(2,1)}), bf16[32,149,128]{2,1,0:T(8,128)(2,1)S(1)}, u32[]{:S(2)}, u32[]{:S(2)}) async-start(bf16[32,149,128]{2,1,0:T(8,128)(2,1)} %reshape.352), calls=%async_computation | async-start | bytes 2490368 | tf_op jit(solution)/shard_map/all_to_all | solution.py:239
  30.4 0.7 copy-start.7
  100.7 2.7 copy-start.1
  113.3 2.0 copy-start.3
  115.3 6.3 %copy-start.4 = (bf16[27,96,128]{2,1,0:T(8,128)(2,1)S(1)}, bf16[27,96,128]{2,1,0:T(8,128)(2,1)}, u32[]{:S(2)}) copy-start(bf16[27,96,128]{2,1,0:T(8,128)(2,1)} %param.20) | copy-start | bytes 1990660
  116.8 5.9 %collective-permute-start = (bf16[256,96]{1,0:T(8,128)(2,1)S(1)}, bf16[256,96]{1,0:T(8,128)(2,1)S(1)}, u32[]{:S(2)}, u32[]{:S(2)}) collective-permute-start(bf16[256,96]{1,0:T(8,128)(2,1)S(1)} %bitcast.97), channel_id=1, source_target_pairs={{0,1},{1,2},{2,3},{3,4},{4,5},{5,6},{6,7},{7,8},{8,9},{9,10},{10,1... | collective-permute-start | bytes 147464 | tf_op jit(solution)/shard_map/ppermute | solution.py:24
  118.7 4.0 %collective-permute-start.1 = (bf16[256,96]{1,0:T(8,128)(2,1)S(1)}, bf16[256,96]{1,0:T(8,128)(2,1)S(1)}, u32[]{:S(2)}, u32[]{:S(2)}) collective-permute-start(bf16[256,96]{1,0:T(8,128)(2,1)S(1)} %bitcast.96), channel_id=1, source_target_pairs={{1,0},{2,1},{3,2},{4,3},{5,4},{6,5},{7,6},{8,7},{9,8},{10,9},{11,1... | collective-permute-start | bytes 147464 | tf_op jit(solution)/shard_map/ppermute | solution.py:24
  162.1 4.8 %collective-permute-start.2 = (bf16[256,128]{1,0:T(8,128)(2,1)S(1)}, bf16[256,128]{1,0:T(8,128)(2,1)S(1)}, u32[]{:S(2)}, u32[]{:S(2)}) collective-permute-start(bf16[256,128]{1,0:T(8,128)(2,1)S(1)} %bitcast.99), channel_id=1, source_target_pairs={{0,1},{1,2},{2,3},{3,4},{4,5},{5,6},{6,7},{7,8},{8,9},{9,10},{10,1... | collective-permute-start | bytes 196616 | tf_op jit(solution)/shard_map/ppermute | solution.py:24
  165.7 18.0 %collective-permute-start.3 = (bf16[256,128]{1,0:T(8,128)(2,1)S(1)}, bf16[256,128]{1,0:T(8,128)(2,1)S(1)}, u32[]{:S(2)}, u32[]{:S(2)}) collective-permute-start(bf16[256,128]{1,0:T(8,128)(2,1)S(1)} %bitcast.98), channel_id=1, source_target_pairs={{1,0},{2,1},{3,2},{4,3},{5,4},{6,5},{7,6},{8,7},{9,8},{10,9},{11,1... | collective-permute-start | bytes 196616 | tf_op jit(solution)/shard_map/ppermute | solution.py:24
  186.2 34.8 %copy-start.8 = (f32[8]{0:T(128)S(1)}, f32[8]{0:T(128)}, u32[]{:S(2)}) copy-start(f32[8]{0:T(128)} %param.27) | copy-start | bytes 100
  231.4 23.3 %copy-start.6 = (s32[1,2048]{1,0:T(1,128)S(1)}, s32[1,2048]{1,0:T(1,128)}, u32[]{:S(2)}) copy-start(s32[1,2048]{1,0:T(1,128)} %param.15) | copy-start | bytes 24580
  234.7 42.9 %all-to-all-start.1 = ((f32[32,192,8]{1,2,0:T(8,128)}), f32[32,192,8]{1,2,0:T(8,128)S(1)}, u32[]{:S(2)}, u32[]{:S(2)}) async-start(f32[32,192,8]{1,2,0:T(8,128)} %copy.36), calls=%async_computation.1 | async-start | bytes 524288 | tf_op jit(solution)/shard_map/all_to_all | solution.py:274
  284.3 8.1 %copy-start.2 = (f32[2048,8]{1,0:T(8,128)S(1)}, f32[2048,8]{1,0:T(8,128)}, u32[]{:S(2)}) copy-start(f32[2048,8]{1,0:T(8,128)} %shard_map.140) | copy-start | bytes 196612
  286.0 6.2 %collective-permute-start.4 = (f32[8,2048]{1,0:T(8,128)S(1)}, f32[8,2048]{1,0:T(8,128)S(1)}, u32[]{:S(2)}, u32[]{:S(2)}) collective-permute-start(f32[8,2048]{1,0:T(8,128)S(1)} %copy.38), channel_id=1, source_target_pairs={{0,32},{32,0},{64,96},{96,64},{128,160},{160,128},{192,224},{224,1... | collective-permute-start | bytes 196616 | tf_op jit(solution)/shard_map/ppermute | solution.py:34
  292.9 7.7 %collective-permute-start.5 = (f32[8,2048]{1,0:T(8,128)S(1)}, f32[8,2048]{1,0:T(8,128)S(1)}, u32[]{:S(2)}, u32[]{:S(2)}) collective-permute-start(f32[8,2048]{1,0:T(8,128)S(1)} %copy.40), channel_id=1, source_target_pairs={{0,64},{32,96},{64,0},{96,32},{128,192},{160,224},{192,128},{224,1... | collective-permute-start | bytes 196616 | tf_op jit(solution)/shard_map/ppermute | solution.py:34
  301.3 7.4 %collective-permute-start.6 = (f32[8,2048]{1,0:T(8,128)S(1)}, f32[8,2048]{1,0:T(8,128)S(1)}, u32[]{:S(2)}, u32[]{:S(2)}) collective-permute-start(f32[8,2048]{1,0:T(8,128)S(1)} %copy.42), channel_id=1, source_target_pairs={{0,128},{32,160},{64,192},{96,224},{128,0},{160,32},{192,64},{224,... | collective-permute-start | bytes 196616 | tf_op jit(solution)/shard_map/ppermute | solution.py:34
  309.5 9.3 %collective-permute-start.7 = (f32[8,2048]{1,0:T(8,128)S(1)}, f32[8,2048]{1,0:T(8,128)S(1)}, u32[]{:S(2)}, u32[]{:S(2)}) collective-permute-start(f32[8,2048]{1,0:T(8,128)S(1)} %copy.44), channel_id=1, source_target_pairs={{0,256},{32,288},{64,320},{96,352},{128,384},{160,416},{192,448},{... | collective-permute-start | bytes 196616 | tf_op jit(solution)/shard_map/ppermute | solution.py:34

commit v7 on v6

--- a/solution.py
+++ b/solution.py
@@ -16,6 +16,7 @@
 POOL_COLS = 512
 DIGIT = 64
 RANK_BLOCK = 128
+GATHER_ROWS = 1024
 
 
 def passed_along(shard, axis, by):
@@ -171,18 +172,23 @@
         out_ref[pl.ds(i, 1), :] = table_ref[pl.ds(index_ref[i], 1), :]
         return carry
 
-    lax.fori_loop(0, out_ref.shape[0], pick, 0, unroll=64)
+    lax.fori_loop(0, out_ref.shape[0], pick, 0, unroll=True)
 
 
 def gather_rows(table, index):
+    count = index.shape[0]
+    rows = GATHER_ROWS if count % GATHER_ROWS == 0 else count
     return pl.pallas_call(
         gather_kernel,
+        grid=(count // rows,),
         in_specs=[
-            pl.BlockSpec(memory_space=pltpu.SMEM),
-            pl.BlockSpec(memory_space=pltpu.VMEM),
+            pl.BlockSpec(
+                (rows,), lambda s: (s,), memory_space=pltpu.SMEM, pipeline_mode=pl.Buffered(1)
+            ),
+            pl.BlockSpec(table.shape, lambda s: (0, 0)),
         ],
-        out_specs=pl.BlockSpec(memory_space=pltpu.VMEM),
-        out_shape=jax.ShapeDtypeStruct((index.shape[0], table.shape[1]), table.dtype),
+        out_specs=pl.BlockSpec((rows, table.shape[1]), lambda s: (s, 0)),
+        out_shape=jax.ShapeDtypeStruct((count, table.shape[1]), table.dtype),
     )(index, table)
 
 

time: 324 us -> 325 us (level)
  Pallas kernels: 92.2 us -> 103 us
  waiting for transfers between devices: 113 us -> 103 us
    ppermute x4, waiting for transfers between devices: 16.7 us -> 1.85 us  [passed_along(): return lax.ppermute(shard, axis, pairs)]
    pallas_call x2, Pallas kernels: 69.5 us -> 79.2 us  [convolve(): pl.pallas_call(functools.partial(conv_kernel, has_residual=residual is no...]
    ppermute x4, starting transfers between devices: 8.2 us -> 17.9 us  [passed_along(): return lax.ppermute(shard, axis, pairs)]
    all_to_all x1, starting transfers between devices: 20.1 us -> 15.7 us  [per_device(): returned = lax.all_to_all(slot_logits, 'slab', 0, 0, tiled=True)]
    ppermute x4, waiting for transfers between devices: 10.8 us -> 15.3 us  [all_summed(): values = values + lax.ppermute(values, axis, pairs)]
    ppermute x4, starting transfers between devices: 19.7 us -> 15.4 us  [all_summed(): values = values + lax.ppermute(values, axis, pairs)]
where the time goes in v7:
time: 325 us; the launch traced here: 321 us
  waiting for transfers between devices  103 us (32%)
  Pallas kernels  103 us (32%)
  starting transfers between devices  64.5 us (20%)
  local copies, waits for them, and re-layouts  32.6 us (10%)
  other arithmetic  14.2 us (4%)
  matrix products  3.27 us (1%)
    pallas_call x2, Pallas kernels, convolve(): pl.pallas_call(functools.partial(conv_kernel, has_residual=residual is no...  79.2 us
    all_to_all x1, waiting for transfers between devices, per_device(): lax.all_to_all(packed.reshape(slab_count, dense // 128, 128), 'slab', 0,...  63.6 us
    all_to_all x1, waiting for transfers between devices, per_device(): returned = lax.all_to_all(slot_logits, 'slab', 0, 0, tiled=True)  21.9 us
    ppermute x4, starting transfers between devices, passed_along(): return lax.ppermute(shard, axis, pairs)  17.9 us
    all_to_all x1, starting transfers between devices, per_device(): returned = lax.all_to_all(slot_logits, 'slab', 0, 0, tiled=True)  15.7 us
    all_to_all x1, starting transfers between devices, per_device(): lax.all_to_all(packed.reshape(slab_count, dense // 128, 128), 'slab', 0,...  15.6 us
    ppermute x4, starting transfers between devices, all_summed(): values = values + lax.ppermute(values, axis, pairs)  15.4 us
    ppermute x4, waiting for transfers between devices, all_summed(): values = values + lax.ppermute(values, axis, pairs)  15.3 us
  transfers between devices with their start and end apart: 10, of which 7 were waited for; matrix products, arithmetic and copies ran while one was open for 1% of the time, Pallas kernels for 0%

profile of v7, /device:TPU:24, one launch (start us, length us, event | category | flops | bytes accessed | tf_op | source)
XLA Modules:
  0.0 320.8 jit_solution(6781265994661144412)
XLA Ops:
  0.0 0.9 convert_reduce_fusion
  0.9 1.0 fusion.2
  1.9 0.7 compare_select_fusion
  2.6 0.7 fusion.12
  3.5 1.1 maximum_maximum_fusion.1
  4.6 0.3 copy.33
  4.9 6.3 %scatter_custom_fusion = bf16[6144,99]{1,0:T(8,128)(2,1)S(1)} fusion(s32[2048]{0:T(1024)S(1)} %bitcast.102, bf16[2048,99]{1,0:T(8,128)(2,1)S(1)} %copy.33, bf16[]{:T(256)} %constant.47.clone.1), kind=kCustom, calls=%fused_computation.17 | custom fusion | bytes 1216514 | tf_op jit(solution)/shard_map/scatter | solution.py:240
  11.2 1.9 reshape.351
  13.2 1.5 reshape.352
  14.7 15.6 %all-to-all-start = ((bf16[32,149,128]{2,1,0:T(8,128)(2,1)}), bf16[32,149,128]{2,1,0:T(8,128)(2,1)S(1)}, u32[]{:S(2)}, u32[]{:S(2)}) async-start(bf16[32,149,128]{2,1,0:T(8,128)(2,1)} %reshape.352), calls=%async_computation | async-start | bytes 2490368 | tf_op jit(solution)/shard_map/all_to_all | solution.py:245
  30.4 0.5 reduce.2
  30.9 0.1 copy.49
  31.1 63.6 %all-to-all-done = bf16[32,149,128]{2,1,0:T(8,128)(2,1)S(1)} async-done(((bf16[32,149,128]{2,1,0:T(8,128)(2,1)}), bf16[32,149,128]{2,1,0:T(8,128)(2,1)S(1)}, u32[]{:S(2)}, u32[]{:S(2)}) %all-to-all-start) | async-done | bytes 1220640 | tf_op jit(solution)/shard_map/all_to_all | solution.py:245
  94.7 0.2 copy.52
  94.9 5.8 %reshape.354.feats_ref = bf16[6144,99]{1,0:T(8,128)(2,1)S(1)} reshape(bf16[32,19008]{1,0:T(8,128)(2,1)S(1)} %bitcast.83) | data formatting | bytes 2433024 | tf_op jit(solution)/shard_map/reshape | solution.py:248
  100.7 2.7 add_reduce_fusion.index_ref
  103.4 9.9 %shard_map.136 = f32[2048,99]{1,0:T(8,128)} custom-call(s32[1,6144]{1,0:T(1,128)} %bitcast.93, bf16[6144,99]{1,0:T(8,128)(2,1)} %copy-done.1), custom_call_target="tpu_custom_call" | custom-call | tf_op jit(solution)/shard_map/pallas_call | solution.py:158
  113.3 1.9 fusion.3
  115.3 0.3 fusion.4
  115.6 0.6 gather_fusion.1
  116.2 0.6 gather_fusion
  116.8 1.9 collective-permute-start
  118.7 1.5 collective-permute-start.1
  120.8 0.7 copy.50
  121.6 1.1 pad.23
  122.6 0.4 maximum_maximum_fusion
  123.1 1.2 pad_convert_fusion.ext_ref
  124.2 39.6 %shard_map.137.rest_0_ = bf16[2048,128]{1,0:T(8,128)(2,1)} custom-call(s32[1]{0:T(128)} %bitcast.9.active_ref, s32[57344]{0:T(1024)} %bitcast.87, f32[2568,128]{1,0:T(8,128)} %pad_convert_fusion.ext_ref, bf16[3456,128]{1,0:T(8,128)(2,1)} %bitcast.84, f32[1,128]{1,0:T(1,128)} %bitcast.103, f32[1,128]{1,0:T(1,128)} %bitcast.104), custom_call_target="tpu_custom_call" | custom-call | tf_op jit(solution)/shard_map/pallas_call | solution.py:136
  163.8 1.6 gather_fusion.3
  165.4 1.6 gather_fusion.2
  167.0 13.2 %collective-permute-start.2 = (bf16[256,128]{1,0:T(8,128)(2,1)S(1)}, bf16[256,128]{1,0:T(8,128)(2,1)S(1)}, u32[]{:S(2)}, u32[]{:S(2)}) collective-permute-start(bf16[256,128]{1,0:T(8,128)(2,1)S(1)} %bitcast.99), channel_id=1, source_target_pairs={{0,1},{1,2},{2,3},{3,4},{4,5},{5,6},{6,7},{7,8},{8,9},{9,10},{10,1... | collective-permute-start | bytes 196616 | tf_op jit(solution)/shard_map/ppermute | solution.py:25
  180.2 1.3 collective-permute-start.3
  181.5 1.8 collective-permute-done.3
  183.4 2.5 maximum_convert_fusion.ext_ref
  185.9 39.6 %shard_map.138 = bf16[2048,128]{1,0:T(8,128)(2,1)} custom-call(s32[1]{0:T(128)} %bitcast.9.active_ref, s32[57344]{0:T(1024)} %bitcast.88, f32[2568,128]{1,0:T(8,128)} %maximum_convert_fusion.ext_ref, bf16[3456,128]{1,0:T(8,128)(2,1)} %bitcast.91, f32[1,128]{1,0:T(1,128)} %bitcast.105, f32[1,128]{1,0:T(1,128)} %bitcast.106, bf16[2048,128]{1,0:T(8,128)(2,1)} %shard_map.137.rest_0_), custom_call_target="tpu_custom_call" | custom-call | tf_op jit(solution)/shard_map/pallas_call | solution.py:136
  225.5 2.3 convolution_add_fusion.table_ref
  227.8 9.0 %shard_map.139 = f32[6144,8]{1,0:T(8,128)} custom-call(s32[6144]{0:T(1024)} %add_reduce_fusion.index_ref, f32[2048,8]{1,0:T(8,128)} %convolution_add_fusion.table_ref), custom_call_target="tpu_custom_call" | custom-call | tf_op jit(solution)/shard_map/pallas_call | solution.py:181
  236.8 3.2 %copy.36 = f32[32,192,8]{1,2,0:T(8,128)} copy(f32[32,192,8]{2,1,0:T(8,128)} %bitcast.77) | data formatting | bytes 393216 | tf_op jit(solution)/shard_map/reshape | solution.py:279
  240.0 15.7 %all-to-all-start.1 = ((f32[32,192,8]{1,2,0:T(8,128)}), f32[32,192,8]{1,2,0:T(8,128)S(1)}, u32[]{:S(2)}, u32[]{:S(2)}) async-start(f32[32,192,8]{1,2,0:T(8,128)} %copy.36), calls=%async_computation.1 | async-start | bytes 524288 | tf_op jit(solution)/shard_map/all_to_all | solution.py:280
  255.7 0.6 bitcast_add_fusion.1.index_ref
  256.3 21.9 %all-to-all-done.1 = f32[32,192,8]{1,2,0:T(8,128)S(1)} async-done(((f32[32,192,8]{1,2,0:T(8,128)}), f32[32,192,8]{1,2,0:T(8,128)S(1)}, u32[]{:S(2)}, u32[]{:S(2)}) %all-to-all-start.1) | async-done | bytes 196640 | tf_op jit(solution)/shard_map/all_to_all | solution.py:280
  278.2 2.2 copy.37
  280.4 4.5 %shard_map.140 = f32[2048,8]{1,0:T(8,128)} custom-call(s32[2048]{0:T(1024)} %bitcast_add_fusion.1.index_ref, f32[6144,8]{1,0:T(8,128)} %bitcast.78), custom_call_target="tpu_custom_call" | custom-call | tf_op jit(solution)/shard_map/pallas_call | solution.py:181
  284.9 1.6 copy.38
  286.5 6.9 %collective-permute-start.4 = (f32[8,2048]{1,0:T(8,128)S(1)}, f32[8,2048]{1,0:T(8,128)S(1)}, u32[]{:S(2)}, u32[]{:S(2)}) collective-permute-start(f32[8,2048]{1,0:T(8,128)S(1)} %copy.38), channel_id=1, source_target_pairs={{0,32},{32,0},{64,96},{96,64},{128,160},{160,128},{192,224},{224,1... | collective-permute-start | bytes 196616 | tf_op jit(solution)/shard_map/ppermute | solution.py:35
  293.5 2.2 collective-permute-done.4
  295.7 0.3 copy.39
  296.0 0.1 bitcast_add_fusion.2
  296.2 0.3 copy.40
  296.5 3.6 %collective-permute-start.5 = (f32[8,2048]{1,0:T(8,128)S(1)}, f32[8,2048]{1,0:T(8,128)S(1)}, u32[]{:S(2)}, u32[]{:S(2)}) collective-permute-start(f32[8,2048]{1,0:T(8,128)S(1)} %copy.40), channel_id=1, source_target_pairs={{0,64},{32,96},{64,0},{96,32},{128,192},{160,224},{192,128},{224,1... | collective-permute-start | bytes 196616 | tf_op jit(solution)/shard_map/ppermute | solution.py:35
  300.1 4.0 %collective-permute-done.5 = f32[8,2048]{1,0:T(8,128)S(1)} collective-permute-done((f32[8,2048]{1,0:T(8,128)S(1)}, f32[8,2048]{1,0:T(8,128)S(1)}, u32[]{:S(2)}, u32[]{:S(2)}) %collective-permute-start.5) | collective-permute-done | bytes 65568 | tf_op jit(solution)/shard_map/ppermute | solution.py:35
  304.1 0.3 copy.41
  304.5 0.1 add.123
  304.6 0.3 copy.42
  304.9 2.2 collective-permute-start.6
  307.1 4.0 %collective-permute-done.6 = f32[8,2048]{1,0:T(8,128)S(1)} collective-permute-done((f32[8,2048]{1,0:T(8,128)S(1)}, f32[8,2048]{1,0:T(8,128)S(1)}, u32[]{:S(2)}, u32[]{:S(2)}) %collective-permute-start.6) | collective-permute-done | bytes 65568 | tf_op jit(solution)/shard_map/ppermute | solution.py:35
  311.0 0.3 copy.43
  311.4 0.1 add.124
  311.5 0.3 copy.44
  311.8 2.6 collective-permute-start.7
  314.4 5.0 %collective-permute-done.7 = f32[8,2048]{1,0:T(8,128)S(1)} collective-permute-done((f32[8,2048]{1,0:T(8,128)S(1)}, f32[8,2048]{1,0:T(8,128)S(1)}, u32[]{:S(2)}, u32[]{:S(2)}) %collective-permute-start.7) | collective-permute-done | bytes 65568 | tf_op jit(solution)/shard_map/ppermute | solution.py:35
  319.4 0.3 copy.45
  319.8 0.1 add_multiply_fusion
  319.9 0.9 copy.46
  (34 shorter events, 0.4 us)
Async XLA Ops:
  0.0 225.5 %copy-start = (bf16[128,8]{0,1:T(8,128)(2,1)S(1)}, bf16[128,8]{0,1:T(8,128)(2,1)}, u32[]{:S(2)}) copy-start(bf16[128,8]{0,1:T(8,128)(2,1)} %param.26) | copy-start | bytes 6148
  14.7 15.6 %copy-start.5 = (s32[1,27,2048]{2,0,1:T(1,128)S(1)}, s32[1,27,2048]{2,0,1:T(1,128)}, u32[]{:S(2)}) copy-start(s32[1,27,2048]{2,0,1:T(1,128)} %param.19) | copy-start | bytes 663556
  14.7 80.0 %all-to-all-start = ((bf16[32,149,128]{2,1,0:T(8,128)(2,1)}), bf16[32,149,128]{2,1,0:T(8,128)(2,1)S(1)}, u32[]{:S(2)}, u32[]{:S(2)}) async-start(bf16[32,149,128]{2,1,0:T(8,128)(2,1)} %reshape.352), calls=%async_computation | async-start | bytes 2490368 | tf_op jit(solution)/shard_map/all_to_all | solution.py:245
  30.4 0.7 copy-start.7
  100.7 2.7 copy-start.1
  113.3 2.0 copy-start.3
  115.3 6.3 %copy-start.4 = (bf16[27,96,128]{2,1,0:T(8,128)(2,1)S(1)}, bf16[27,96,128]{2,1,0:T(8,128)(2,1)}, u32[]{:S(2)}) copy-start(bf16[27,96,128]{2,1,0:T(8,128)(2,1)} %param.20) | copy-start | bytes 1990660
  116.8 5.9 %collective-permute-start = (bf16[256,96]{1,0:T(8,128)(2,1)S(1)}, bf16[256,96]{1,0:T(8,128)(2,1)S(1)}, u32[]{:S(2)}, u32[]{:S(2)}) collective-permute-start(bf16[256,96]{1,0:T(8,128)(2,1)S(1)} %bitcast.97), channel_id=1, source_target_pairs={{0,1},{1,2},{2,3},{3,4},{4,5},{5,6},{6,7},{7,8},{8,9},{9,10},{10,1... | collective-permute-start | bytes 147464 | tf_op jit(solution)/shard_map/ppermute | solution.py:25
  118.7 4.0 %collective-permute-start.1 = (bf16[256,96]{1,0:T(8,128)(2,1)S(1)}, bf16[256,96]{1,0:T(8,128)(2,1)S(1)}, u32[]{:S(2)}, u32[]{:S(2)}) collective-permute-start(bf16[256,96]{1,0:T(8,128)(2,1)S(1)} %bitcast.96), channel_id=1, source_target_pairs={{1,0},{2,1},{3,2},{4,3},{5,4},{6,5},{7,6},{8,7},{9,8},{10,9},{11,1... | collective-permute-start | bytes 147464 | tf_op jit(solution)/shard_map/ppermute | solution.py:25
  167.0 14.5 %collective-permute-start.2 = (bf16[256,128]{1,0:T(8,128)(2,1)S(1)}, bf16[256,128]{1,0:T(8,128)(2,1)S(1)}, u32[]{:S(2)}, u32[]{:S(2)}) collective-permute-start(bf16[256,128]{1,0:T(8,128)(2,1)S(1)} %bitcast.99), channel_id=1, source_target_pairs={{0,1},{1,2},{2,3},{3,4},{4,5},{5,6},{6,7},{7,8},{8,9},{9,10},{10,1... | collective-permute-start | bytes 196616 | tf_op jit(solution)/shard_map/ppermute | solution.py:25
  180.2 3.1 collective-permute-start.3
  185.9 39.7 %copy-start.8 = (f32[8]{0:T(128)S(1)}, f32[8]{0:T(128)}, u32[]{:S(2)}) copy-start(f32[8]{0:T(128)} %param.27) | copy-start | bytes 100
  236.8 18.9 %copy-start.6 = (s32[1,2048]{1,0:T(1,128)S(1)}, s32[1,2048]{1,0:T(1,128)}, u32[]{:S(2)}) copy-start(s32[1,2048]{1,0:T(1,128)} %param.15) | copy-start | bytes 24580
  240.0 38.2 %all-to-all-start.1 = ((f32[32,192,8]{1,2,0:T(8,128)}), f32[32,192,8]{1,2,0:T(8,128)S(1)}, u32[]{:S(2)}, u32[]{:S(2)}) async-start(f32[32,192,8]{1,2,0:T(8,128)} %copy.36), calls=%async_computation.1 | async-start | bytes 524288 | tf_op jit(solution)/shard_map/all_to_all | solution.py:280
  284.9 11.1 %copy-start.2 = (f32[2048,8]{1,0:T(8,128)S(1)}, f32[2048,8]{1,0:T(8,128)}, u32[]{:S(2)}) copy-start(f32[2048,8]{1,0:T(8,128)} %shard_map.140) | copy-start | bytes 196612
  286.5 9.2 %collective-permute-start.4 = (f32[8,2048]{1,0:T(8,128)S(1)}, f32[8,2048]{1,0:T(8,128)S(1)}, u32[]{:S(2)}, u32[]{:S(2)}) collective-permute-start(f32[8,2048]{1,0:T(8,128)S(1)} %copy.38), channel_id=1, source_target_pairs={{0,32},{32,0},{64,96},{96,64},{128,160},{160,128},{192,224},{224,1... | collective-permute-start | bytes 196616 | tf_op jit(solution)/shard_map/ppermute | solution.py:35
  296.5 7.7 %collective-permute-start.5 = (f32[8,2048]{1,0:T(8,128)S(1)}, f32[8,2048]{1,0:T(8,128)S(1)}, u32[]{:S(2)}, u32[]{:S(2)}) collective-permute-start(f32[8,2048]{1,0:T(8,128)S(1)} %copy.40), channel_id=1, source_target_pairs={{0,64},{32,96},{64,0},{96,32},{128,192},{160,224},{192,128},{224,1... | collective-permute-start | bytes 196616 | tf_op jit(solution)/shard_map/ppermute | solution.py:35
  304.9 6.2 %collective-permute-start.6 = (f32[8,2048]{1,0:T(8,128)S(1)}, f32[8,2048]{1,0:T(8,128)S(1)}, u32[]{:S(2)}, u32[]{:S(2)}) collective-permute-start(f32[8,2048]{1,0:T(8,128)S(1)} %copy.42), channel_id=1, source_target_pairs={{0,128},{32,160},{64,192},{96,224},{128,0},{160,32},{192,64},{224,... | collective-permute-start | bytes 196616 | tf_op jit(solution)/shard_map/ppermute | solution.py:35
  311.8 7.7 %collective-permute-start.7 = (f32[8,2048]{1,0:T(8,128)S(1)}, f32[8,2048]{1,0:T(8,128)S(1)}, u32[]{:S(2)}, u32[]{:S(2)}) collective-permute-start(f32[8,2048]{1,0:T(8,128)S(1)} %copy.44), channel_id=1, source_target_pairs={{0,256},{32,288},{64,320},{96,352},{128,384},{160,416},{192,448},{... | collective-permute-start | bytes 196616 | tf_op jit(solution)/shard_map/ppermute | solution.py:35

commit v8 on v6

--- a/solution.py
+++ b/solution.py
@@ -43,22 +43,37 @@
     downward = block_tiles[halo_list[0]].reshape(-1, channels)
     from_below = passed_along(upward, "slab", 1)
     from_above = passed_along(downward, "slab", -1)
-    rows = features.shape[0] + from_below.shape[0] + from_above.shape[0] + 1
-    padding = -rows % 8 + 1
-    blank_rows = jnp.zeros((padding, channels), features.dtype)
-    extended = jnp.concatenate([features, from_below, from_above, blank_rows], axis=0)
-    return extended.astype(jnp.float32)
-
-
-def conv_kernel(active_ref, nbr_ref, ext_ref, w_ref, scale_ref, shift_ref, *rest, has_residual):
+    return features, from_below, from_above
+
+
+def conv_kernel(
+    active_ref, nbr_ref, own_ref, below_ref, above_ref, w_ref, scale_ref, shift_ref, *rest,
+    has_residual
+):
     if has_residual:
-        res_ref, out_ref, gathered_ref = rest
+        res_ref, out_ref, gathered_ref, ext_ref = rest
     else:
-        out_ref, gathered_ref = rest
+        out_ref, gathered_ref, ext_ref = rest
     rows = out_ref.shape[0]
     channels = ext_ref.shape[1]
+    width_in = own_ref.shape[1]
     first = pl.multiple_of(pl.program_id(0) * rows, rows)
     active = active_ref[0]
+
+    @pl.when(pl.program_id(0) == 0)
+    def _():
+        own_rows = own_ref.shape[0]
+        halo_rows = below_ref.shape[0]
+        if width_in != channels:
+            ext_ref[...] = jnp.zeros(ext_ref.shape, ext_ref.dtype)
+        else:
+            tail = own_rows + 2 * halo_rows
+            ext_ref[tail:, :] = jnp.zeros((ext_ref.shape[0] - tail, channels), ext_ref.dtype)
+        ext_ref[:own_rows, :width_in] = own_ref[...].astype(jnp.float32)
+        ext_ref[own_rows : own_rows + halo_rows, :width_in] = below_ref[...].astype(jnp.float32)
+        ext_ref[own_rows + halo_rows : own_rows + 2 * halo_rows, :width_in] = above_ref[
+            ...
+        ].astype(jnp.float32)
 
     @pl.when(first < active)
     def _():
@@ -89,7 +104,7 @@
         out_ref[...] = jnp.zeros(out_ref.shape, out_ref.dtype)
 
 
-def convolve(extended, neighbor_table, weight, scale_vec, shift_vec, residual, active_rows):
+def convolve(pieces, neighbor_table, weight, scale_vec, shift_vec, residual, active_rows):
     total = neighbor_table.shape[1]
     steps = total // CONV_ROWS
     per_step = OFFSETS * CONV_ROWS
@@ -98,10 +113,11 @@
         neighbor_table.reshape(OFFSETS, steps, CONV_ROWS).transpose(1, 0, 2).reshape(steps, -1),
         ((0, 0), (0, step_block - per_step)),
     ).reshape(-1)
-    ext_rows, width_in = extended.shape
+    own, below, above = pieces
+    width_in = own.shape[1]
+    ext_rows = -(own.shape[0] + below.shape[0] + above.shape[0] + 1) // 8 * -8
     channels = -width_in // 128 * -128
     width = weight.shape[2]
-    extended = jnp.pad(extended, ((0, 0), (0, channels - width_in)))
     weight_flat = jnp.pad(weight, ((0, 0), (0, channels - width_in), (0, 0))).reshape(-1, width)
     in_specs = [
         pl.BlockSpec(
@@ -110,14 +126,18 @@
             memory_space=pltpu.SMEM,
             pipeline_mode=pl.Buffered(1),
         ),
-        pl.BlockSpec((ext_rows, channels), lambda s, a: (0, 0)),
+        pl.BlockSpec(own.shape, lambda s, a: (0, 0)),
+        pl.BlockSpec(below.shape, lambda s, a: (0, 0)),
+        pl.BlockSpec(above.shape, lambda s, a: (0, 0)),
         pl.BlockSpec(weight_flat.shape, lambda s, a: (0, 0)),
         pl.BlockSpec((1, width), lambda s, a: (0, 0)),
         pl.BlockSpec((1, width), lambda s, a: (0, 0)),
     ]
     operands = [
         neighbor_steps,
-        extended,
+        own,
+        below,
+        above,
         weight_flat,
         scale_vec.reshape(1, width),
         shift_vec.reshape(1, width),
@@ -130,7 +150,10 @@
         grid=(steps,),
         in_specs=in_specs,
         out_specs=pl.BlockSpec((CONV_ROWS, width), lambda s, a: (s, 0)),
-        scratch_shapes=[pltpu.VMEM((CONV_ROWS, OFFSETS * channels), jnp.float32)],
+        scratch_shapes=[
+            pltpu.VMEM((CONV_ROWS, OFFSETS * channels), jnp.float32),
+            pltpu.VMEM((ext_rows, channels), jnp.float32),
+        ],
     )
     return pl.pallas_call(
         functools.partial(conv_kernel, has_residual=residual is not None),

time: 324 us -> 321 us (level)
  starting transfers between devices: 63.6 us -> 99.8 us
  Pallas kernels: 92.2 us -> 62.9 us
  waiting for transfers between devices: 113 us -> 108 us
  other arithmetic: 14.2 us -> 10.1 us
    all_to_all x1, starting transfers between devices: 20.1 us -> 53.7 us  [per_device(): returned = lax.all_to_all(slot_logits, 'slab', 0, 0, tiled=True)]
    pallas_call x2, Pallas kernels: 69.5 us -> 40.2 us  [convolve(): pl.pallas_call(functools.partial(conv_kernel, has_residual=residual is no...]
    ppermute x4, waiting for transfers between devices: 16.7 us -> 1.83 us  [passed_along(): return lax.ppermute(shard, axis, pairs)]
    ppermute x4, starting transfers between devices: 8.2 us -> 22.7 us  [passed_along(): return lax.ppermute(shard, axis, pairs)]
    ppermute x4, starting transfers between devices: 19.7 us -> 7.68 us  [all_summed(): values = values + lax.ppermute(values, axis, pairs)]
    ppermute x4, waiting for transfers between devices: 10.8 us -> 19.9 us  [all_summed(): values = values + lax.ppermute(values, axis, pairs)]
where the time goes in v8:
time: 321 us; the launch traced here: 318 us
  waiting for transfers between devices  108 us (34%)
  starting transfers between devices  99.8 us (31%)
  Pallas kernels  62.9 us (20%)
  local copies, waits for them, and re-layouts  33.8 us (11%)
  other arithmetic  10.1 us (3%)
  matrix products  3.27 us (1%)
    all_to_all x1, waiting for transfers between devices, per_device(): lax.all_to_all(packed.reshape(slab_count, dense // 128, 128), 'slab', 0,...  63.6 us
    all_to_all x1, starting transfers between devices, per_device(): returned = lax.all_to_all(slot_logits, 'slab', 0, 0, tiled=True)  53.7 us
    pallas_call x2, Pallas kernels, convolve(): pl.pallas_call(functools.partial(conv_kernel, has_residual=residual is no...  40.2 us
    ppermute x4, starting transfers between devices, passed_along(): return lax.ppermute(shard, axis, pairs)  22.7 us
    all_to_all x1, waiting for transfers between devices, per_device(): returned = lax.all_to_all(slot_logits, 'slab', 0, 0, tiled=True)  22.1 us
    ppermute x4, waiting for transfers between devices, all_summed(): values = values + lax.ppermute(values, axis, pairs)  19.9 us
    all_to_all x1, starting transfers between devices, per_device(): lax.all_to_all(packed.reshape(slab_count, dense // 128, 128), 'slab', 0,...  15.6 us
    pallas_call x2, Pallas kernels, gather_rows(): pl.pallas_call(gather_kernel, in_specs=[pl.BlockSpec(memory_space=pltpu.S...  12.8 us
  transfers between devices with their start and end apart: 10, of which 7 were waited for; matrix products, arithmetic and copies ran while one was open for 1% of the time, Pallas kernels for 0%

profile of v8, /device:TPU:24, one launch (start us, length us, event | category | flops | bytes accessed | tf_op | source)
XLA Modules:
  0.0 318.5 jit_solution(15725068506951140620)
XLA Ops:
  0.0 0.9 convert_reduce_fusion
  0.9 1.0 fusion.2
  1.9 0.7 compare_select_fusion
  2.6 0.7 fusion.12
  3.5 1.1 maximum_maximum_fusion
  4.6 0.3 copy.33
  4.9 6.3 %scatter_custom_fusion = bf16[6144,99]{1,0:T(8,128)(2,1)S(1)} fusion(s32[2048]{0:T(1024)S(1)} %bitcast.102, bf16[2048,99]{1,0:T(8,128)(2,1)S(1)} %copy.33, bf16[]{:T(256)} %constant.43.clone.1), kind=kCustom, calls=%fused_computation.17 | custom fusion | bytes 1216514 | tf_op jit(solution)/shard_map/scatter | solution.py:257
  11.2 1.9 reshape.351
  13.2 0.1 pad.13
  13.2 1.5 reshape.352
  14.7 15.6 %all-to-all-start = ((bf16[32,149,128]{2,1,0:T(8,128)(2,1)}), bf16[32,149,128]{2,1,0:T(8,128)(2,1)S(1)}, u32[]{:S(2)}, u32[]{:S(2)}) async-start(bf16[32,149,128]{2,1,0:T(8,128)(2,1)} %reshape.352), calls=%async_computation | async-start | bytes 2490368 | tf_op jit(solution)/shard_map/all_to_all | solution.py:262
  30.4 0.5 reduce.2
  30.9 0.1 copy.49
  31.1 63.6 %all-to-all-done = bf16[32,149,128]{2,1,0:T(8,128)(2,1)S(1)} async-done(((bf16[32,149,128]{2,1,0:T(8,128)(2,1)}), bf16[32,149,128]{2,1,0:T(8,128)(2,1)S(1)}, u32[]{:S(2)}, u32[]{:S(2)}) %all-to-all-start) | async-done | bytes 1220640 | tf_op jit(solution)/shard_map/all_to_all | solution.py:262
  94.7 0.2 copy.52
  94.9 5.8 %reshape.354.feats_ref = bf16[6144,99]{1,0:T(8,128)(2,1)S(1)} reshape(bf16[32,19008]{1,0:T(8,128)(2,1)S(1)} %bitcast.83) | data formatting | bytes 2433024 | tf_op jit(solution)/shard_map/reshape | solution.py:265
  100.7 2.7 add_reduce_fusion.index_ref
  103.4 9.9 %shard_map.136 = f32[2048,99]{1,0:T(8,128)} custom-call(s32[1,6144]{1,0:T(1,128)} %bitcast.93, bf16[6144,99]{1,0:T(8,128)(2,1)} %copy-done.1), custom_call_target="tpu_custom_call" | custom-call | tf_op jit(solution)/shard_map/pallas_call | solution.py:180
  113.3 1.9 fusion.3
  115.3 0.3 fusion.4.own_ref
  115.6 0.6 gather_fusion.1
  116.2 0.6 gather_fusion
  116.8 1.9 collective-permute-start
  118.7 1.5 collective-permute-start.1
  120.8 0.8 copy.50
  121.6 1.1 pad.15
  122.7 0.6 copy-done.8
  123.3 20.1 %shard_map.137.own_ref.rest_0_ = bf16[2048,128]{1,0:T(8,128)(2,1)} custom-call(s32[1]{0:T(128)} %bitcast.9.active_ref, s32[57344]{0:T(1024)} %bitcast.87, bf16[2048,96]{1,0:T(8,128)(2,1)} %copy-done.4, bf16[256,96]{1,0:T(8,128)(2,1)} %copy-done.8, bf16[256,96]{1,0:T(8,128)(2,1)} %copy-done.9, bf16[3456,128]{1,0:T(8,128)(2,1)} %bitcast.84, ...), custom_call_target="tpu_custom_call" | custom-call | tf_op jit(solution)/shard_map/pallas_call | solution.py:158
  143.4 1.6 gather_fusion.3
  145.0 1.6 gather_fusion.2
  146.6 18.1 %collective-permute-start.2 = (bf16[256,128]{1,0:T(8,128)(2,1)S(1)}, bf16[256,128]{1,0:T(8,128)(2,1)S(1)}, u32[]{:S(2)}, u32[]{:S(2)}) collective-permute-start(bf16[256,128]{1,0:T(8,128)(2,1)S(1)} %bitcast.99), channel_id=1, source_target_pairs={{0,1},{1,2},{2,3},{3,4},{4,5},{5,6},{6,7},{7,8},{8,9},{9,10},{10,1... | collective-permute-start | bytes 196616 | tf_op jit(solution)/shard_map/ppermute | solution.py:24
  164.7 1.3 collective-permute-start.3
  166.0 1.8 collective-permute-done.3.above_ref
  167.9 0.6 copy-done.11
  168.5 20.1 %shard_map.138 = bf16[2048,128]{1,0:T(8,128)(2,1)} custom-call(s32[1]{0:T(128)} %bitcast.9.active_ref, s32[57344]{0:T(1024)} %bitcast.88, bf16[2048,128]{1,0:T(8,128)(2,1)} %shard_map.137.own_ref.rest_0_, bf16[256,128]{1,0:T(8,128)(2,1)} %copy-done.10, bf16[256,128]{1,0:T(8,128)(2,1)} %copy-done.11, bf16[3456,128]{1,0:T(8,128)(2,1)} %bitcast.91, ...), custom_call_target="tpu_custom_call" | custom-call | tf_op jit(solution)/shard_map/pallas_call | solution.py:158
  188.6 2.3 convolution_add_fusion.table_ref
  190.9 8.2 %shard_map.139 = f32[6144,8]{1,0:T(8,128)} custom-call(s32[6144]{0:T(1024)} %add_reduce_fusion.index_ref, f32[2048,8]{1,0:T(8,128)} %convolution_add_fusion.table_ref), custom_call_target="tpu_custom_call" | custom-call | tf_op jit(solution)/shard_map/pallas_call | solution.py:201
  199.0 3.2 %copy.36 = f32[32,192,8]{1,2,0:T(8,128)} copy(f32[32,192,8]{2,1,0:T(8,128)} %bitcast.77) | data formatting | bytes 393216 | tf_op jit(solution)/shard_map/reshape | solution.py:296
  202.3 53.7 %all-to-all-start.1 = ((f32[32,192,8]{1,2,0:T(8,128)}), f32[32,192,8]{1,2,0:T(8,128)S(1)}, u32[]{:S(2)}, u32[]{:S(2)}) async-start(f32[32,192,8]{1,2,0:T(8,128)} %copy.36), calls=%async_computation.1 | async-start | bytes 524288 | tf_op jit(solution)/shard_map/all_to_all | solution.py:297
  256.0 0.6 bitcast_add_fusion.1.index_ref
  256.6 22.1 %all-to-all-done.1 = f32[32,192,8]{1,2,0:T(8,128)S(1)} async-done(((f32[32,192,8]{1,2,0:T(8,128)}), f32[32,192,8]{1,2,0:T(8,128)S(1)}, u32[]{:S(2)}, u32[]{:S(2)}) %all-to-all-start.1) | async-done | bytes 196640 | tf_op jit(solution)/shard_map/all_to_all | solution.py:297
  278.8 2.2 copy.37
  280.9 4.6 %shard_map.140 = f32[2048,8]{1,0:T(8,128)} custom-call(s32[2048]{0:T(1024)} %bitcast_add_fusion.1.index_ref, f32[6144,8]{1,0:T(8,128)} %bitcast.78), custom_call_target="tpu_custom_call" | custom-call | tf_op jit(solution)/shard_map/pallas_call | solution.py:201
  285.6 1.6 copy.38
  287.2 1.9 collective-permute-start.4
  289.1 4.2 %collective-permute-done.4 = f32[8,2048]{1,0:T(8,128)S(1)} collective-permute-done((f32[8,2048]{1,0:T(8,128)S(1)}, f32[8,2048]{1,0:T(8,128)S(1)}, u32[]{:S(2)}, u32[]{:S(2)}) %collective-permute-start.4) | collective-permute-done | bytes 65568 | tf_op jit(solution)/shard_map/ppermute | solution.py:34
  293.4 0.3 copy.39
  293.7 0.1 bitcast_add_fusion.2
  293.8 0.3 copy.40
  294.1 1.9 collective-permute-start.5
  296.0 5.7 %collective-permute-done.5 = f32[8,2048]{1,0:T(8,128)S(1)} collective-permute-done((f32[8,2048]{1,0:T(8,128)S(1)}, f32[8,2048]{1,0:T(8,128)S(1)}, u32[]{:S(2)}, u32[]{:S(2)}) %collective-permute-start.5) | collective-permute-done | bytes 65568 | tf_op jit(solution)/shard_map/ppermute | solution.py:34
  301.8 0.3 copy.41
  302.1 0.1 add.121
  302.2 0.3 copy.42
  302.5 1.9 collective-permute-start.6
  304.5 4.2 %collective-permute-done.6 = f32[8,2048]{1,0:T(8,128)S(1)} collective-permute-done((f32[8,2048]{1,0:T(8,128)S(1)}, f32[8,2048]{1,0:T(8,128)S(1)}, u32[]{:S(2)}, u32[]{:S(2)}) %collective-permute-start.6) | collective-permute-done | bytes 65568 | tf_op jit(solution)/shard_map/ppermute | solution.py:34
  308.7 0.3 copy.43
  309.0 0.1 add.122
  309.1 0.3 copy.44
  309.4 1.9 collective-permute-start.7
  311.4 5.7 %collective-permute-done.7 = f32[8,2048]{1,0:T(8,128)S(1)} collective-permute-done((f32[8,2048]{1,0:T(8,128)S(1)}, f32[8,2048]{1,0:T(8,128)S(1)}, u32[]{:S(2)}, u32[]{:S(2)}) %collective-permute-start.7) | collective-permute-done | bytes 65568 | tf_op jit(solution)/shard_map/ppermute | solution.py:34
  317.1 0.3 copy.45
  317.4 0.1 add_multiply_fusion
  317.6 0.9 copy.46
  (40 shorter events, 0.3 us)
Async XLA Ops:
  0.0 188.6 %copy-start = (bf16[128,8]{0,1:T(8,128)(2,1)S(1)}, bf16[128,8]{0,1:T(8,128)(2,1)}, u32[]{:S(2)}) copy-start(bf16[128,8]{0,1:T(8,128)(2,1)} %param.26) | copy-start | bytes 6148
  14.7 15.6 %copy-start.6 = (s32[1,27,2048]{2,0,1:T(1,128)S(1)}, s32[1,27,2048]{2,0,1:T(1,128)}, u32[]{:S(2)}) copy-start(s32[1,27,2048]{2,0,1:T(1,128)} %param.19) | copy-start | bytes 663556
  14.7 16.3 %copy-start.12 = (s32[1,1,2,2]{3,2,1,0:T(2,128)S(1)}, s32[1,1,2,2]{3,2,1,0:T(2,128)}, u32[]{:S(2)}) copy-start(s32[1,1,2,2]{3,2,1,0:T(2,128)} %param.18) | copy-start | bytes 52
  14.7 80.0 %all-to-all-start = ((bf16[32,149,128]{2,1,0:T(8,128)(2,1)}), bf16[32,149,128]{2,1,0:T(8,128)(2,1)S(1)}, u32[]{:S(2)}, u32[]{:S(2)}) async-start(bf16[32,149,128]{2,1,0:T(8,128)(2,1)} %reshape.352), calls=%async_computation | async-start | bytes 2490368 | tf_op jit(solution)/shard_map/all_to_all | solution.py:262
  100.7 2.7 copy-start.1
  113.3 2.0 copy-start.3
  115.3 6.3 %copy-start.5 = (bf16[27,96,128]{2,1,0:T(8,128)(2,1)S(1)}, bf16[27,96,128]{2,1,0:T(8,128)(2,1)}, u32[]{:S(2)}) copy-start(bf16[27,96,128]{2,1,0:T(8,128)(2,1)} %param.20) | copy-start | bytes 1990660
  115.6 7.1 %copy-start.4 = (bf16[2048,96]{1,0:T(8,128)(2,1)}, bf16[2048,96]{1,0:T(8,128)(2,1)S(1)}, u32[]{:S(2)}) copy-start(bf16[2048,96]{1,0:T(8,128)(2,1)S(1)} %fusion.4.own_ref) | copy-start | bytes 1179652
  116.8 5.9 %collective-permute-start = (bf16[256,96]{1,0:T(8,128)(2,1)S(1)}, bf16[256,96]{1,0:T(8,128)(2,1)S(1)}, u32[]{:S(2)}, u32[]{:S(2)}) collective-permute-start(bf16[256,96]{1,0:T(8,128)(2,1)S(1)} %bitcast.97), channel_id=1, source_target_pairs={{0,1},{1,2},{2,3},{3,4},{4,5},{5,6},{6,7},{7,8},{8,9},{9,10},{10,1... | collective-permute-start | bytes 147464 | tf_op jit(solution)/shard_map/ppermute | solution.py:24
  118.7 4.0 %collective-permute-start.1 = (bf16[256,96]{1,0:T(8,128)(2,1)S(1)}, bf16[256,96]{1,0:T(8,128)(2,1)S(1)}, u32[]{:S(2)}, u32[]{:S(2)}) collective-permute-start(bf16[256,96]{1,0:T(8,128)(2,1)S(1)} %bitcast.96), channel_id=1, source_target_pairs={{1,0},{2,1},{3,2},{4,3},{5,4},{6,5},{7,6},{8,7},{9,8},{10,9},{11,1... | collective-permute-start | bytes 147464 | tf_op jit(solution)/shard_map/ppermute | solution.py:24
  122.7 0.6 copy-start.8
  122.7 0.6 copy-start.9
  143.4 45.2 %copy-start.13 = (f32[8]{0:T(128)S(1)}, f32[8]{0:T(128)}, u32[]{:S(2)}) copy-start(f32[8]{0:T(128)} %param.27) | copy-start | bytes 100
  146.6 19.4 %collective-permute-start.2 = (bf16[256,128]{1,0:T(8,128)(2,1)S(1)}, bf16[256,128]{1,0:T(8,128)(2,1)S(1)}, u32[]{:S(2)}, u32[]{:S(2)}) collective-permute-start(bf16[256,128]{1,0:T(8,128)(2,1)S(1)} %bitcast.99), channel_id=1, source_target_pairs={{0,1},{1,2},{2,3},{3,4},{4,5},{5,6},{6,7},{7,8},{8,9},{9,10},{10,1... | collective-permute-start | bytes 196616 | tf_op jit(solution)/shard_map/ppermute | solution.py:24
  164.7 3.1 collective-permute-start.3
  166.0 1.8 copy-start.10
  167.9 0.6 copy-start.11
  199.0 57.0 %copy-start.7 = (s32[1,2048]{1,0:T(1,128)S(1)}, s32[1,2048]{1,0:T(1,128)}, u32[]{:S(2)}) copy-start(s32[1,2048]{1,0:T(1,128)} %param.15) | copy-start | bytes 24580
  202.3 76.5 %all-to-all-start.1 = ((f32[32,192,8]{1,2,0:T(8,128)}), f32[32,192,8]{1,2,0:T(8,128)S(1)}, u32[]{:S(2)}, u32[]{:S(2)}) async-start(f32[32,192,8]{1,2,0:T(8,128)} %copy.36), calls=%async_computation.1 | async-start | bytes 524288 | tf_op jit(solution)/shard_map/all_to_all | solution.py:297
  285.6 8.1 %copy-start.2 = (f32[2048,8]{1,0:T(8,128)S(1)}, f32[2048,8]{1,0:T(8,128)}, u32[]{:S(2)}) copy-start(f32[2048,8]{1,0:T(8,128)} %shard_map.140) | copy-start | bytes 196612
  287.2 6.2 %collective-permute-start.4 = (f32[8,2048]{1,0:T(8,128)S(1)}, f32[8,2048]{1,0:T(8,128)S(1)}, u32[]{:S(2)}, u32[]{:S(2)}) collective-permute-start(f32[8,2048]{1,0:T(8,128)S(1)} %copy.38), channel_id=1, source_target_pairs={{0,32},{32,0},{64,96},{96,64},{128,160},{160,128},{192,224},{224,1... | collective-permute-start | bytes 196616 | tf_op jit(solution)/shard_map/ppermute | solution.py:34
  294.1 7.7 %collective-permute-start.5 = (f32[8,2048]{1,0:T(8,128)S(1)}, f32[8,2048]{1,0:T(8,128)S(1)}, u32[]{:S(2)}, u32[]{:S(2)}) collective-permute-start(f32[8,2048]{1,0:T(8,128)S(1)} %copy.40), channel_id=1, source_target_pairs={{0,64},{32,96},{64,0},{96,32},{128,192},{160,224},{192,128},{224,1... | collective-permute-start | bytes 196616 | tf_op jit(solution)/shard_map/ppermute | solution.py:34
  302.5 6.2 %collective-permute-start.6 = (f32[8,2048]{1,0:T(8,128)S(1)}, f32[8,2048]{1,0:T(8,128)S(1)}, u32[]{:S(2)}, u32[]{:S(2)}) collective-permute-start(f32[8,2048]{1,0:T(8,128)S(1)} %copy.42), channel_id=1, source_target_pairs={{0,128},{32,160},{64,192},{96,224},{128,0},{160,32},{192,64},{224,... | collective-permute-start | bytes 196616 | tf_op jit(solution)/shard_map/ppermute | solution.py:34
  309.4 7.7 %collective-permute-start.7 = (f32[8,2048]{1,0:T(8,128)S(1)}, f32[8,2048]{1,0:T(8,128)S(1)}, u32[]{:S(2)}, u32[]{:S(2)}) collective-permute-start(f32[8,2048]{1,0:T(8,128)S(1)} %copy.44), channel_id=1, source_target_pairs={{0,256},{32,288},{64,320},{96,352},{128,384},{160,416},{192,448},{... | collective-permute-start | bytes 196616 | tf_op jit(solution)/shard_map/ppermute | solution.py:34

commit v9 on v8

--- a/solution.py
+++ b/solution.py
@@ -12,7 +12,7 @@
 CENTRE = 13
 UNROLL = 32
 CONV_ROWS = 256
-POOL_ROWS = 256
+POOL_ROWS = 512
 POOL_COLS = 512
 DIGIT = 64
 RANK_BLOCK = 128

time: 321 us -> 320 us (level)
  Pallas kernels: 62.9 us -> 81.8 us
  starting transfers between devices: 99.8 us -> 86.9 us
  waiting for transfers between devices: 108 us -> 98.8 us
    pallas_call x2, Pallas kernels: 40.2 us -> 59.7 us  [convolve(): pl.pallas_call(functools.partial(conv_kernel, has_residual=residual is no...]
    ppermute x4, starting transfers between devices: 22.7 us -> 5.79 us  [passed_along(): return lax.ppermute(shard, axis, pairs)]
    ppermute x4, starting transfers between devices: 7.68 us -> 18.7 us  [all_summed(): values = values + lax.ppermute(values, axis, pairs)]
    ppermute x4, waiting for transfers between devices: 19.9 us -> 11.2 us  [all_summed(): values = values + lax.ppermute(values, axis, pairs)]
    all_to_all x1, starting transfers between devices: 53.7 us -> 46.7 us  [per_device(): returned = lax.all_to_all(slot_logits, 'slab', 0, 0, tiled=True)]
where the time goes in v9:
time: 320 us; the launch traced here: 316 us
  waiting for transfers between devices  98.8 us (31%)
  starting transfers between devices  86.9 us (27%)
  Pallas kernels  81.8 us (26%)
  local copies, waits for them, and re-layouts  33.8 us (11%)
  other arithmetic  10.1 us (3%)
  matrix products  3.27 us (1%)
    all_to_all x1, waiting for transfers between devices, per_device(): lax.all_to_all(packed.reshape(slab_count, dense // 128, 128), 'slab', 0,...  63.6 us
    pallas_call x2, Pallas kernels, convolve(): pl.pallas_call(functools.partial(conv_kernel, has_residual=residual is no...  59.7 us
    all_to_all x1, starting transfers between devices, per_device(): returned = lax.all_to_all(slot_logits, 'slab', 0, 0, tiled=True)  46.7 us
    all_to_all x1, waiting for transfers between devices, per_device(): returned = lax.all_to_all(slot_logits, 'slab', 0, 0, tiled=True)  22.1 us
    ppermute x4, starting transfers between devices, all_summed(): values = values + lax.ppermute(values, axis, pairs)  18.7 us
    all_to_all x1, starting transfers between devices, per_device(): lax.all_to_all(packed.reshape(slab_count, dense // 128, 128), 'slab', 0,...  15.6 us
    pallas_call x2, Pallas kernels, gather_rows(): pl.pallas_call(gather_kernel, in_specs=[pl.BlockSpec(memory_space=pltpu.S...  12.8 us
    ppermute x4, waiting for transfers between devices, all_summed(): values = values + lax.ppermute(values, axis, pairs)  11.2 us
  transfers between devices with their start and end apart: 10, of which 7 were waited for; matrix products, arithmetic and copies ran while one was open for 1% of the time, Pallas kernels for 0%

profile of v9, /device:TPU:24, one launch (start us, length us, event | category | flops | bytes accessed | tf_op | source)
XLA Modules:
  0.0 315.7 jit_solution(6780575357977262666)
XLA Ops:
  0.0 0.9 convert_reduce_fusion
  0.9 1.0 fusion.2
  1.9 0.7 compare_select_fusion
  2.6 0.7 fusion.12
  3.5 1.1 maximum_maximum_fusion
  4.6 0.3 copy.33
  4.9 6.3 %scatter_custom_fusion = bf16[6144,99]{1,0:T(8,128)(2,1)S(1)} fusion(s32[2048]{0:T(1024)S(1)} %bitcast.102, bf16[2048,99]{1,0:T(8,128)(2,1)S(1)} %copy.33, bf16[]{:T(256)} %constant.43.clone.1), kind=kCustom, calls=%fused_computation.17 | custom fusion | bytes 1216514 | tf_op jit(solution)/shard_map/scatter | solution.py:257
  11.2 1.9 reshape.351
  13.2 0.1 pad.13
  13.2 1.5 reshape.352
  14.7 15.6 %all-to-all-start = ((bf16[32,149,128]{2,1,0:T(8,128)(2,1)}), bf16[32,149,128]{2,1,0:T(8,128)(2,1)S(1)}, u32[]{:S(2)}, u32[]{:S(2)}) async-start(bf16[32,149,128]{2,1,0:T(8,128)(2,1)} %reshape.352), calls=%async_computation | async-start | bytes 2490368 | tf_op jit(solution)/shard_map/all_to_all | solution.py:262
  30.4 0.5 reduce.2
  30.9 0.1 copy.49
  31.1 63.6 %all-to-all-done = bf16[32,149,128]{2,1,0:T(8,128)(2,1)S(1)} async-done(((bf16[32,149,128]{2,1,0:T(8,128)(2,1)}), bf16[32,149,128]{2,1,0:T(8,128)(2,1)S(1)}, u32[]{:S(2)}, u32[]{:S(2)}) %all-to-all-start) | async-done | bytes 1220640 | tf_op jit(solution)/shard_map/all_to_all | solution.py:262
  94.7 0.2 copy.52
  94.9 5.8 %reshape.354.feats_ref = bf16[6144,99]{1,0:T(8,128)(2,1)S(1)} reshape(bf16[32,19008]{1,0:T(8,128)(2,1)S(1)} %bitcast.83) | data formatting | bytes 2433024 | tf_op jit(solution)/shard_map/reshape | solution.py:265
  100.7 2.7 add_reduce_fusion.index_ref
  103.4 9.3 %shard_map.136 = f32[2048,99]{1,0:T(8,128)} custom-call(s32[1,6144]{1,0:T(1,128)} %bitcast.93, bf16[6144,99]{1,0:T(8,128)(2,1)} %copy-done.1), custom_call_target="tpu_custom_call" | custom-call | tf_op jit(solution)/shard_map/pallas_call | solution.py:180
  112.7 1.9 fusion.3
  114.6 0.3 fusion.4.own_ref
  115.0 0.6 gather_fusion.1
  115.6 0.6 gather_fusion
  116.1 1.9 collective-permute-start
  118.1 1.3 collective-permute-start.1
  120.0 0.8 copy.50
  120.8 1.1 pad.15
  121.9 0.6 copy-done.8
  122.5 29.8 %shard_map.137.own_ref.rest_0_ = bf16[2048,128]{1,0:T(8,128)(2,1)} custom-call(s32[1]{0:T(128)} %bitcast.9.active_ref, s32[57344]{0:T(1024)} %bitcast.87, bf16[2048,96]{1,0:T(8,128)(2,1)} %copy-done.4, bf16[256,96]{1,0:T(8,128)(2,1)} %copy-done.8, bf16[256,96]{1,0:T(8,128)(2,1)} %copy-done.9, bf16[3456,128]{1,0:T(8,128)(2,1)} %bitcast.84, ...), custom_call_target="tpu_custom_call" | custom-call | tf_op jit(solution)/shard_map/pallas_call | solution.py:158
  152.3 1.6 gather_fusion.3
  154.0 1.6 gather_fusion.2
  155.6 1.3 collective-permute-start.2
  156.9 1.3 collective-permute-start.3
  158.2 1.8 collective-permute-done.3.above_ref
  160.0 0.6 copy-done.11
  160.6 29.8 %shard_map.138 = bf16[2048,128]{1,0:T(8,128)(2,1)} custom-call(s32[1]{0:T(128)} %bitcast.9.active_ref, s32[57344]{0:T(1024)} %bitcast.88, bf16[2048,128]{1,0:T(8,128)(2,1)} %shard_map.137.own_ref.rest_0_, bf16[256,128]{1,0:T(8,128)(2,1)} %copy-done.10, bf16[256,128]{1,0:T(8,128)(2,1)} %copy-done.11, bf16[3456,128]{1,0:T(8,128)(2,1)} %bitcast.91, ...), custom_call_target="tpu_custom_call" | custom-call | tf_op jit(solution)/shard_map/pallas_call | solution.py:158
  190.5 2.3 convolution_add_fusion.table_ref
  192.8 8.2 %shard_map.139 = f32[6144,8]{1,0:T(8,128)} custom-call(s32[6144]{0:T(1024)} %add_reduce_fusion.index_ref, f32[2048,8]{1,0:T(8,128)} %convolution_add_fusion.table_ref), custom_call_target="tpu_custom_call" | custom-call | tf_op jit(solution)/shard_map/pallas_call | solution.py:201
  200.9 3.2 %copy.36 = f32[32,192,8]{1,2,0:T(8,128)} copy(f32[32,192,8]{2,1,0:T(8,128)} %bitcast.77) | data formatting | bytes 393216 | tf_op jit(solution)/shard_map/reshape | solution.py:296
  204.2 46.7 %all-to-all-start.1 = ((f32[32,192,8]{1,2,0:T(8,128)}), f32[32,192,8]{1,2,0:T(8,128)S(1)}, u32[]{:S(2)}, u32[]{:S(2)}) async-start(f32[32,192,8]{1,2,0:T(8,128)} %copy.36), calls=%async_computation.1 | async-start | bytes 524288 | tf_op jit(solution)/shard_map/all_to_all | solution.py:297
  251.0 0.6 bitcast_add_fusion.1.index_ref
  251.6 22.1 %all-to-all-done.1 = f32[32,192,8]{1,2,0:T(8,128)S(1)} async-done(((f32[32,192,8]{1,2,0:T(8,128)}), f32[32,192,8]{1,2,0:T(8,128)S(1)}, u32[]{:S(2)}, u32[]{:S(2)}) %all-to-all-start.1) | async-done | bytes 196640 | tf_op jit(solution)/shard_map/all_to_all | solution.py:297
  273.7 2.2 copy.37
  275.9 4.6 %shard_map.140 = f32[2048,8]{1,0:T(8,128)} custom-call(s32[2048]{0:T(1024)} %bitcast_add_fusion.1.index_ref, f32[6144,8]{1,0:T(8,128)} %bitcast.78), custom_call_target="tpu_custom_call" | custom-call | tf_op jit(solution)/shard_map/pallas_call | solution.py:201
  280.5 1.6 copy.38
  282.1 3.5 %collective-permute-start.4 = (f32[8,2048]{1,0:T(8,128)S(1)}, f32[8,2048]{1,0:T(8,128)S(1)}, u32[]{:S(2)}, u32[]{:S(2)}) collective-permute-start(f32[8,2048]{1,0:T(8,128)S(1)} %copy.38), channel_id=1, source_target_pairs={{0,32},{32,0},{64,96},{96,64},{128,160},{160,128},{192,224},{224,1... | collective-permute-start | bytes 196616 | tf_op jit(solution)/shard_map/ppermute | solution.py:34
  285.7 2.6 collective-permute-done.4
  288.3 0.3 copy.39
  288.6 0.1 bitcast_add_fusion.2
  288.7 0.3 copy.40
  289.0 3.6 %collective-permute-start.5 = (f32[8,2048]{1,0:T(8,128)S(1)}, f32[8,2048]{1,0:T(8,128)S(1)}, u32[]{:S(2)}, u32[]{:S(2)}) collective-permute-start(f32[8,2048]{1,0:T(8,128)S(1)} %copy.40), channel_id=1, source_target_pairs={{0,64},{32,96},{64,0},{96,32},{128,192},{160,224},{192,128},{224,1... | collective-permute-start | bytes 196616 | tf_op jit(solution)/shard_map/ppermute | solution.py:34
  292.6 4.1 %collective-permute-done.5 = f32[8,2048]{1,0:T(8,128)S(1)} collective-permute-done((f32[8,2048]{1,0:T(8,128)S(1)}, f32[8,2048]{1,0:T(8,128)S(1)}, u32[]{:S(2)}, u32[]{:S(2)}) %collective-permute-start.5) | collective-permute-done | bytes 65568 | tf_op jit(solution)/shard_map/ppermute | solution.py:34
  296.7 0.3 copy.41
  297.0 0.1 add.121
  297.1 0.3 copy.42
  297.4 5.1 %collective-permute-start.6 = (f32[8,2048]{1,0:T(8,128)S(1)}, f32[8,2048]{1,0:T(8,128)S(1)}, u32[]{:S(2)}, u32[]{:S(2)}) collective-permute-start(f32[8,2048]{1,0:T(8,128)S(1)} %copy.42), channel_id=1, source_target_pairs={{0,128},{32,160},{64,192},{96,224},{128,0},{160,32},{192,64},{224,... | collective-permute-start | bytes 196616 | tf_op jit(solution)/shard_map/ppermute | solution.py:34
  302.6 2.2 collective-permute-done.6
  304.8 0.3 copy.43
  305.1 0.1 add.122
  305.2 0.3 copy.44
  305.5 6.5 %collective-permute-start.7 = (f32[8,2048]{1,0:T(8,128)S(1)}, f32[8,2048]{1,0:T(8,128)S(1)}, u32[]{:S(2)}, u32[]{:S(2)}) collective-permute-start(f32[8,2048]{1,0:T(8,128)S(1)} %copy.44), channel_id=1, source_target_pairs={{0,256},{32,288},{64,320},{96,352},{128,384},{160,416},{192,448},{... | collective-permute-start | bytes 196616 | tf_op jit(solution)/shard_map/ppermute | solution.py:34
  312.1 2.2 collective-permute-done.7
  314.3 0.3 copy.45
  314.7 0.1 add_multiply_fusion
  314.8 0.9 copy.46
  (40 shorter events, 0.3 us)
Async XLA Ops:
  0.0 190.5 %copy-start = (bf16[128,8]{0,1:T(8,128)(2,1)S(1)}, bf16[128,8]{0,1:T(8,128)(2,1)}, u32[]{:S(2)}) copy-start(bf16[128,8]{0,1:T(8,128)(2,1)} %param.26) | copy-start | bytes 6148
  14.7 15.6 %copy-start.6 = (s32[1,27,2048]{2,0,1:T(1,128)S(1)}, s32[1,27,2048]{2,0,1:T(1,128)}, u32[]{:S(2)}) copy-start(s32[1,27,2048]{2,0,1:T(1,128)} %param.19) | copy-start | bytes 663556
  14.7 16.3 %copy-start.12 = (s32[1,1,2,2]{3,2,1,0:T(2,128)S(1)}, s32[1,1,2,2]{3,2,1,0:T(2,128)}, u32[]{:S(2)}) copy-start(s32[1,1,2,2]{3,2,1,0:T(2,128)} %param.18) | copy-start | bytes 52
  14.7 80.0 %all-to-all-start = ((bf16[32,149,128]{2,1,0:T(8,128)(2,1)}), bf16[32,149,128]{2,1,0:T(8,128)(2,1)S(1)}, u32[]{:S(2)}, u32[]{:S(2)}) async-start(bf16[32,149,128]{2,1,0:T(8,128)(2,1)} %reshape.352), calls=%async_computation | async-start | bytes 2490368 | tf_op jit(solution)/shard_map/all_to_all | solution.py:262
  100.7 2.7 copy-start.1
  112.7 2.0 copy-start.3
  114.6 6.2 %copy-start.5 = (bf16[27,96,128]{2,1,0:T(8,128)(2,1)S(1)}, bf16[27,96,128]{2,1,0:T(8,128)(2,1)}, u32[]{:S(2)}) copy-start(bf16[27,96,128]{2,1,0:T(8,128)(2,1)} %param.20) | copy-start | bytes 1990660
  115.0 6.9 %copy-start.4 = (bf16[2048,96]{1,0:T(8,128)(2,1)}, bf16[2048,96]{1,0:T(8,128)(2,1)S(1)}, u32[]{:S(2)}) copy-start(bf16[2048,96]{1,0:T(8,128)(2,1)S(1)} %fusion.4.own_ref) | copy-start | bytes 1179652
  116.1 5.7 %collective-permute-start = (bf16[256,96]{1,0:T(8,128)(2,1)S(1)}, bf16[256,96]{1,0:T(8,128)(2,1)S(1)}, u32[]{:S(2)}, u32[]{:S(2)}) collective-permute-start(bf16[256,96]{1,0:T(8,128)(2,1)S(1)} %bitcast.97), channel_id=1, source_target_pairs={{0,1},{1,2},{2,3},{3,4},{4,5},{5,6},{6,7},{7,8},{8,9},{9,10},{10,1... | collective-permute-start | bytes 147464 | tf_op jit(solution)/shard_map/ppermute | solution.py:24
  118.1 3.8 %collective-permute-start.1 = (bf16[256,96]{1,0:T(8,128)(2,1)S(1)}, bf16[256,96]{1,0:T(8,128)(2,1)S(1)}, u32[]{:S(2)}, u32[]{:S(2)}) collective-permute-start(bf16[256,96]{1,0:T(8,128)(2,1)S(1)} %bitcast.96), channel_id=1, source_target_pairs={{1,0},{2,1},{3,2},{4,3},{5,4},{6,5},{7,6},{8,7},{9,8},{10,9},{11,1... | collective-permute-start | bytes 147464 | tf_op jit(solution)/shard_map/ppermute | solution.py:24
  121.9 0.6 copy-start.8
  121.9 0.6 copy-start.9
  152.3 38.1 %copy-start.13 = (f32[8]{0:T(128)S(1)}, f32[8]{0:T(128)}, u32[]{:S(2)}) copy-start(f32[8]{0:T(128)} %param.27) | copy-start | bytes 100
  155.6 2.6 collective-permute-start.2
  156.9 3.1 collective-permute-start.3
  158.2 1.8 copy-start.10
  160.0 0.6 copy-start.11
  200.9 50.0 %copy-start.7 = (s32[1,2048]{1,0:T(1,128)S(1)}, s32[1,2048]{1,0:T(1,128)}, u32[]{:S(2)}) copy-start(s32[1,2048]{1,0:T(1,128)} %param.15) | copy-start | bytes 24580
  204.2 69.5 %all-to-all-start.1 = ((f32[32,192,8]{1,2,0:T(8,128)}), f32[32,192,8]{1,2,0:T(8,128)S(1)}, u32[]{:S(2)}, u32[]{:S(2)}) async-start(f32[32,192,8]{1,2,0:T(8,128)} %copy.36), calls=%async_computation.1 | async-start | bytes 524288 | tf_op jit(solution)/shard_map/all_to_all | solution.py:297
  280.5 8.1 %copy-start.2 = (f32[2048,8]{1,0:T(8,128)S(1)}, f32[2048,8]{1,0:T(8,128)}, u32[]{:S(2)}) copy-start(f32[2048,8]{1,0:T(8,128)} %shard_map.140) | copy-start | bytes 196612
  282.1 6.2 %collective-permute-start.4 = (f32[8,2048]{1,0:T(8,128)S(1)}, f32[8,2048]{1,0:T(8,128)S(1)}, u32[]{:S(2)}, u32[]{:S(2)}) collective-permute-start(f32[8,2048]{1,0:T(8,128)S(1)} %copy.38), channel_id=1, source_target_pairs={{0,32},{32,0},{64,96},{96,64},{128,160},{160,128},{192,224},{224,1... | collective-permute-start | bytes 196616 | tf_op jit(solution)/shard_map/ppermute | solution.py:34
  289.0 7.7 %collective-permute-start.5 = (f32[8,2048]{1,0:T(8,128)S(1)}, f32[8,2048]{1,0:T(8,128)S(1)}, u32[]{:S(2)}, u32[]{:S(2)}) collective-permute-start(f32[8,2048]{1,0:T(8,128)S(1)} %copy.40), channel_id=1, source_target_pairs={{0,64},{32,96},{64,0},{96,32},{128,192},{160,224},{192,128},{224,1... | collective-permute-start | bytes 196616 | tf_op jit(solution)/shard_map/ppermute | solution.py:34
  297.4 7.3 %collective-permute-start.6 = (f32[8,2048]{1,0:T(8,128)S(1)}, f32[8,2048]{1,0:T(8,128)S(1)}, u32[]{:S(2)}, u32[]{:S(2)}) collective-permute-start(f32[8,2048]{1,0:T(8,128)S(1)} %copy.42), channel_id=1, source_target_pairs={{0,128},{32,160},{64,192},{96,224},{128,0},{160,32},{192,64},{224,... | collective-permute-start | bytes 196616 | tf_op jit(solution)/shard_map/ppermute | solution.py:34
  305.5 8.8 %collective-permute-start.7 = (f32[8,2048]{1,0:T(8,128)S(1)}, f32[8,2048]{1,0:T(8,128)S(1)}, u32[]{:S(2)}, u32[]{:S(2)}) collective-permute-start(f32[8,2048]{1,0:T(8,128)S(1)} %copy.44), channel_id=1, source_target_pairs={{0,256},{32,288},{64,320},{96,352},{128,384},{160,416},{192,448},{... | collective-permute-start | bytes 196616 | tf_op jit(solution)/shard_map/ppermute | solution.py:34

commit v10 on v9

--- a/solution.py
+++ b/solution.py
@@ -12,7 +12,7 @@
 CENTRE = 13
 UNROLL = 32
 CONV_ROWS = 256
-POOL_ROWS = 512
+POOL_ROWS = 1024
 POOL_COLS = 512
 DIGIT = 64
 RANK_BLOCK = 128

time: 320 us -> 319 us (level)
  starting transfers between devices: 86.9 us -> 52.4 us
  Pallas kernels: 81.8 us -> 111 us
  waiting for transfers between devices: 98.8 us -> 103 us
    all_to_all x1, starting transfers between devices: 46.7 us -> 16.1 us  [per_device(): returned = lax.all_to_all(slot_logits, 'slab', 0, 0, tiled=True)]
    pallas_call x2, Pallas kernels: 59.7 us -> 88.8 us  [convolve(): pl.pallas_call(functools.partial(conv_kernel, has_residual=residual is no...]
    ppermute x4, starting transfers between devices: 18.7 us -> 14.4 us  [all_summed(): values = values + lax.ppermute(values, axis, pairs)]
where the time goes in v10:
time: 319 us; the launch traced here: 315 us
  Pallas kernels  111 us (35%)
  waiting for transfers between devices  103 us (32%)
  starting transfers between devices  52.4 us (16%)
  local copies, waits for them, and re-layouts  33.8 us (11%)
  other arithmetic  10.1 us (3%)
  matrix products  3.28 us (1%)
    pallas_call x2, Pallas kernels, convolve(): pl.pallas_call(functools.partial(conv_kernel, has_residual=residual is no...  88.8 us
    all_to_all x1, waiting for transfers between devices, per_device(): lax.all_to_all(packed.reshape(slab_count, dense // 128, 128), 'slab', 0,...  63.4 us
    all_to_all x1, waiting for transfers between devices, per_device(): returned = lax.all_to_all(slot_logits, 'slab', 0, 0, tiled=True)  22.1 us
    all_to_all x1, starting transfers between devices, per_device(): returned = lax.all_to_all(slot_logits, 'slab', 0, 0, tiled=True)  16.1 us
    all_to_all x1, starting transfers between devices, per_device(): lax.all_to_all(packed.reshape(slab_count, dense // 128, 128), 'slab', 0,...  15.8 us
    ppermute x4, starting transfers between devices, all_summed(): values = values + lax.ppermute(values, axis, pairs)  14.4 us
    ppermute x4, waiting for transfers between devices, all_summed(): values = values + lax.ppermute(values, axis, pairs)  13.4 us
    pallas_call x2, Pallas kernels, gather_rows(): pl.pallas_call(gather_kernel, in_specs=[pl.BlockSpec(memory_space=pltpu.S...  12.8 us
  transfers between devices with their start and end apart: 10, of which 7 were waited for; matrix products, arithmetic and copies ran while one was open for 1% of the time, Pallas kernels for 0%

profile of v10, /device:TPU:24, one launch (start us, length us, event | category | flops | bytes accessed | tf_op | source)
XLA Modules:
  0.0 314.7 jit_solution(9283362031360692889)
XLA Ops:
  0.0 0.9 convert_reduce_fusion
  0.9 1.0 fusion.2
  1.9 0.7 compare_select_fusion
  2.6 0.7 fusion.12
  3.5 1.1 maximum_maximum_fusion
  4.6 0.3 copy.33
  4.9 6.3 %scatter_custom_fusion = bf16[6144,99]{1,0:T(8,128)(2,1)S(1)} fusion(s32[2048]{0:T(1024)S(1)} %bitcast.102, bf16[2048,99]{1,0:T(8,128)(2,1)S(1)} %copy.33, bf16[]{:T(256)} %constant.43.clone.1), kind=kCustom, calls=%fused_computation.17 | custom fusion | bytes 1216514 | tf_op jit(solution)/shard_map/scatter | solution.py:257
  11.2 1.9 reshape.351
  13.2 0.1 pad.13
  13.2 1.5 reshape.352
  14.7 15.8 %all-to-all-start = ((bf16[32,149,128]{2,1,0:T(8,128)(2,1)}), bf16[32,149,128]{2,1,0:T(8,128)(2,1)S(1)}, u32[]{:S(2)}, u32[]{:S(2)}) async-start(bf16[32,149,128]{2,1,0:T(8,128)(2,1)} %reshape.352), calls=%async_computation | async-start | bytes 2490368 | tf_op jit(solution)/shard_map/all_to_all | solution.py:262
  30.5 0.5 reduce.2
  31.1 0.1 copy.49
  31.2 63.4 %all-to-all-done = bf16[32,149,128]{2,1,0:T(8,128)(2,1)S(1)} async-done(((bf16[32,149,128]{2,1,0:T(8,128)(2,1)}), bf16[32,149,128]{2,1,0:T(8,128)(2,1)S(1)}, u32[]{:S(2)}, u32[]{:S(2)}) %all-to-all-start) | async-done | bytes 1220640 | tf_op jit(solution)/shard_map/all_to_all | solution.py:262
  94.7 0.2 copy.52
  94.9 5.8 %reshape.354.feats_ref = bf16[6144,99]{1,0:T(8,128)(2,1)S(1)} reshape(bf16[32,19008]{1,0:T(8,128)(2,1)S(1)} %bitcast.83) | data formatting | bytes 2433024 | tf_op jit(solution)/shard_map/reshape | solution.py:265
  100.7 2.7 add_reduce_fusion.index_ref
  103.4 9.1 %shard_map.136 = f32[2048,99]{1,0:T(8,128)} custom-call(s32[1,6144]{1,0:T(1,128)} %bitcast.93, bf16[6144,99]{1,0:T(8,128)(2,1)} %copy-done.1), custom_call_target="tpu_custom_call" | custom-call | tf_op jit(solution)/shard_map/pallas_call | solution.py:180
  112.4 1.9 fusion.3
  114.4 0.3 fusion.4.own_ref
  114.8 0.6 gather_fusion.1
  115.3 0.6 gather_fusion
  115.9 1.9 collective-permute-start
  117.8 1.5 collective-permute-start.1
  120.0 0.8 copy.50
  120.8 1.1 pad.15
  121.9 0.6 copy-done.8
  122.5 44.4 %shard_map.137.own_ref.rest_0_ = bf16[2048,128]{1,0:T(8,128)(2,1)} custom-call(s32[1]{0:T(128)} %bitcast.9.active_ref, s32[57344]{0:T(1024)} %bitcast.87, bf16[2048,96]{1,0:T(8,128)(2,1)} %copy-done.4, bf16[256,96]{1,0:T(8,128)(2,1)} %copy-done.8, bf16[256,96]{1,0:T(8,128)(2,1)} %copy-done.9, bf16[3456,128]{1,0:T(8,128)(2,1)} %bitcast.84, ...), custom_call_target="tpu_custom_call" | custom-call | tf_op jit(solution)/shard_map/pallas_call | solution.py:158
  166.9 1.6 gather_fusion.3
  168.5 1.6 gather_fusion.2
  170.1 1.3 collective-permute-start.2
  171.4 1.3 collective-permute-start.3
  172.7 4.3 %collective-permute-done.3.above_ref = bf16[256,128]{1,0:T(8,128)(2,1)S(1)} collective-permute-done((bf16[256,128]{1,0:T(8,128)(2,1)S(1)}, bf16[256,128]{1,0:T(8,128)(2,1)S(1)}, u32[]{:S(2)}, u32[]{:S(2)}) %collective-permute-start.3) | collective-permute-done | bytes 65568 | tf_op jit(solution)/shard_map/ppermute | solution.py:24
  177.1 0.6 copy-done.11
  177.7 44.4 %shard_map.138 = bf16[2048,128]{1,0:T(8,128)(2,1)} custom-call(s32[1]{0:T(128)} %bitcast.9.active_ref, s32[57344]{0:T(1024)} %bitcast.88, bf16[2048,128]{1,0:T(8,128)(2,1)} %shard_map.137.own_ref.rest_0_, bf16[256,128]{1,0:T(8,128)(2,1)} %copy-done.10, bf16[256,128]{1,0:T(8,128)(2,1)} %copy-done.11, bf16[3456,128]{1,0:T(8,128)(2,1)} %bitcast.91, ...), custom_call_target="tpu_custom_call" | custom-call | tf_op jit(solution)/shard_map/pallas_call | solution.py:158
  222.1 2.3 convolution_add_fusion.table_ref
  224.4 8.2 %shard_map.139 = f32[6144,8]{1,0:T(8,128)} custom-call(s32[6144]{0:T(1024)} %add_reduce_fusion.index_ref, f32[2048,8]{1,0:T(8,128)} %convolution_add_fusion.table_ref), custom_call_target="tpu_custom_call" | custom-call | tf_op jit(solution)/shard_map/pallas_call | solution.py:201
  232.6 3.2 %copy.36 = f32[32,192,8]{1,2,0:T(8,128)} copy(f32[32,192,8]{2,1,0:T(8,128)} %bitcast.77) | data formatting | bytes 393216 | tf_op jit(solution)/shard_map/reshape | solution.py:296
  235.8 16.1 %all-to-all-start.1 = ((f32[32,192,8]{1,2,0:T(8,128)}), f32[32,192,8]{1,2,0:T(8,128)S(1)}, u32[]{:S(2)}, u32[]{:S(2)}) async-start(f32[32,192,8]{1,2,0:T(8,128)} %copy.36), calls=%async_computation.1 | async-start | bytes 524288 | tf_op jit(solution)/shard_map/all_to_all | solution.py:297
  252.0 0.6 bitcast_add_fusion.1.index_ref
  252.6 22.1 %all-to-all-done.1 = f32[32,192,8]{1,2,0:T(8,128)S(1)} async-done(((f32[32,192,8]{1,2,0:T(8,128)}), f32[32,192,8]{1,2,0:T(8,128)S(1)}, u32[]{:S(2)}, u32[]{:S(2)}) %all-to-all-start.1) | async-done | bytes 196640 | tf_op jit(solution)/shard_map/all_to_all | solution.py:297
  274.7 2.2 copy.37
  276.9 4.6 %shard_map.140 = f32[2048,8]{1,0:T(8,128)} custom-call(s32[2048]{0:T(1024)} %bitcast_add_fusion.1.index_ref, f32[6144,8]{1,0:T(8,128)} %bitcast.78), custom_call_target="tpu_custom_call" | custom-call | tf_op jit(solution)/shard_map/pallas_call | solution.py:201
  281.5 1.6 copy.38
  283.1 3.5 %collective-permute-start.4 = (f32[8,2048]{1,0:T(8,128)S(1)}, f32[8,2048]{1,0:T(8,128)S(1)}, u32[]{:S(2)}, u32[]{:S(2)}) collective-permute-start(f32[8,2048]{1,0:T(8,128)S(1)} %copy.38), channel_id=1, source_target_pairs={{0,32},{32,0},{64,96},{96,64},{128,160},{160,128},{192,224},{224,1... | collective-permute-start | bytes 196616 | tf_op jit(solution)/shard_map/ppermute | solution.py:34
  286.6 2.7 collective-permute-done.4
  289.3 0.3 copy.39
  289.6 0.1 bitcast_add_fusion.2
  289.8 0.3 copy.40
  290.0 2.0 collective-permute-start.5
  292.1 5.6 %collective-permute-done.5 = f32[8,2048]{1,0:T(8,128)S(1)} collective-permute-done((f32[8,2048]{1,0:T(8,128)S(1)}, f32[8,2048]{1,0:T(8,128)S(1)}, u32[]{:S(2)}, u32[]{:S(2)}) %collective-permute-start.5) | collective-permute-done | bytes 65568 | tf_op jit(solution)/shard_map/ppermute | solution.py:34
  297.7 0.3 copy.41
  298.0 0.1 add.121
  298.2 0.3 copy.42
  298.5 4.2 %collective-permute-start.6 = (f32[8,2048]{1,0:T(8,128)S(1)}, f32[8,2048]{1,0:T(8,128)S(1)}, u32[]{:S(2)}, u32[]{:S(2)}) collective-permute-start(f32[8,2048]{1,0:T(8,128)S(1)} %copy.42), channel_id=1, source_target_pairs={{0,128},{32,160},{64,192},{96,224},{128,0},{160,32},{192,64},{224,... | collective-permute-start | bytes 196616 | tf_op jit(solution)/shard_map/ppermute | solution.py:34
  302.6 2.2 collective-permute-done.6
  304.9 0.3 copy.43
  305.2 0.1 add.122
  305.3 0.3 copy.44
  305.6 4.8 %collective-permute-start.7 = (f32[8,2048]{1,0:T(8,128)S(1)}, f32[8,2048]{1,0:T(8,128)S(1)}, u32[]{:S(2)}, u32[]{:S(2)}) collective-permute-start(f32[8,2048]{1,0:T(8,128)S(1)} %copy.44), channel_id=1, source_target_pairs={{0,256},{32,288},{64,320},{96,352},{128,384},{160,416},{192,448},{... | collective-permute-start | bytes 196616 | tf_op jit(solution)/shard_map/ppermute | solution.py:34
  310.4 2.9 collective-permute-done.7
  313.3 0.3 copy.45
  313.6 0.1 add_multiply_fusion
  313.7 0.9 copy.46
  (40 shorter events, 0.3 us)
Async XLA Ops:
  0.0 222.1 %copy-start = (bf16[128,8]{0,1:T(8,128)(2,1)S(1)}, bf16[128,8]{0,1:T(8,128)(2,1)}, u32[]{:S(2)}) copy-start(bf16[128,8]{0,1:T(8,128)(2,1)} %param.26) | copy-start | bytes 6148
  14.7 15.8 %copy-start.6 = (s32[1,27,2048]{2,0,1:T(1,128)S(1)}, s32[1,27,2048]{2,0,1:T(1,128)}, u32[]{:S(2)}) copy-start(s32[1,27,2048]{2,0,1:T(1,128)} %param.19) | copy-start | bytes 663556
  14.7 16.5 %copy-start.12 = (s32[1,1,2,2]{3,2,1,0:T(2,128)S(1)}, s32[1,1,2,2]{3,2,1,0:T(2,128)}, u32[]{:S(2)}) copy-start(s32[1,1,2,2]{3,2,1,0:T(2,128)} %param.18) | copy-start | bytes 52
  14.7 80.0 %all-to-all-start = ((bf16[32,149,128]{2,1,0:T(8,128)(2,1)}), bf16[32,149,128]{2,1,0:T(8,128)(2,1)S(1)}, u32[]{:S(2)}, u32[]{:S(2)}) async-start(bf16[32,149,128]{2,1,0:T(8,128)(2,1)} %reshape.352), calls=%async_computation | async-start | bytes 2490368 | tf_op jit(solution)/shard_map/all_to_all | solution.py:262
  100.7 2.7 copy-start.1
  112.4 2.0 copy-start.3
  114.4 6.4 %copy-start.5 = (bf16[27,96,128]{2,1,0:T(8,128)(2,1)S(1)}, bf16[27,96,128]{2,1,0:T(8,128)(2,1)}, u32[]{:S(2)}) copy-start(bf16[27,96,128]{2,1,0:T(8,128)(2,1)} %param.20) | copy-start | bytes 1990660
  114.7 7.1 %copy-start.4 = (bf16[2048,96]{1,0:T(8,128)(2,1)}, bf16[2048,96]{1,0:T(8,128)(2,1)S(1)}, u32[]{:S(2)}) copy-start(bf16[2048,96]{1,0:T(8,128)(2,1)S(1)} %fusion.4.own_ref) | copy-start | bytes 1179652
  115.9 6.0 %collective-permute-start = (bf16[256,96]{1,0:T(8,128)(2,1)S(1)}, bf16[256,96]{1,0:T(8,128)(2,1)S(1)}, u32[]{:S(2)}, u32[]{:S(2)}) collective-permute-start(bf16[256,96]{1,0:T(8,128)(2,1)S(1)} %bitcast.97), channel_id=1, source_target_pairs={{0,1},{1,2},{2,3},{3,4},{4,5},{5,6},{6,7},{7,8},{8,9},{9,10},{10,1... | collective-permute-start | bytes 147464 | tf_op jit(solution)/shard_map/ppermute | solution.py:24
  117.8 4.0 %collective-permute-start.1 = (bf16[256,96]{1,0:T(8,128)(2,1)S(1)}, bf16[256,96]{1,0:T(8,128)(2,1)S(1)}, u32[]{:S(2)}, u32[]{:S(2)}) collective-permute-start(bf16[256,96]{1,0:T(8,128)(2,1)S(1)} %bitcast.96), channel_id=1, source_target_pairs={{1,0},{2,1},{3,2},{4,3},{5,4},{6,5},{7,6},{8,7},{9,8},{10,9},{11,1... | collective-permute-start | bytes 147464 | tf_op jit(solution)/shard_map/ppermute | solution.py:24
  121.8 0.6 copy-start.8
  121.9 0.6 copy-start.9
  166.9 55.2 %copy-start.13 = (f32[8]{0:T(128)S(1)}, f32[8]{0:T(128)}, u32[]{:S(2)}) copy-start(f32[8]{0:T(128)} %param.27) | copy-start | bytes 100
  170.1 2.6 collective-permute-start.2
  171.4 5.7 %collective-permute-start.3 = (bf16[256,128]{1,0:T(8,128)(2,1)S(1)}, bf16[256,128]{1,0:T(8,128)(2,1)S(1)}, u32[]{:S(2)}, u32[]{:S(2)}) collective-permute-start(bf16[256,128]{1,0:T(8,128)(2,1)S(1)} %bitcast.98), channel_id=1, source_target_pairs={{1,0},{2,1},{3,2},{4,3},{5,4},{6,5},{7,6},{8,7},{9,8},{10,9},{11,1... | collective-permute-start | bytes 196616 | tf_op jit(solution)/shard_map/ppermute | solution.py:24
  172.7 4.3 %copy-start.10 = (bf16[256,128]{1,0:T(8,128)(2,1)}, bf16[256,128]{1,0:T(8,128)(2,1)S(1)}, u32[]{:S(2)}) copy-start(bf16[256,128]{1,0:T(8,128)(2,1)S(1)} %collective-permute-done.2.below_ref) | copy-start | bytes 196612
  177.1 0.6 copy-start.11
  232.6 19.4 %copy-start.7 = (s32[1,2048]{1,0:T(1,128)S(1)}, s32[1,2048]{1,0:T(1,128)}, u32[]{:S(2)}) copy-start(s32[1,2048]{1,0:T(1,128)} %param.15) | copy-start | bytes 24580
  235.8 38.9 %all-to-all-start.1 = ((f32[32,192,8]{1,2,0:T(8,128)}), f32[32,192,8]{1,2,0:T(8,128)S(1)}, u32[]{:S(2)}, u32[]{:S(2)}) async-start(f32[32,192,8]{1,2,0:T(8,128)} %copy.36), calls=%async_computation.1 | async-start | bytes 524288 | tf_op jit(solution)/shard_map/all_to_all | solution.py:297
  281.5 8.1 %copy-start.2 = (f32[2048,8]{1,0:T(8,128)S(1)}, f32[2048,8]{1,0:T(8,128)}, u32[]{:S(2)}) copy-start(f32[2048,8]{1,0:T(8,128)} %shard_map.140) | copy-start | bytes 196612
  283.1 6.2 %collective-permute-start.4 = (f32[8,2048]{1,0:T(8,128)S(1)}, f32[8,2048]{1,0:T(8,128)S(1)}, u32[]{:S(2)}, u32[]{:S(2)}) collective-permute-start(f32[8,2048]{1,0:T(8,128)S(1)} %copy.38), channel_id=1, source_target_pairs={{0,32},{32,0},{64,96},{96,64},{128,160},{160,128},{192,224},{224,1... | collective-permute-start | bytes 196616 | tf_op jit(solution)/shard_map/ppermute | solution.py:34
  290.0 7.7 %collective-permute-start.5 = (f32[8,2048]{1,0:T(8,128)S(1)}, f32[8,2048]{1,0:T(8,128)S(1)}, u32[]{:S(2)}, u32[]{:S(2)}) collective-permute-start(f32[8,2048]{1,0:T(8,128)S(1)} %copy.40), channel_id=1, source_target_pairs={{0,64},{32,96},{64,0},{96,32},{128,192},{160,224},{192,128},{224,1... | collective-permute-start | bytes 196616 | tf_op jit(solution)/shard_map/ppermute | solution.py:34
  298.5 6.4 %collective-permute-start.6 = (f32[8,2048]{1,0:T(8,128)S(1)}, f32[8,2048]{1,0:T(8,128)S(1)}, u32[]{:S(2)}, u32[]{:S(2)}) collective-permute-start(f32[8,2048]{1,0:T(8,128)S(1)} %copy.42), channel_id=1, source_target_pairs={{0,128},{32,160},{64,192},{96,224},{128,0},{160,32},{192,64},{224,... | collective-permute-start | bytes 196616 | tf_op jit(solution)/shard_map/ppermute | solution.py:34
  305.6 7.7 %collective-permute-start.7 = (f32[8,2048]{1,0:T(8,128)S(1)}, f32[8,2048]{1,0:T(8,128)S(1)}, u32[]{:S(2)}, u32[]{:S(2)}) collective-permute-start(f32[8,2048]{1,0:T(8,128)S(1)} %copy.44), channel_id=1, source_target_pairs={{0,256},{32,288},{64,320},{96,352},{128,384},{160,416},{192,448},{... | collective-permute-start | bytes 196616 | tf_op jit(solution)/shard_map/ppermute | solution.py:34
